TPU v7x, 128 devices: a whole 4x4x4 slice. The times are simulated.
128 devices in a mesh: dp: 8 (over y, z_hi), fsdp: 16 (over x, z_lo, core).
Axes of the slice: x: 4, y: 4, z: 4 (z_hi: 2, z_lo: 2; z = z_hi * 2 + z_lo), core: 2. Of those that a mesh axis runs over, the one named last changes fastest.
Arguments:
- x_src: bfloat16 [512, 8192], P('fsdp', 'dp'), may hold values from -6 to 6
- doc_lengths: int32 [16, 4], replicated, may hold values from 1 to 16, as said below
- doc_dests: int32 [16, 4], replicated, may hold values from 0 to 15, as said below
- w_gate: bfloat16 [8192, 14336], P('dp', 'fsdp'), may hold values from -0.0625 to 0.0625
- w_up: bfloat16 [8192, 14336], P('dp', 'fsdp'), may hold values from -0.0625 to 0.0625
- w_down: bfloat16 [14336, 8192], P('fsdp', 'dp'), may hold values from -0.046875 to 0.046875
- basis: float32 [8192, 512], P('dp'), may hold values from -0.0625 to 0.0625
- out_cotangent: bfloat16 [1024, 8192], P('fsdp', 'dp'), may hold values from -6 to 6
Outputs:
- layer_out: bfloat16 [1024, 8192], P('fsdp', 'dp')
- input_grad: bfloat16 [1024, 8192], P('fsdp', 'dp')
- grad_gate: float32 [8192, 14336], P('dp', 'fsdp')
- grad_up: float32 [8192, 14336], P('dp', 'fsdp')
- grad_down: float32 [14336, 8192], P('fsdp', 'dp')
Inputs may be any that keep to these rules, and one draw needn't show every extreme that they name: `doc_lengths`: the 4 lengths of a source sum to 32 and one of them equals 16. `doc_dests`: document c of every source s goes to destination (s + o_c) modulo 16, for 4 different offsets o_c shared by all sources, one of which is 8; a destination receives at most 64 tokens in all, and some destination receives exactly 64.
All inputs are finite; a program needn't handle non-finite values.
Results may differ from a plain program's by a relative error of at most 0.034.
Values may be sent and summed in bfloat16 or wider, within the bound.
No kernel may reach another device: no remote copies, remote signals or barrier semaphores. Data moves between devices by JAX's collectives and lax.ppermute only.
A program may use at most 128 MiB of HBM per device.

v0:
```python
import jax
import jax.numpy as jnp
from jax import lax
from jax.sharding import PartitionSpec as P

MOST = 16


def deal_tables(doc_lengths, doc_dests):
    groups = doc_lengths.shape[0]
    starts = jnp.cumsum(doc_lengths, axis=1) - doc_lengths
    targets = jnp.arange(groups, dtype=jnp.int32)
    hits = (doc_dests[:, :, None] == targets[None, None, :]).astype(jnp.int32)
    loads = jnp.sum(doc_lengths[:, :, None] * hits, axis=1)
    firsts = jnp.sum(starts[:, :, None] * hits, axis=1)
    return (loads, firsts)


def settle(term):
    return lax.optimization_barrier(term.astype(jnp.bfloat16)).astype(jnp.float32)


def pack_slots(rows, loads_out, firsts_out, depth):
    inner = jnp.arange(depth, dtype=jnp.int32)
    valid = inner[None, :] < loads_out[:, None]
    index = jnp.where(valid, firsts_out[:, None] + inner[None, :], 0).reshape(-1)
    taken = jnp.take(rows, index, axis=0).reshape(loads_out.shape[0], depth, rows.shape[1])
    return jnp.where(valid[:, :, None], taken, jnp.zeros_like(taken))


def compact_rows(slots, loads_in, count):
    sources, depth = (slots.shape[0], slots.shape[1])
    offsets = jnp.cumsum(loads_in) - loads_in
    ends = offsets + loads_in
    place = jnp.arange(count, dtype=jnp.int32)
    owner = jnp.sum((ends[:, None] <= place[None, :]).astype(jnp.int32), axis=0)
    owner = jnp.minimum(owner, sources - 1)
    inner = place - jnp.take(offsets, owner)
    valid = place < jnp.sum(loads_in)
    flat = jnp.where(valid, owner * depth + inner, 0)
    taken = jnp.take(slots.reshape(sources * depth, slots.shape[2]), flat, axis=0)
    return jnp.where(valid[:, None], taken, jnp.zeros_like(taken))


def layer(x_rows, dy_rows, w_gate, w_up, w_down, basis):
    hidden_width = w_gate.shape[1]
    high = lax.Precision.HIGHEST
    xall = lax.all_gather(x_rows, "fsdp", axis=0, tiled=True)
    block = xall
    first = settle(jnp.dot(block, w_gate, preferred_element_type=jnp.float32))
    second = settle(jnp.dot(block, w_up, preferred_element_type=jnp.float32))
    both = lax.psum_scatter(
        jnp.concatenate([first, second], axis=1).astype(jnp.bfloat16),
        "dp",
        scatter_dimension=0,
        tiled=True,
    ).astype(jnp.float32)
    gate = both[:, :hidden_width]
    up = both[:, hidden_width:]
    sig = jax.nn.sigmoid(gate)
    hidden = (gate * sig * up).astype(jnp.bfloat16)
    hall = lax.all_gather(hidden, "dp", axis=0, tiled=True)
    block = hall
    layer_out = lax.psum_scatter(
        settle(jnp.dot(block, w_down, preferred_element_type=jnp.float32)).astype(jnp.bfloat16),
        "fsdp",
        scatter_dimension=0,
        tiled=True,
    )
    dyall = lax.all_gather(dy_rows, "fsdp", axis=0, tiled=True)
    block = dyall
    hidden_grad = lax.psum_scatter(
        settle(
            lax.dot_general(
                block, w_down, (((1,), (1,)), ((), ())), preferred_element_type=jnp.float32
            )
        ).astype(jnp.bfloat16),
        "dp",
        scatter_dimension=0,
        tiled=True,
    ).astype(jnp.float32)
    gate_grad = (hidden_grad * up * sig * (1.0 + gate * (1.0 - sig))).astype(jnp.bfloat16)
    up_grad = (hidden_grad * gate * sig).astype(jnp.bfloat16)
    gate_all, up_all = (
        lax.all_gather(gate_grad, "dp", axis=0, tiled=True),
        lax.all_gather(up_grad, "dp", axis=0, tiled=True),
    )
    contract_rows = (((0,), (0,)), ((), ()))
    grad_down = lax.dot_general(hall, dyall, contract_rows, preferred_element_type=jnp.float32)
    raw_gate = lax.dot_general(xall, gate_all, contract_rows, preferred_element_type=jnp.float32)
    raw_up = lax.dot_general(xall, up_all, contract_rows, preferred_element_type=jnp.float32)
    first = gate_all
    second = up_all
    total = lax.dot_general(
        first, w_gate, (((1,), (1,)), ((), ())), preferred_element_type=jnp.float32
    )
    total = total + lax.dot_general(
        second, w_up, (((1,), (1,)), ((), ())), preferred_element_type=jnp.float32
    )
    input_grad = lax.psum_scatter(
        settle(total).astype(jnp.bfloat16), "fsdp", scatter_dimension=0, tiled=True
    )
    local_gate = lax.dot_general(basis, raw_gate, contract_rows, precision=high)
    local_up = lax.dot_general(basis, raw_up, contract_rows, precision=high)
    over_gate, over_up = (
        lax.psum(local_gate.astype(jnp.bfloat16), "dp").astype(jnp.float32),
        lax.psum(local_up.astype(jnp.bfloat16), "dp").astype(jnp.float32),
    )
    grad_gate = raw_gate - jnp.dot(basis, over_gate, precision=high)
    grad_up = raw_up - jnp.dot(basis, over_up, precision=high)
    return (layer_out, input_grad, grad_gate, grad_up, grad_down)


def per_device(x_src, doc_lengths, doc_dests, w_gate, w_up, w_down, basis, out_cotangent):
    loads, firsts = deal_tables(doc_lengths, doc_dests)
    myself = lax.axis_index("fsdp")
    loads_out = jnp.take(loads, myself, axis=0)
    firsts_out = jnp.take(firsts, myself, axis=0)
    loads_in = jnp.take(loads, myself, axis=1)
    dealt_rows = out_cotangent.shape[0]
    slots = pack_slots(x_src, loads_out, firsts_out, MOST)
    arrived = lax.all_to_all(slots, "fsdp", split_axis=0, concat_axis=0, tiled=True)
    x_rows = compact_rows(arrived, loads_in, dealt_rows)
    layer_out, input_grad, grad_gate, grad_up, grad_down = layer(
        x_rows, out_cotangent, w_gate, w_up, w_down, basis
    )
    return (layer_out, input_grad, grad_gate, grad_up, grad_down)


def solution(mesh):
    return jax.shard_map(
        per_device,
        mesh=mesh,
        in_specs=(
            P("fsdp", "dp"),
            P(),
            P(),
            P("dp", "fsdp"),
            P("dp", "fsdp"),
            P("fsdp", "dp"),
            P("dp", None),
            P("fsdp", "dp"),
        ),
        out_specs=(
            P("fsdp", "dp"),
            P("fsdp", "dp"),
            P("dp", "fsdp"),
            P("dp", "fsdp"),
            P("fsdp", "dp"),
        ),
        check_vma=False,
    )
```

profile of v0, /device:TPU:33, one launch (start us, length us, event | category | flops | bytes accessed | tf_op | source)
XLA Modules:
  0.0 666.4 jit_solution(16519514606444433728)
XLA Ops:
  9.8 1.2 gather_fusion.1
  11.0 0.9 select_select_fusion
  11.9 6.1 all-to-all-start
  21.2 6.3 all-to-all-done
  29.7 33.7 %all-gather.6.cloned.1.call-done = bf16[1024,1024]{1,0:T(8,128)(2,1)} async-done(((bf16[64,1024]{1,0:T(8,128)(2,1)}), bf16[1024,1024]{1,0:T(8,128)(2,1)}) %all-gather.6.cloned.1.call-update) | async-done | bytes 2097168 | tf_op jit(solution)/shard_map/all_gather | solution.py:48
  63.5 4.6 convolution_convert_fusion.2
  68.1 2.3 convolution_convert_fusion.3
  70.4 2.1 pad_maximum_fusion
  72.6 26.5 %all-gather.10.cloned.1.call-done = bf16[1024,1024]{1,0:T(8,128)(2,1)} async-done(((bf16[64,1024]{1,0:T(8,128)(2,1)}), bf16[1024,1024]{1,0:T(8,128)(2,1)}) %all-gather.10.cloned.1.call-update) | async-done | bytes 2097168 | tf_op jit(solution)/shard_map/all_gather | solution.py:70
  99.1 5.7 convolution_convert_fusion.1
  104.9 79.8 %reduce-scatter.5.cloned.1.call-done = bf16[128,1792]{1,0:T(8,128)(2,1)} async-done(((bf16[1024,1792]{1,0:T(8,128)(2,1)}), bf16[128,1792]{1,0:T(8,128)(2,1)}) %reduce-scatter.5.cloned.1.call-update) | async-done | bytes 458768 | tf_op jit(solution)/shard_map/reduce_scatter | solution.py:52
  184.7 1.1 convert_element_type.60
  185.8 77.7 %reduce-scatter.9.cloned.1.call-done = bf16[128,896]{1,0:T(8,128)(2,1)} async-done(((bf16[1024,896]{1,0:T(8,128)(2,1)}), bf16[128,896]{1,0:T(8,128)(2,1)}) %reduce-scatter.9.cloned.1.call-update) | async-done | bytes 229392 | tf_op jit(solution)/shard_map/reduce_scatter | solution.py:72
  263.5 2.0 fusion.6
  267.0 50.5 %all-gather.12.cloned.1.call-done = bf16[1024,896]{1,0:T(8,128)(2,1)} async-done(((bf16[128,896]{1,0:T(8,128)(2,1)}), bf16[1024,896]{1,0:T(8,128)(2,1)}) %all-gather.12.cloned.1.call-update) | async-done | bytes 1835024 | tf_op jit(solution)/shard_map/all_gather | solution.py:85
  317.5 4.5 fusion.16
  322.1 1.8 copy-done.2
  323.9 6.9 %fusion = bf16[512,896]{0,1:T(8,128)(2,1)} fusion(f32[1024,896]{1,0:T(8,128)S(1)} %fusion.16, f32[1024,512]{1,0:T(8,128)S(1)} %copy-done), kind=kOutput, calls=%fused_computation.13 | convolution fusion | flops 5637603328 | bytes 6684672 | tf_op jit(solution)/shard_map/dot_general | solution.py:103
  330.8 41.2 %all-gather.14.cloned.1.call-done = bf16[1024,896]{1,0:T(8,128)(2,1)} async-done(((bf16[128,896]{1,0:T(8,128)(2,1)}), bf16[1024,896]{1,0:T(8,128)(2,1)}) %all-gather.14.cloned.1.call-update) | async-done | bytes 1835024 | tf_op jit(solution)/shard_map/all_gather | solution.py:86
  372.0 4.5 fusion.17
  376.5 1.8 copy-done.3
  378.4 7.2 %fusion.1 = bf16[512,896]{0,1:T(8,128)(2,1)} fusion(f32[1024,896]{1,0:T(8,128)S(1)} %fusion.17, f32[1024,512]{1,0:T(8,128)S(1)} %copy-done), kind=kOutput, calls=%fused_computation.14 | convolution fusion | flops 5637603328 | bytes 6684672 | tf_op jit(solution)/shard_map/dot_general | solution.py:104
  385.6 40.4 %all-gather.8.cloned.1.call-done = bf16[1024,896]{1,0:T(8,128)(2,1)} async-done(((bf16[128,896]{1,0:T(8,128)(2,1)}), bf16[1024,896]{1,0:T(8,128)(2,1)}) %all-gather.8.cloned.1.call-update) | async-done | bytes 1835024 | tf_op jit(solution)/shard_map/all_gather | solution.py:62
  426.0 5.8 convolution_convert_fusion
  431.9 4.6 fusion.15
  436.5 3.7 add_convert_fusion
  440.2 6.1 fusion.18
  446.3 84.3 %all-reduce.3.cloned.1.call-done = (bf16[512,896]{0,1:T(8,128)(2,1)}, bf16[512,896]{0,1:T(8,128)(2,1)}) async-done(((bf16[512,896]{0,1:T(8,128)(2,1)}, bf16[512,896]{0,1:T(8,128)(2,1)}), (bf16[512,896]{0,1:T(8,128)(2,1)}, bf16[512,896]{0,1:T(8,128)(2,1)})) %all-reduce.3.cloned.1.call-update) | async-done | bytes 1835024 | tf_op jit(solution)/shard_map/psum | solution.py:106
  530.5 6.8 %bitcast_subtract_fusion.1 = f32[1024,896]{1,0:T(8,128)} fusion(f32[1024,896]{1,0:T(8,128)} %copy-done.2, bf16[512,896]{0,1:T(8,128)(2,1)} %get-tuple-element.32, f32[1024,512]{1,0:T(8,128)S(1)} %copy-done), kind=kOutput, calls=%fused_computation.6 | convolution fusion | flops 5638062080 | bytes 10354688 | tf_op jit(solution)/shard_map/dot_general | solution.py:109
  537.4 5.5 bitcast_subtract_fusion
  542.8 50.7 %reduce-scatter.7.cloned.1.call-done = bf16[64,1024]{1,0:T(8,128)(2,1)} async-done(((bf16[1024,1024]{1,0:T(8,128)(2,1)}), bf16[64,1024]{1,0:T(8,128)(2,1)}) %reduce-scatter.7.cloned.1.call-update) | async-done | bytes 131088 | tf_op jit(solution)/shard_map/reduce_scatter | solution.py:64
  593.5 66.1 %reduce-scatter.11.cloned.1.call-done = bf16[64,1024]{1,0:T(8,128)(2,1)} async-done(((bf16[1024,1024]{1,0:T(8,128)(2,1)}), bf16[64,1024]{1,0:T(8,128)(2,1)}) %reduce-scatter.11.cloned.1.call-update) | async-done | bytes 131088 | tf_op jit(solution)/shard_map/reduce_scatter | solution.py:100
  (60 shorter events, 9.8 us)
Async XLA Ops:
  7.2 316.7 %copy-start = (f32[1024,512]{1,0:T(8,128)S(1)}, f32[1024,512]{1,0:T(8,128)}, u32[]{:S(2)}) copy-start(f32[1024,512]{1,0:T(8,128)} %param.16) | copy-start | bytes 6291460
  7.2 2.6 copy-start.1
  11.9 15.5 %all-to-all-start = ((bf16[16,16,1024]{2,1,0:T(8,128)(2,1)}), bf16[16,16,1024]{2,1,0:T(8,128)(2,1)S(1)}, u32[]{:S(2)}, u32[]{:S(2)}) async-start(bf16[16,16,1024]{2,1,0:T(8,128)(2,1)} %select_select_fusion), calls=%async_computation | async-start | bytes 1048576 | tf_op jit(solution)/shard_map/all_to_all | solution.py:122
  18.0 45.5 %all-gather.6.cloned.1.call-start = ((), (), s32[]{:S(2)}) async-start(), calls=%async_computation.5 | async-start | bytes 2228224 | tf_op jit(solution)/shard_map/all_gather | solution.py:48
  28.9 70.1 %all-gather.10.cloned.1.call-start = ((), (), s32[]{:S(2)}) async-start(), calls=%async_computation.9 | async-start | bytes 2228224 | tf_op jit(solution)/shard_map/all_gather | solution.py:70
  29.7 155.0 %reduce-scatter.5.cloned.1.call-start = ((), (), s32[]{:S(2)}) async-start(), calls=%async_computation.6 | async-start | bytes 4128768 | tf_op jit(solution)/shard_map/reduce_scatter | solution.py:52
  63.5 4.6 copy-start.6
  63.5 4.6 copy-start.7
  72.6 190.9 %reduce-scatter.9.cloned.1.call-start = ((), (), s32[]{:S(2)}) async-start(), calls=%async_computation.10 | async-start | bytes 2064384 | tf_op jit(solution)/shard_map/reduce_scatter | solution.py:72
  104.8 212.7 %all-gather.12.cloned.1.call-start = ((), (), s32[]{:S(2)}) async-start(), calls=%async_computation.11 | async-start | bytes 2064384 | tf_op jit(solution)/shard_map/all_gather | solution.py:85
  265.5 106.5 %all-gather.14.cloned.1.call-start = ((), (), s32[]{:S(2)}) async-start(), calls=%async_computation.12 | async-start | bytes 2064384 | tf_op jit(solution)/shard_map/all_gather | solution.py:86
  266.1 159.9 %all-gather.8.cloned.1.call-start = ((), (), s32[]{:S(2)}) async-start(), calls=%async_computation.7 | async-start | bytes 2064384 | tf_op jit(solution)/shard_map/all_gather | solution.py:62
  266.8 263.7 %all-reduce.3.cloned.1.call-start = ((), (), s32[]{:S(2)}) async-start(), calls=%async_computation.14 | async-start | bytes 3670016 | tf_op jit(solution)/shard_map/psum | solution.py:106
  322.0 1.8 copy-start.2
  376.5 1.8 copy-start.3
  385.6 208.0 %reduce-scatter.7.cloned.1.call-start = ((), (), s32[]{:S(2)}) async-start(), calls=%async_computation.8 | async-start | bytes 2228224 | tf_op jit(solution)/shard_map/reduce_scatter | solution.py:64
  431.8 227.8 %reduce-scatter.11.cloned.1.call-start = ((), (), s32[]{:S(2)}) async-start(), calls=%async_computation.13 | async-start | bytes 2228224 | tf_op jit(solution)/shard_map/reduce_scatter | solution.py:100
  431.8 4.6 copy-start.8
  431.9 4.6 copy-start.9
  530.5 6.8 %copy-start.4 = (f32[1024,896]{1,0:T(8,128)S(1)}, f32[1024,896]{1,0:T(8,128)}, u32[]{:S(2)}) copy-start(f32[1024,896]{1,0:T(8,128)} %copy-done.3) | copy-start | bytes 11010052
  530.5 6.8 %copy-start.5 = (bf16[512,896]{0,1:T(8,128)(2,1)S(1)}, bf16[512,896]{0,1:T(8,128)(2,1)}, u32[]{:S(2)}) copy-start(bf16[512,896]{0,1:T(8,128)(2,1)} %get-tuple-element.33) | copy-start | bytes 2752516
Sparse Core Ops, SparseCore 0:
  29.1 34.3 all-gather.5
  65.2 33.8 all-gather.9
  103.6 81.0 reduce-scatter.4
  188.9 74.5 reduce-scatter.8
  266.2 51.2 all-gather.11
  320.2 51.6 all-gather.13
  374.3 51.6 all-gather.7
  429.2 101.3 all-reduce.2
  533.5 59.9 reduce-scatter.6
  596.3 63.2 reduce-scatter.10
where the time goes:
time: 675 us; the launch traced here: 666 us
  waiting for transfers between devices  559 us (83%)
  matrix products  68.2 us (10%)
  between operations  14.4 us (2%)
  other arithmetic  11.7 us (2%)
    psum x1, waiting for transfers between devices, layer(): lax.psum(local_gate.astype(jnp.bfloat16), 'dp').astype(jnp.float32)  84.3 us
    reduce_scatter x1, waiting for transfers between devices, layer(): lax.psum_scatter(jnp.concatenate([first, second], axis=1).astype(jnp.bflo...  79.8 us
    reduce_scatter x1, waiting for transfers between devices, layer(): lax.psum_scatter(settle(lax.dot_general(block, w_down, (((1,), (1,)), (()...  77.7 us
    reduce_scatter x1, waiting for transfers between devices, layer(): lax.psum_scatter(settle(total).astype(jnp.bfloat16), 'fsdp', scatter_dime...  66.1 us
    reduce_scatter x1, waiting for transfers between devices, layer(): lax.psum_scatter(settle(jnp.dot(block, w_down, preferred_element_type=jnp...  50.7 us
    all_gather x1, waiting for transfers between devices, layer(): lax.all_gather(gate_grad, 'dp', axis=0, tiled=True)  50.5 us
    all_gather x1, waiting for transfers between devices, layer(): lax.all_gather(up_grad, 'dp', axis=0, tiled=True)  41.2 us
    all_gather x1, waiting for transfers between devices, layer(): hall = lax.all_gather(hidden, 'dp', axis=0, tiled=True)  40.4 us
  transfers between devices with their start and end apart: 11, of which 11 were waited for; matrix products, arithmetic and copies ran while one was open for 11% of the time, Pallas kernels for 0%

commit v1 on v0

v1 whole, which is shorter than its diff:
```python
import jax
import jax.numpy as jnp
from jax import lax
from jax.sharding import PartitionSpec as P

MOST = 16


def deal_tables(doc_lengths, doc_dests):
    groups = doc_lengths.shape[0]
    starts = jnp.cumsum(doc_lengths, axis=1) - doc_lengths
    targets = jnp.arange(groups, dtype=jnp.int32)
    hits = (doc_dests[:, :, None] == targets[None, None, :]).astype(jnp.int32)
    loads = jnp.sum(doc_lengths[:, :, None] * hits, axis=1)
    firsts = jnp.sum(starts[:, :, None] * hits, axis=1)
    return (loads, firsts)


def token_rows(doc_lengths, doc_dests, loads, tok, recv):
    starts = jnp.cumsum(doc_lengths, axis=1) - doc_lengths
    ends = starts + doc_lengths
    offsets = jnp.cumsum(loads, axis=0) - loads
    t = jnp.arange(tok, dtype=jnp.int32)
    doc_of = jnp.sum((ends[:, :, None] <= t[None, None, :]).astype(jnp.int32), axis=1)
    doc_of = jnp.minimum(doc_of, doc_lengths.shape[1] - 1)
    dst = jnp.take_along_axis(doc_dests, doc_of, axis=1)
    st = jnp.take_along_axis(starts, doc_of, axis=1)
    off = jnp.take_along_axis(offsets, dst, axis=1)
    row = dst * recv + off + t[None, :] - st
    return jnp.clip(row, 0, loads.shape[0] * recv - 1).reshape(-1)


def settle(term):
    return lax.optimization_barrier(term.astype(jnp.bfloat16)).astype(jnp.float32)


def pack_slots(rows, loads_out, firsts_out, depth):
    inner = jnp.arange(depth, dtype=jnp.int32)
    valid = inner[None, :] < loads_out[:, None]
    index = jnp.where(valid, firsts_out[:, None] + inner[None, :], 0).reshape(-1)
    taken = jnp.take(rows, index, axis=0).reshape(loads_out.shape[0], depth, rows.shape[1])
    return jnp.where(valid[:, :, None], taken, jnp.zeros_like(taken))


def compact_rows(slots, loads_in, count):
    sources, depth = (slots.shape[0], slots.shape[1])
    offsets = jnp.cumsum(loads_in) - loads_in
    ends = offsets + loads_in
    place = jnp.arange(count, dtype=jnp.int32)
    owner = jnp.sum((ends[:, None] <= place[None, :]).astype(jnp.int32), axis=0)
    owner = jnp.minimum(owner, sources - 1)
    inner = place - jnp.take(offsets, owner)
    valid = place < jnp.sum(loads_in)
    flat = jnp.where(valid, owner * depth + inner, 0)
    taken = jnp.take(slots.reshape(sources * depth, slots.shape[2]), flat, axis=0)
    return jnp.where(valid[:, None], taken, jnp.zeros_like(taken))


def deal_out(rows, loads_out, firsts_out, loads_in, count):
    slots = pack_slots(rows, loads_out, firsts_out, MOST)
    arrived = lax.all_to_all(slots, "fsdp", split_axis=0, concat_axis=0, tiled=True)
    return compact_rows(arrived, loads_in, count)


def per_device(x_src, doc_lengths, doc_dests, w_gate, w_up, w_down, basis, out_cotangent):
    hidden_width = w_gate.shape[1]
    tok = x_src.shape[0]
    recv = out_cotangent.shape[0]
    loads, firsts = deal_tables(doc_lengths, doc_dests)
    myself = lax.axis_index("fsdp")
    loads_out = jnp.take(loads, myself, axis=0)
    firsts_out = jnp.take(firsts, myself, axis=0)
    loads_in = jnp.take(loads, myself, axis=1)
    rows_of = token_rows(doc_lengths, doc_dests, loads, tok, recv)
    contract_rows = (((0,), (0,)), ((), ()))
    contract_cols = (((1,), (1,)), ((), ()))

    xall = lax.all_gather(x_src, "fsdp", axis=0, tiled=True)
    dy_dealt = lax.all_gather(out_cotangent, "fsdp", axis=0, tiled=True)
    dyall = jnp.take(dy_dealt, rows_of, axis=0)

    first = settle(jnp.dot(xall, w_gate, preferred_element_type=jnp.float32))
    second = settle(jnp.dot(xall, w_up, preferred_element_type=jnp.float32))
    both = lax.psum(
        jnp.concatenate([first, second], axis=1).astype(jnp.bfloat16), "dp"
    ).astype(jnp.float32)
    gate = both[:, :hidden_width]
    up = both[:, hidden_width:]
    sig = jax.nn.sigmoid(gate)
    hidden = (gate * sig * up).astype(jnp.bfloat16)
    out_part = settle(jnp.dot(hidden, w_down, preferred_element_type=jnp.float32))
    out_src = lax.psum_scatter(
        out_part.astype(jnp.bfloat16), "fsdp", scatter_dimension=0, tiled=True
    )
    layer_out = deal_out(out_src, loads_out, firsts_out, loads_in, recv)

    hg_part = settle(
        lax.dot_general(dyall, w_down, contract_cols, preferred_element_type=jnp.float32)
    )
    hidden_grad = lax.psum(hg_part.astype(jnp.bfloat16), "dp").astype(jnp.float32)
    gate_grad = (hidden_grad * up * sig * (1.0 + gate * (1.0 - sig))).astype(jnp.bfloat16)
    up_grad = (hidden_grad * gate * sig).astype(jnp.bfloat16)
    grad_down = lax.dot_general(hidden, dyall, contract_rows, preferred_element_type=jnp.float32)
    raw_gate = lax.dot_general(xall, gate_grad, contract_rows, preferred_element_type=jnp.float32)
    raw_up = lax.dot_general(xall, up_grad, contract_rows, preferred_element_type=jnp.float32)
    total = lax.dot_general(
        gate_grad, w_gate, contract_cols, preferred_element_type=jnp.float32
    )
    total = total + lax.dot_general(
        up_grad, w_up, contract_cols, preferred_element_type=jnp.float32
    )
    in_src = lax.psum_scatter(
        settle(total).astype(jnp.bfloat16), "fsdp", scatter_dimension=0, tiled=True
    )
    input_grad = deal_out(in_src, loads_out, firsts_out, loads_in, recv)

    keys_local = jnp.dot(xall, basis, preferred_element_type=jnp.float32)
    keys_all = lax.psum(keys_local.astype(jnp.bfloat16), "dp")
    over_gate = lax.dot_general(keys_all, gate_grad, contract_rows, preferred_element_type=jnp.float32)
    over_up = lax.dot_general(keys_all, up_grad, contract_rows, preferred_element_type=jnp.float32)
    grad_gate = raw_gate - jnp.dot(basis, over_gate, preferred_element_type=jnp.float32)
    grad_up = raw_up - jnp.dot(basis, over_up, preferred_element_type=jnp.float32)
    return (layer_out, input_grad, grad_gate, grad_up, grad_down)


def solution(mesh):
    return jax.shard_map(
        per_device,
        mesh=mesh,
        in_specs=(
            P("fsdp", "dp"),
            P(),
            P(),
            P("dp", "fsdp"),
            P("dp", "fsdp"),
            P("fsdp", "dp"),
            P("dp", None),
            P("fsdp", "dp"),
        ),
        out_specs=(
            P("fsdp", "dp"),
            P("fsdp", "dp"),
            P("dp", "fsdp"),
            P("dp", "fsdp"),
            P("fsdp", "dp"),
        ),
        check_vma=False,
    )
```

time: 675 us -> 432 us (0.64)
  waiting for transfers between devices: 559 us -> 308 us
  local copies, waits for them, and re-layouts: 6.44 us -> 38.3 us
  matrix products: 68.2 us -> 40.9 us
  starting transfers between devices: 6.64 us -> 17.3 us
    reduce_scatter x4 -> x2, waiting for transfers between devices: 274 us -> 105 us  [the longest x1 61 us: per_device(): lax.psum_scatter(out_part.astype(jnp.bfloat16), 'fsdp', scatter_dimension...]
    all_gather x5 -> x2, waiting for transfers between devices: 192 us -> 47.9 us  [the longest x1 28.1 us: per_device(): dy_dealt = lax.all_gather(out_cotangent, 'fsdp', axis=0, tiled=True)]
    psum x1, waiting for transfers between devices: 84.3 us -> 150 us  [per_device(): lax.psum(jnp.concatenate([first, second], axis=1).astype(jnp.bfloat16), '...]
    dot_general x13 -> x12, matrix products: 68.2 us -> 40.9 us  [the longest x1 6.08 us: per_device(): jnp.dot(basis, over_gate, preferred_element_type=jnp.float32)]
    gather x0 -> x9, local copies, waits for them, and re-layouts: none -> 18.9 us  [the longest x1 5.35 us: per_device(): dyall = jnp.take(dy_dealt, rows_of, axis=0)]
    all_to_all x1 -> x2, starting transfers between devices: 6.06 us -> 16.9 us  [deal_out(): lax.all_to_all(slots, 'fsdp', split_axis=0, concat_axis=0, tiled=True)]
    unnamed x20 -> x28, local copies, waits for them, and re-layouts: 3.71 us -> 11 us
  transfers between devices with their start and end apart: 11 -> 7, of which waited for: 11 -> 6; matrix products, arithmetic and copies ran while one was open for 11% -> 15% of each run, Pallas kernels for 0% -> 0%
where the time goes in v1:
time: 432 us; the launch traced here: 430 us
  waiting for transfers between devices  308 us (71%)
  matrix products  40.9 us (9%)
  local copies, waits for them, and re-layouts  38.3 us (9%)
  starting transfers between devices  17.3 us (4%)
  between operations  14 us (3%)
  other arithmetic  10.8 us (2%)
    psum x1, waiting for transfers between devices, per_device(): lax.psum(jnp.concatenate([first, second], axis=1).astype(jnp.bfloat16), '...  150 us
    reduce_scatter x1, waiting for transfers between devices, per_device(): lax.psum_scatter(out_part.astype(jnp.bfloat16), 'fsdp', scatter_dimension...  61 us
    reduce_scatter x1, waiting for transfers between devices, per_device(): lax.psum_scatter(settle(total).astype(jnp.bfloat16), 'fsdp', scatter_dime...  44.2 us
    all_gather x1, waiting for transfers between devices, per_device(): dy_dealt = lax.all_gather(out_cotangent, 'fsdp', axis=0, tiled=True)  28.1 us
    all_gather x1, waiting for transfers between devices, per_device(): xall = lax.all_gather(x_src, 'fsdp', axis=0, tiled=True)  19.9 us
    all_to_all x2, starting transfers between devices, deal_out(): lax.all_to_all(slots, 'fsdp', split_axis=0, concat_axis=0, tiled=True)  16.9 us
    unnamed x28, local copies, waits for them, and re-layouts  11 us
  transfers between devices with their start and end apart: 7, of which 6 were waited for; matrix products, arithmetic and copies ran while one was open for 15% of the time, Pallas kernels for 0%

profile of v1, /device:TPU:33, one launch (start us, length us, event | category | flops | bytes accessed | tf_op | source)
XLA Modules:
  0.0 429.6 jit_solution(13565888470477834014)
XLA Ops:
  10.3 4.7 %gather_fusion.5 = s32[512]{0:T(512)S(1)} fusion(s32[16,4]{0,1:T(4,128)S(1)} %copy-done.1, s32[512]{0:T(512)S(1)} %reshape.346), kind=kCustom, calls=%fused_computation.3.clone | custom fusion | bytes 8192 | tf_op jit(solution)/shard_map/jit(take_along_axis)/gather | solution.py:26
  15.1 4.7 %gather_fusion.6 = s32[512]{0:T(512)S(1)} fusion(s32[16,4]{0,1:T(4,128)S(1)} %sub.33, s32[512]{0:T(512)S(1)} %reshape.346), kind=kCustom, calls=%fused_computation.6.clone | custom fusion | bytes 8192 | tf_op jit(solution)/shard_map/jit(take_along_axis)/gather | solution.py:27
  20.1 3.8 gather_fusion.1
  24.1 19.9 %all-gather.3.cloned.1.call-done = bf16[512,1024]{1,0:T(8,128)(2,1)} async-done(((bf16[32,1024]{1,0:T(8,128)(2,1)}), bf16[512,1024]{1,0:T(8,128)(2,1)}) %all-gather.3.cloned.1.call-update) | async-done | bytes 1048592 | tf_op jit(solution)/shard_map/all_gather | solution.py:78
  44.0 3.2 convolution_convert_fusion.2
  47.2 1.3 convolution_convert_fusion.3
  48.5 1.4 pad_maximum_fusion
  49.9 1.5 fusion.20
  51.4 28.1 %all-gather.5.cloned.1.call-done = bf16[1024,1024]{1,0:T(8,128)(2,1)} async-done(((bf16[64,1024]{1,0:T(8,128)(2,1)}), bf16[1024,1024]{1,0:T(8,128)(2,1)}) %all-gather.5.cloned.1.call-update) | async-done | bytes 2097168 | tf_op jit(solution)/shard_map/all_gather | solution.py:79
  79.5 5.4 %gather_fusion = bf16[512,1024]{1,0:T(8,128)(2,1)} fusion(bf16[1024,1024]{1,0:T(8,128)(2,1)} %all-gather.5.cloned.1.call-done, s32[1024]{0:T(1024)S(1)} %pad_clamp_fusion), kind=kCustom, calls=%fused_computation.7 | custom fusion | bytes 2099200 | tf_op jit(solution)/shard_map/jit(_take)/gather | solution.py:80
  84.8 4.0 convolution_convert_fusion.1
  88.9 150.4 %all-reduce.3.cloned.1.call-done = (bf16[512,1792]{1,0:T(8,128)(2,1)}, bf16[512,896]{1,0:T(8,128)(2,1)}, bf16[512,512]{1,0:T(8,128)(2,1)}) async-done(((bf16[512,1792]{1,0:T(8,128)(2,1)}, bf16[512,896]{1,0:T(8,128)(2,1)}, bf16[512,512]{1,0:T(8,128)(2,1)}), (bf16[512,1792]{1,0:T(8,128)(2,1)}, bf16[512,896]{1,0:T(8,128)(2,1)}, bf16[512,512]{1,0:T(8,128)(2,1)})) %all-reduce.3.cloned.1.call-update) | async-done | bytes 3276816 | tf_op jit(solution)/shard_map/psum | solution.py:84
  239.3 1.8 convert_element_type.52
  241.2 2.0 fusion.4
  243.2 1.3 fusion.17
  245.3 2.3 add_convert_fusion
  249.0 4.0 convolution_convert_fusion
  254.6 4.3 fusion.18
  258.9 3.0 fusion.19
  261.9 44.2 %reduce-scatter.5.cloned.1.call-done = bf16[32,1024]{1,0:T(8,128)(2,1)} async-done(((bf16[512,1024]{1,0:T(8,128)(2,1)}), bf16[32,1024]{1,0:T(8,128)(2,1)}) %reduce-scatter.5.cloned.1.call-update) | async-done | bytes 65552 | tf_op jit(solution)/shard_map/reduce_scatter | solution.py:112
  306.1 2.4 gather_fusion.7
  308.5 61.0 %reduce-scatter.3.cloned.1.call-done = bf16[32,1024]{1,0:T(8,128)(2,1)} async-done(((bf16[512,1024]{1,0:T(8,128)(2,1)}), bf16[32,1024]{1,0:T(8,128)(2,1)}) %reduce-scatter.3.cloned.1.call-update) | async-done | bytes 65552 | tf_op jit(solution)/shard_map/reduce_scatter | solution.py:92
  369.5 2.4 gather_fusion.2
  373.2 11.4 %all-to-all-start.1 = ((bf16[16,16,1024]{2,1,0:T(8,128)(2,1)}), bf16[16,16,1024]{2,1,0:T(8,128)(2,1)S(1)}, u32[]{:S(2)}, u32[]{:S(2)}) async-start(bf16[16,16,1024]{2,1,0:T(8,128)(2,1)} %get-tuple-element.62), calls=%async_computation.3 | async-start | bytes 1048576 | tf_op jit(solution)/shard_map/all_to_all | solution.py:61
  384.6 6.1 %subtract_bitcast_fusion.1 = f32[1024,896]{0,1:T(8,128)} fusion(f32[896,1024]{1,0:T(8,128)} %fusion.18, f32[1024,512]{1,0:T(8,128)S(1)} %copy-done, bf16[512,512]{1,0:T(8,128)(2,1)} %get-tuple-element.53, bf16[512,896]{1,0:T(8,128)(2,1)} %copy-done.6), kind=kOutput, calls=%fused_computation.10 | convolution fusion | flops 1410203648 | bytes 10878976 | tf_op jit(solution)/shard_map/dot_general | solution.py:121
  390.6 3.4 all-to-all-done.1
  394.1 5.5 %all-to-all-start = ((bf16[16,16,1024]{2,1,0:T(8,128)(2,1)}), bf16[16,16,1024]{2,1,0:T(8,128)(2,1)}, u32[]{:S(2)}, u32[]{:S(2)}) async-start(bf16[16,16,1024]{2,1,0:T(8,128)(2,1)} %get-tuple-element.63), calls=%async_computation.1 | async-start | bytes 1048576 | tf_op jit(solution)/shard_map/all_to_all | solution.py:61
  399.6 5.7 %subtract_bitcast_fusion = f32[1024,896]{0,1:T(8,128)} fusion(f32[896,1024]{1,0:T(8,128)} %fusion.19, f32[1024,512]{1,0:T(8,128)S(1)} %copy-done, bf16[512,512]{1,0:T(8,128)(2,1)} %get-tuple-element.53, bf16[512,896]{1,0:T(8,128)(2,1)S(1)} %copy-done.5), kind=kOutput, calls=%fused_computation.9 | convolution fusion | flops 1410203648 | bytes 10878976 | tf_op jit(solution)/shard_map/dot_general | solution.py:122
  405.2 5.0 %copy.25 = f32[1024,896]{1,0:T(8,128)} copy(f32[1024,896]{0,1:T(8,128)} %subtract_bitcast_fusion.1) | data formatting | bytes 7340032
  410.3 5.1 %copy.26 = f32[1024,896]{1,0:T(8,128)} copy(f32[1024,896]{0,1:T(8,128)} %subtract_bitcast_fusion) | data formatting | bytes 7340032
  415.4 4.3 fusion.9
  420.3 1.9 gather_fusion.4
  (77 shorter events, 10.4 us)
Async XLA Ops:
  7.2 42.7 %copy-start = (f32[1024,512]{1,0:T(8,128)S(1)}, f32[1024,512]{1,0:T(8,128)}, u32[]{:S(2)}) copy-start(f32[1024,512]{1,0:T(8,128)} %param.24) | copy-start | bytes 6291460
  7.2 3.1 copy-start.1
  7.2 36.8 %all-gather.3.cloned.1.call-start = ((), (), s32[]{:S(2)}) async-start(), calls=%async_computation.4 | async-start | bytes 1114112 | tf_op jit(solution)/shard_map/all_gather | solution.py:78
  7.9 71.5 %all-gather.5.cloned.1.call-start = ((), (), s32[]{:S(2)}) async-start(), calls=%async_computation.6 | async-start | bytes 2228224 | tf_op jit(solution)/shard_map/all_gather | solution.py:79
  8.7 230.6 %all-reduce.3.cloned.1.call-start = ((), (), s32[]{:S(2)}) async-start(), calls=%async_computation.8 | async-start | bytes 6553600 | tf_op jit(solution)/shard_map/psum | solution.py:84
  15.1 4.8 %copy-start.9 = (s32[16,4]{0,1:T(4,128)S(1)}, s32[16,4]{0,1:T(4,128)}, u32[]{:S(2)}) copy-start(s32[16,4]{0,1:T(4,128)} %param.19) | copy-start | bytes 772
  44.0 3.2 copy-start.2
  44.0 3.2 copy-start.10
  88.9 217.2 %reduce-scatter.5.cloned.1.call-start = ((), (), s32[]{:S(2)}) async-start(), calls=%async_computation.7 | async-start | bytes 1114112 | tf_op jit(solution)/shard_map/reduce_scatter | solution.py:112
  239.3 1.8 copy-start.8
  241.2 2.0 copy-start.11
  243.2 1.3 copy-start.6
  243.2 1.3 copy-start.3
  243.2 2.2 copy-start.12
  247.7 121.8 %reduce-scatter.3.cloned.1.call-start = ((), (), s32[]{:S(2)}) async-start(), calls=%async_computation.5 | async-start | bytes 1114112 | tf_op jit(solution)/shard_map/reduce_scatter | solution.py:92
  254.6 4.3 copy-start.4
  373.2 20.9 %all-to-all-start.1 = ((bf16[16,16,1024]{2,1,0:T(8,128)(2,1)}), bf16[16,16,1024]{2,1,0:T(8,128)(2,1)S(1)}, u32[]{:S(2)}, u32[]{:S(2)}) async-start(bf16[16,16,1024]{2,1,0:T(8,128)(2,1)} %get-tuple-element.62), calls=%async_computation.3 | async-start | bytes 1048576 | tf_op jit(solution)/shard_map/all_to_all | solution.py:61
  384.6 15.0 %copy-start.5 = (bf16[512,896]{1,0:T(8,128)(2,1)S(1)}, bf16[512,896]{1,0:T(8,128)(2,1)}, u32[]{:S(2)}) copy-start(bf16[512,896]{1,0:T(8,128)(2,1)} %copy-done.3) | copy-start | bytes 2752516
  394.1 26.3 %all-to-all-start = ((bf16[16,16,1024]{2,1,0:T(8,128)(2,1)}), bf16[16,16,1024]{2,1,0:T(8,128)(2,1)}, u32[]{:S(2)}, u32[]{:S(2)}) async-start(bf16[16,16,1024]{2,1,0:T(8,128)(2,1)} %get-tuple-element.63), calls=%async_computation.1 | async-start | bytes 1048576 | tf_op jit(solution)/shard_map/all_to_all | solution.py:61
  410.3 5.1 %copy-start.7 = (bf16[512,896]{1,0:T(8,128)(2,1)S(1)}, bf16[512,896]{1,0:T(8,128)(2,1)}, u32[]{:S(2)}) copy-start(bf16[512,896]{1,0:T(8,128)(2,1)} %get-tuple-element.61) | copy-start | bytes 2752516
Sparse Core Ops, SparseCore 0:
  9.7 34.2 all-gather.2
  45.7 33.7 all-gather.4
  89.0 150.2 all-reduce.2
  247.8 58.2 reduce-scatter.4
  308.3 61.1 reduce-scatter.2

commit v2 on v1

v2 whole, which is shorter than its diff:
```python
import functools

import jax
import jax.numpy as jnp
from jax import lax
from jax.sharding import PartitionSpec as P

MOST = 16


def deal_tables(doc_lengths, doc_dests):
    groups = doc_lengths.shape[0]
    starts = jnp.cumsum(doc_lengths, axis=1) - doc_lengths
    targets = jnp.arange(groups, dtype=jnp.int32)
    hits = (doc_dests[:, :, None] == targets[None, None, :]).astype(jnp.int32)
    loads = jnp.sum(doc_lengths[:, :, None] * hits, axis=1)
    firsts = jnp.sum(starts[:, :, None] * hits, axis=1)
    return (loads, firsts)


def token_rows(doc_lengths, doc_dests, loads, tok, recv):
    starts = jnp.cumsum(doc_lengths, axis=1) - doc_lengths
    ends = starts + doc_lengths
    offsets = jnp.cumsum(loads, axis=0) - loads
    t = jnp.arange(tok, dtype=jnp.int32)
    doc_of = jnp.sum((ends[:, :, None] <= t[None, None, :]).astype(jnp.int32), axis=1)
    doc_of = jnp.minimum(doc_of, doc_lengths.shape[1] - 1)
    dst = jnp.take_along_axis(doc_dests, doc_of, axis=1)
    st = jnp.take_along_axis(starts, doc_of, axis=1)
    off = jnp.take_along_axis(offsets, dst, axis=1)
    row = dst * recv + off + t[None, :] - st
    return jnp.clip(row, 0, loads.shape[0] * recv - 1).reshape(-1)


def settle(term):
    return lax.optimization_barrier(term.astype(jnp.bfloat16)).astype(jnp.float32)


def deal_index(doc_lengths, doc_dests, loads, firsts, tok, recv):
    sources = loads.shape[0]
    offsets = jnp.cumsum(loads, axis=0) - loads
    ends = offsets + loads
    place = jnp.arange(recv, dtype=jnp.int32)
    owner = jnp.sum((ends[:, :, None] <= place[None, None, :]).astype(jnp.int32), axis=0)
    owner = jnp.minimum(owner, sources - 1)
    pick = (owner[None, :, :] == jnp.arange(sources, dtype=jnp.int32)[:, None, None]).astype(jnp.int32)
    own_offset = jnp.sum(pick * offsets[:, :, None], axis=0)
    own_first = jnp.sum(pick * firsts[:, :, None], axis=0)
    valid = place[None, :] < jnp.sum(loads, axis=0)[:, None]
    index = owner * tok + own_first + place[None, :] - own_offset
    index = jnp.where(valid, index, 0)
    return jnp.clip(index, 0, sources * tok - 1).reshape(-1), valid


def reduce_rows(part, axis, n):
    rows, cols = part.shape
    got = lax.all_to_all(part.astype(jnp.bfloat16).reshape(n, rows // n, cols), axis, 0, 0, tiled=True)
    return jnp.sum(got.astype(jnp.float32), axis=0)


def gather_rows(block, axis, n):
    rows, cols = block.shape
    got = lax.all_to_all(jnp.broadcast_to(block[None], (n, rows, cols)), axis, 0, 0, tiled=True)
    return got.reshape(n * rows, cols)


def reduce_dealt(part, index, valid, n):
    cols = part.shape[1]
    send = jnp.take(part.astype(jnp.bfloat16), index, axis=0).reshape(valid.shape[0], valid.shape[1], cols)
    send = jnp.where(valid[:, :, None], send, jnp.zeros_like(send))
    got = lax.all_to_all(send, "fsdp", 0, 0, tiled=True)
    return jnp.sum(got.astype(jnp.float32), axis=0).astype(jnp.bfloat16)


def per_device(n_dp, n_fsdp, x_src, doc_lengths, doc_dests, w_gate, w_up, w_down, basis, out_cotangent):
    hidden_width = w_gate.shape[1]
    tok = x_src.shape[0]
    recv = out_cotangent.shape[0]
    loads, firsts = deal_tables(doc_lengths, doc_dests)
    rows_of = token_rows(doc_lengths, doc_dests, loads, tok, recv)
    index, valid = deal_index(doc_lengths, doc_dests, loads, firsts, tok, recv)
    contract_rows = (((0,), (0,)), ((), ()))
    contract_cols = (((1,), (1,)), ((), ()))

    xall = gather_rows(x_src, "fsdp", n_fsdp)
    dy_dealt = lax.all_gather(out_cotangent, "fsdp", axis=0, tiled=True)
    dyall = jnp.take(dy_dealt, rows_of, axis=0)
    first = jnp.dot(xall, w_gate, preferred_element_type=jnp.float32)
    second = jnp.dot(xall, w_up, preferred_element_type=jnp.float32)
    keys_local = jnp.dot(xall, basis, preferred_element_type=jnp.float32)
    both = reduce_rows(jnp.concatenate([first, second, keys_local], axis=1), "dp", n_dp)
    gate = both[:, :hidden_width]
    up = both[:, hidden_width:2 * hidden_width]
    keys = both[:, 2 * hidden_width:].astype(jnp.bfloat16)
    sig = jax.nn.sigmoid(gate)
    hidden = (gate * sig * up).astype(jnp.bfloat16)
    gathered = gather_rows(jnp.concatenate([hidden, keys], axis=1), "dp", n_dp)
    hall = gathered[:, :hidden_width]
    keys_all = gathered[:, hidden_width:]
    out_part = jnp.dot(hall, w_down, preferred_element_type=jnp.float32)
    layer_out = reduce_dealt(out_part, index, valid, n_fsdp)

    hg_part = lax.dot_general(dyall, w_down, contract_cols, preferred_element_type=jnp.float32)
    hidden_grad = reduce_rows(hg_part, "dp", n_dp)
    gate_grad = (hidden_grad * up * sig * (1.0 + gate * (1.0 - sig))).astype(jnp.bfloat16)
    up_grad = (hidden_grad * gate * sig).astype(jnp.bfloat16)
    grads = gather_rows(jnp.concatenate([gate_grad, up_grad], axis=1), "dp", n_dp)
    gate_all = grads[:, :hidden_width]
    up_all = grads[:, hidden_width:]
    grad_down = lax.dot_general(hall, dyall, contract_rows, preferred_element_type=jnp.float32)
    raw_gate = lax.dot_general(xall, gate_all, contract_rows, preferred_element_type=jnp.float32)
    raw_up = lax.dot_general(xall, up_all, contract_rows, preferred_element_type=jnp.float32)
    total = lax.dot_general(gate_all, w_gate, contract_cols, preferred_element_type=jnp.float32)
    total = total + lax.dot_general(up_all, w_up, contract_cols, preferred_element_type=jnp.float32)
    input_grad = reduce_dealt(total, index, valid, n_fsdp)

    over_gate = lax.dot_general(keys_all, gate_all, contract_rows, preferred_element_type=jnp.float32)
    over_up = lax.dot_general(keys_all, up_all, contract_rows, preferred_element_type=jnp.float32)
    grad_gate = raw_gate - jnp.dot(basis, over_gate, preferred_element_type=jnp.float32)
    grad_up = raw_up - jnp.dot(basis, over_up, preferred_element_type=jnp.float32)
    return (layer_out, input_grad, grad_gate, grad_up, grad_down)


def solution(mesh):
    body = functools.partial(per_device, mesh.shape["dp"], mesh.shape["fsdp"])
    return jax.shard_map(
        body,
        mesh=mesh,
        in_specs=(
            P("fsdp", "dp"),
            P(),
            P(),
            P("dp", "fsdp"),
            P("dp", "fsdp"),
            P("fsdp", "dp"),
            P("dp", None),
            P("fsdp", "dp"),
        ),
        out_specs=(
            P("fsdp", "dp"),
            P("fsdp", "dp"),
            P("dp", "fsdp"),
            P("dp", "fsdp"),
            P("fsdp", "dp"),
        ),
        check_vma=False,
    )
```

time: 432 us -> 265 us (0.61)
  waiting for transfers between devices: 308 us -> 71.7 us
  blocking collectives: 0 us -> 32 us
  starting transfers between devices: 17.3 us -> 35.7 us
  other arithmetic: 10.8 us -> 20.4 us
  local copies, waits for them, and re-layouts: 38.3 us -> 47.1 us
    psum x1 -> x0, waiting for transfers between devices: 150 us -> none  [per_device(): lax.psum(jnp.concatenate([first, second], axis=1).astype(jnp.bfloat16), '...]
    reduce_scatter x2 -> x0, waiting for transfers between devices: 105 us -> none  [the longest x1 61 us: per_device(): lax.psum_scatter(out_part.astype(jnp.bfloat16), 'fsdp', scatter_dimension...]
    all_to_all x2 -> x6, waiting for transfers between devices: 3.42 us -> 62.7 us  [the longest x3 48.2 us: gather_rows(): lax.all_to_all(jnp.broadcast_to(block[None], (n, rows, cols)), axis, 0, 0...]
    all_to_all x0 -> x1, blocking collectives: none -> 32 us  [reduce_dealt(): got = lax.all_to_all(send, 'fsdp', 0, 0, tiled=True)]
    all_gather x1 -> x0, waiting for transfers between devices: 19.9 us -> none  [per_device(): xall = lax.all_gather(x_src, 'fsdp', axis=0, tiled=True)]
    all_gather x1, waiting for transfers between devices: 28.1 us -> 8.34 us  [per_device(): dy_dealt = lax.all_gather(out_cotangent, 'fsdp', axis=0, tiled=True)]
    all_to_all x2 -> x6, starting transfers between devices: 16.9 us -> 35.7 us  [the longest x2 15.6 us: reduce_rows(): lax.all_to_all(part.astype(jnp.bfloat16).reshape(n, rows // n, cols), axi...]
    reduce_sum x3 -> x7, other arithmetic: 0.89 us -> 9.15 us  [the longest x2 5.35 us: reduce_dealt(): return jnp.sum(got.astype(jnp.float32), axis=0).astype(jnp.bfloat16)]
  transfers between devices with their start and end apart: 7 -> 7, of which waited for: 6 -> 6; matrix products, arithmetic and copies ran while one was open for 15% -> 31% of each run, Pallas kernels for 0% -> 0%
where the time goes in v2:
time: 265 us; the launch traced here: 262 us
  waiting for transfers between devices  71.7 us (27%)
  local copies, waits for them, and re-layouts  47.1 us (18%)
  matrix products  41 us (15%)
  starting transfers between devices  35.7 us (13%)
  blocking collectives  32 us (12%)
  other arithmetic  20.4 us (8%)
  between operations  14.3 us (5%)
    all_to_all x3, waiting for transfers between devices, gather_rows(): lax.all_to_all(jnp.broadcast_to(block[None], (n, rows, cols)), axis, 0, 0...  48.2 us
    all_to_all x1, blocking collectives, reduce_dealt(): got = lax.all_to_all(send, 'fsdp', 0, 0, tiled=True)  32 us
    all_to_all x2, starting transfers between devices, reduce_rows(): lax.all_to_all(part.astype(jnp.bfloat16).reshape(n, rows // n, cols), axi...  15.6 us
    all_to_all x2, waiting for transfers between devices, reduce_rows(): lax.all_to_all(part.astype(jnp.bfloat16).reshape(n, rows // n, cols), axi...  14.5 us
    all_to_all x3, starting transfers between devices, gather_rows(): lax.all_to_all(jnp.broadcast_to(block[None], (n, rows, cols)), axis, 0, 0...  14.3 us
    unnamed x28, local copies, waits for them, and re-layouts  12.3 us
    gather x2, local copies, waits for them, and re-layouts, reduce_dealt(): jnp.take(part.astype(jnp.bfloat16), index, axis=0)  10.7 us
    all_gather x1, waiting for transfers between devices, per_device(): dy_dealt = lax.all_gather(out_cotangent, 'fsdp', axis=0, tiled=True)  8.34 us
  transfers between devices with their start and end apart: 7, of which 6 were waited for; matrix products, arithmetic and copies ran while one was open for 31% of the time, Pallas kernels for 0%

profile of v2, /device:TPU:33, one launch (start us, length us, event | category | flops | bytes accessed | tf_op | source)
XLA Modules:
  0.0 262.3 jit_solution(3739783738311355215)
XLA Ops:
  9.3 6.1 %all-to-all-start = ((bf16[16,32,1024]{2,1,0:T(8,128)(2,1)}), bf16[16,32,1024]{2,1,0:T(8,128)(2,1)S(1)}, u32[]{:S(2)}, u32[]{:S(2)}) async-start(bf16[16,32,1024]{2,1,0:T(8,128)(2,1)} %broadcast_in_dim.43), calls=%async_computation | async-start | bytes 2097152 | tf_op jit(solution)/shard_map/all_to_all | solution.py:63
  16.1 14.4 %all-to-all-done = bf16[16,32,1024]{2,1,0:T(8,128)(2,1)S(1)} async-done(((bf16[16,32,1024]{2,1,0:T(8,128)(2,1)}), bf16[16,32,1024]{2,1,0:T(8,128)(2,1)S(1)}, u32[]{:S(2)}, u32[]{:S(2)}) %all-to-all-start) | async-done | bytes 1048608 | tf_op jit(solution)/shard_map/all_to_all | solution.py:63
  36.7 6.7 %all-to-all-start.1 = ((bf16[8,64,2304]{2,1,0:T(8,128)(2,1)}), bf16[8,64,2304]{2,1,0:T(8,128)(2,1)}, u32[]{:S(2)}, u32[]{:S(2)}) async-start(bf16[8,64,2304]{2,1,0:T(8,128)(2,1)} %pad_maximum_fusion), calls=%async_computation.1 | async-start | bytes 4718592 | tf_op jit(solution)/shard_map/all_to_all | solution.py:57
  43.7 4.7 %gather_fusion.3 = s32[512]{0:T(512)S(1)} fusion(s32[16,4]{0,1:T(4,128)S(1)} %copy-done.1, s32[512]{0:T(512)S(1)} %reshape.229), kind=kCustom, calls=%fused_computation.1.clone | custom fusion | bytes 8192 | tf_op jit(solution)/shard_map/jit(take_along_axis)/gather | solution.py:28
  48.5 4.7 %gather_fusion.4 = s32[512]{0:T(512)S(1)} fusion(s32[16,4]{0,1:T(4,128)S(1)} %sub.34, s32[512]{0:T(512)S(1)} %reshape.229), kind=kCustom, calls=%fused_computation.3.clone | custom fusion | bytes 8192 | tf_op jit(solution)/shard_map/jit(take_along_axis)/gather | solution.py:29
  54.1 3.8 %gather_fusion.1 = s32[512]{0:T(512)S(1)} fusion(s32[16,16]{1,0:T(8,128)S(1)} %sub.35, s32[512]{0:T(512)S(1)} %reshape.203), kind=kCustom, calls=%fused_computation.5 | custom fusion | bytes 8192 | tf_op jit(solution)/shard_map/jit(take_along_axis)/gather | solution.py:30
  58.1 8.3 %all-gather.2.cloned.1.call-done = bf16[1024,1024]{1,0:T(8,128)(2,1)} async-done(((bf16[64,1024]{1,0:T(8,128)(2,1)}), bf16[1024,1024]{1,0:T(8,128)(2,1)}) %all-gather.2.cloned.1.call-update) | async-done | bytes 2097168 | tf_op jit(solution)/shard_map/all_gather | solution.py:86
  66.5 4.6 %gather_fusion = bf16[512,1024]{1,0:T(8,128)(2,1)S(1)} fusion(bf16[1024,1024]{1,0:T(8,128)(2,1)} %all-gather.2.cloned.1.call-done, s32[1024]{0:T(1024)S(1)} %pad_clamp_fusion), kind=kCustom, calls=%fused_computation.4 | custom fusion | bytes 2099200 | tf_op jit(solution)/shard_map/jit(_take)/gather | solution.py:87
  71.1 4.1 %convolution_convert_fusion.1 = bf16[512,896]{1,0:T(8,128)(2,1)} fusion(bf16[896,1024]{1,0:T(8,128)(2,1)} %param.17, bf16[512,1024]{1,0:T(8,128)(2,1)S(1)} %gather_fusion, pred[512]{0:T(512)(128)(4,1)S(1)} %compare_and_fusion.2), kind=kOutput, calls=%fused_computation.25 | convolution fusion | flops 940507136 | bytes 3801600 | tf_op jit(solution)/shard_map/dot_general | solution.py:103
  75.2 3.0 %all-to-all-done.1 = bf16[8,64,2304]{2,1,0:T(8,128)(2,1)} async-done(((bf16[8,64,2304]{2,1,0:T(8,128)(2,1)}), bf16[8,64,2304]{2,1,0:T(8,128)(2,1)}, u32[]{:S(2)}, u32[]{:S(2)}) %all-to-all-start.1) | async-done | bytes 2359328 | tf_op jit(solution)/shard_map/all_to_all | solution.py:57
  78.2 8.9 %all-to-all-start.4 = ((bf16[8,64,896]{2,1,0:T(8,128)(2,1)}), bf16[8,64,896]{2,1,0:T(8,128)(2,1)S(1)}, u32[]{:S(2)}, u32[]{:S(2)}) async-start(bf16[8,64,896]{2,1,0:T(8,128)(2,1)} %bitcast.67), calls=%async_computation.4 | async-start | bytes 1835008 | tf_op jit(solution)/shard_map/all_to_all | solution.py:57
  90.0 11.5 %all-to-all-done.4 = bf16[8,64,896]{2,1,0:T(8,128)(2,1)S(1)} async-done(((bf16[8,64,896]{2,1,0:T(8,128)(2,1)}), bf16[8,64,896]{2,1,0:T(8,128)(2,1)S(1)}, u32[]{:S(2)}, u32[]{:S(2)}) %all-to-all-start.4) | async-done | bytes 917536 | tf_op jit(solution)/shard_map/all_to_all | solution.py:57
  104.7 3.7 %all-to-all-start.2 = ((bf16[8,64,1408]{2,1,0:T(8,128)(2,1)}), bf16[8,64,1408]{2,1,0:T(8,128)(2,1)S(1)}, u32[]{:S(2)}, u32[]{:S(2)}) async-start(bf16[8,64,1408]{2,1,0:T(8,128)(2,1)} %broadcast_in_dim.44), calls=%async_computation.2 | async-start | bytes 2883584 | tf_op jit(solution)/shard_map/all_to_all | solution.py:63
  110.1 18.9 %all-to-all-done.2 = bf16[8,64,1408]{2,1,0:T(8,128)(2,1)S(1)} async-done(((bf16[8,64,1408]{2,1,0:T(8,128)(2,1)}), bf16[8,64,1408]{2,1,0:T(8,128)(2,1)S(1)}, u32[]{:S(2)}, u32[]{:S(2)}) %all-to-all-start.2) | async-done | bytes 1441824 | tf_op jit(solution)/shard_map/all_to_all | solution.py:63
  131.6 4.5 %all-to-all-start.5 = ((bf16[8,64,1792]{2,1,0:T(8,128)(2,1)}), bf16[8,64,1792]{2,1,0:T(8,128)(2,1)}, u32[]{:S(2)}, u32[]{:S(2)}) async-start(bf16[8,64,1792]{2,1,0:T(8,128)(2,1)} %broadcast_in_dim.51), calls=%async_computation.5 | async-start | bytes 3670016 | tf_op jit(solution)/shard_map/all_to_all | solution.py:63
  138.6 3.0 %convolution_convert_fusion = bf16[512,1024]{1,0:T(8,128)(2,1)S(1)} fusion(bf16[896,1024]{1,0:T(8,128)(2,1)} %param.17, bf16[512,1408]{1,0:T(8,128)(2,1)} %bitcast.61), kind=kOutput, calls=%fused_computation.22 | convolution fusion | flops 940048384 | bytes 3801088 | tf_op jit(solution)/shard_map/dot_general | solution.py:100
  141.7 5.3 %gather_fusion.2 = bf16[1024,1024]{1,0:T(8,128)(2,1)} fusion(bf16[512,1024]{1,0:T(8,128)(2,1)S(1)} %convolution_convert_fusion, s32[1024]{0:T(1024)S(1)} %fusion.38), kind=kCustom, calls=%fused_computation.clone | custom fusion | bytes 4198400 | tf_op jit(solution)/shard_map/jit(_take)/gather | solution.py:69
  147.0 14.8 %all-to-all-done.5 = bf16[8,64,1792]{2,1,0:T(8,128)(2,1)} async-done(((bf16[8,64,1792]{2,1,0:T(8,128)(2,1)}), bf16[8,64,1792]{2,1,0:T(8,128)(2,1)}, u32[]{:S(2)}, u32[]{:S(2)}) %all-to-all-start.5) | async-done | bytes 1835040 | tf_op jit(solution)/shard_map/all_to_all | solution.py:63
  161.9 3.2 %fusion.31 = f32[512,1024]{1,0:T(8,128)S(1)} fusion(bf16[1024,896]{1,0:T(8,128)(2,1)} %param.15, bf16[512,1792]{1,0:T(8,128)(2,1)} %bitcast.11), kind=kOutput, calls=%fused_computation.40 | convolution fusion | flops 939524096 | bytes 4849664 | tf_op jit(solution)/shard_map/dot_general | solution.py:113
  167.6 5.3 %gather_fusion.5 = bf16[1024,1024]{1,0:T(8,128)(2,1)} fusion(bf16[512,1024]{1,0:T(8,128)(2,1)S(1)} %add_convert_fusion, s32[1024]{0:T(1024)S(1)} %fusion.38), kind=kCustom, calls=%fused_computation.2.clone | custom fusion | bytes 4198400 | tf_op jit(solution)/shard_map/jit(_take)/gather | solution.py:69
  172.9 2.7 %broadcast_select_fusion = (bf16[1024,1024]{1,0:T(8,128)(2,1)S(1)}, bf16[1024,1024]{1,0:T(8,128)(2,1)S(1)}) fusion(bf16[1024,1024]{1,0:T(8,128)(2,1)} %gather_fusion.5, pred[1024]{0:T(1024)(128)(4,1)S(1)} %compare_and_fusion.1, bf16[1024,1024]{1,0:T(8,128)(2,1)} %gather_fusion.2), kind=kLoop, calls=%fused_computation.13 | loop fusion | flops 2097152 | bytes 8389632 | tf_op jit(solution)/shard_map/jit(_take)/select_n | solution.py:69
  177.3 32.0 %all_to_all.35 = bf16[16,64,1024]{2,1,0:T(8,128)(2,1)} all-to-all(bf16[16,64,1024]{2,1,0:T(8,128)(2,1)S(1)} %get-tuple-element.33), channel_id=1, replica_groups=mesh['dp'=8,'fsdp'=16] {'fsdp'}, dimensions={0} | all-to-all | bytes 4194304 | tf_op jit(solution)/shard_map/all_to_all | solution.py:71
  209.3 5.8 %all-to-all-start.6 = ((bf16[16,64,1024]{2,1,0:T(8,128)(2,1)}), bf16[16,64,1024]{2,1,0:T(8,128)(2,1)}, u32[]{:S(2)}, u32[]{:S(2)}) async-start(bf16[16,64,1024]{2,1,0:T(8,128)(2,1)} %get-tuple-element.32), calls=%async_computation.6 | async-start | bytes 4194304 | tf_op jit(solution)/shard_map/all_to_all | solution.py:71
  215.2 4.6 %fusion.19 = f32[896,1024]{1,0:T(8,128)} fusion(bf16[512,1408]{1,0:T(8,128)(2,1)} %bitcast.62, bf16[512,1024]{1,0:T(8,128)(2,1)} %copy-done.5, pred[512]{0:T(512)(128)(4,1)S(1)} %copy-done.9), kind=kOutput, calls=%fused_computation.30 | convolution fusion | flops 940048384 | bytes 5636608 | tf_op jit(solution)/shard_map/dot_general | solution.py:110
  219.8 4.2 %fusion.29 = f32[896,1024]{1,0:T(8,128)} fusion(bf16[512,1024]{1,0:T(8,128)(2,1)S(1)} %bitcast.59, bf16[512,1792]{1,0:T(8,128)(2,1)} %bitcast.11), kind=kOutput, calls=%fused_computation.38 | convolution fusion | flops 939524096 | bytes 5636096 | tf_op jit(solution)/shard_map/dot_general | solution.py:111
  223.9 6.0 %subtract_bitcast_fusion.1 = f32[1024,896]{0,1:T(8,128)} fusion(f32[896,1024]{1,0:T(8,128)} %fusion.29, f32[1024,512]{1,0:T(8,128)S(1)} %copy-done, bf16[512,1792]{1,0:T(8,128)(2,1)} %bitcast.11, bf16[512,1408]{1,0:T(8,128)(2,1)} %bitcast.63), kind=kOutput, calls=%fused_computation.8 | convolution fusion | flops 1410203648 | bytes 10878976 | tf_op jit(solution)/shard_map/dot_general | solution.py:119
  230.0 5.0 %copy.25 = f32[1024,896]{1,0:T(8,128)} copy(f32[1024,896]{0,1:T(8,128)} %subtract_bitcast_fusion.1) | data formatting | bytes 7340032
  235.0 4.2 %fusion.24 = f32[896,1024]{1,0:T(8,128)} fusion(bf16[512,1024]{1,0:T(8,128)(2,1)S(1)} %bitcast.60, bf16[512,1792]{1,0:T(8,128)(2,1)} %bitcast.11), kind=kOutput, calls=%fused_computation.34 | convolution fusion | flops 939524096 | bytes 5636096 | tf_op jit(solution)/shard_map/dot_general | solution.py:112
  239.1 6.0 %subtract_bitcast_fusion = f32[1024,896]{0,1:T(8,128)} fusion(f32[896,1024]{1,0:T(8,128)} %fusion.24, f32[1024,512]{1,0:T(8,128)S(1)} %copy-done, bf16[512,1792]{1,0:T(8,128)(2,1)} %bitcast.11, bf16[512,1408]{1,0:T(8,128)(2,1)} %bitcast.64), kind=kOutput, calls=%fused_computation.7 | convolution fusion | flops 1410203648 | bytes 10878976 | tf_op jit(solution)/shard_map/dot_general | solution.py:120
  245.1 5.0 %copy.26 = f32[1024,896]{1,0:T(8,128)} copy(f32[1024,896]{0,1:T(8,128)} %subtract_bitcast_fusion) | data formatting | bytes 7340032
  250.1 2.7 %reduce_sum.115 = bf16[64,1024]{1,0:T(8,128)(2,1)} reduce(bf16[16,64,1024]{2,1,0:T(8,128)(2,1)} %all_to_all.35, bf16[]{:T(256)} %constant.74.clone.1), dimensions={0}, to_apply=%region_9.11 | reduce | flops 983040 | bytes 2228226 | tf_op jit(solution)/shard_map/reduce_sum | solution.py:72
  252.8 2.7 %reduce_sum.118 = bf16[64,1024]{1,0:T(8,128)(2,1)} reduce(bf16[16,64,1024]{2,1,0:T(8,128)(2,1)} %all-to-all-done.6, bf16[]{:T(256)} %constant.74.clone.1), dimensions={0}, to_apply=%region_12.15 | reduce | flops 983040 | bytes 2228226 | tf_op jit(solution)/shard_map/reduce_sum | solution.py:72
  (71 shorter events, 27.5 us)
Async XLA Ops:
  7.2 23.3 %copy-start = (f32[1024,512]{1,0:T(8,128)S(1)}, f32[1024,512]{1,0:T(8,128)}, u32[]{:S(2)}) copy-start(f32[1024,512]{1,0:T(8,128)} %param.18) | copy-start | bytes 6291460
  9.3 21.2 %all-to-all-start = ((bf16[16,32,1024]{2,1,0:T(8,128)(2,1)}), bf16[16,32,1024]{2,1,0:T(8,128)(2,1)S(1)}, u32[]{:S(2)}, u32[]{:S(2)}) async-start(bf16[16,32,1024]{2,1,0:T(8,128)(2,1)} %broadcast_in_dim.43), calls=%async_computation | async-start | bytes 2097152 | tf_op jit(solution)/shard_map/all_to_all | solution.py:63
  15.3 51.2 %all-gather.2.cloned.1.call-start = ((), (), s32[]{:S(2)}) async-start(), calls=%async_computation.7 | async-start | bytes 2228224 | tf_op jit(solution)/shard_map/all_gather | solution.py:86
  30.5 3.2 %copy-start.2 = (bf16[16,32,1024]{2,1,0:T(8,128)(2,1)}, bf16[16,32,1024]{2,1,0:T(8,128)(2,1)S(1)}, u32[]{:S(2)}) copy-start(bf16[16,32,1024]{2,1,0:T(8,128)(2,1)S(1)} %all-to-all-done) | copy-start | bytes 3145732
  30.5 1.9 copy-start.11
  32.4 1.5 copy-start.10
  36.7 6.7 %copy-start.7 = (s32[16,4]{0,1:T(4,128)S(1)}, s32[16,4]{0,1:T(4,128)}, u32[]{:S(2)}) copy-start(s32[16,4]{0,1:T(4,128)} %param.13) | copy-start | bytes 772
  36.7 7.0 %copy-start.1 = (s32[16,4]{0,1:T(4,128)S(1)}, s32[16,4]{0,1:T(4,128)}, u32[]{:S(2)}) copy-start(s32[16,4]{0,1:T(4,128)} %param.14) | copy-start | bytes 772
  36.7 41.5 %all-to-all-start.1 = ((bf16[8,64,2304]{2,1,0:T(8,128)(2,1)}), bf16[8,64,2304]{2,1,0:T(8,128)(2,1)}, u32[]{:S(2)}, u32[]{:S(2)}) async-start(bf16[8,64,2304]{2,1,0:T(8,128)(2,1)} %pad_maximum_fusion), calls=%async_computation.1 | async-start | bytes 4718592 | tf_op jit(solution)/shard_map/all_to_all | solution.py:57
  58.1 13.0 %copy-start.8 = (pred[512]{0:T(512)(128)(4,1)}, pred[512]{0:T(512)(128)(4,1)S(1)}, u32[]{:S(2)}) copy-start(pred[512]{0:T(512)(128)(4,1)S(1)} %compare_and_fusion.2) | copy-start | bytes 1540
  71.1 4.1 %copy-start.5 = (bf16[512,1024]{1,0:T(8,128)(2,1)}, bf16[512,1024]{1,0:T(8,128)(2,1)S(1)}, u32[]{:S(2)}) copy-start(bf16[512,1024]{1,0:T(8,128)(2,1)S(1)} %gather_fusion) | copy-start | bytes 3145732
  78.2 23.3 %all-to-all-start.4 = ((bf16[8,64,896]{2,1,0:T(8,128)(2,1)}), bf16[8,64,896]{2,1,0:T(8,128)(2,1)S(1)}, u32[]{:S(2)}, u32[]{:S(2)}) async-start(bf16[8,64,896]{2,1,0:T(8,128)(2,1)} %bitcast.67), calls=%async_computation.4 | async-start | bytes 1835008 | tf_op jit(solution)/shard_map/all_to_all | solution.py:57
  89.2 0.8 copy-start.6
  104.7 24.3 %all-to-all-start.2 = ((bf16[8,64,1408]{2,1,0:T(8,128)(2,1)}), bf16[8,64,1408]{2,1,0:T(8,128)(2,1)S(1)}, u32[]{:S(2)}, u32[]{:S(2)}) async-start(bf16[8,64,1408]{2,1,0:T(8,128)(2,1)} %broadcast_in_dim.44), calls=%async_computation.2 | async-start | bytes 2883584 | tf_op jit(solution)/shard_map/all_to_all | solution.py:63
  129.0 2.5 copy-start.4
  131.6 30.3 %all-to-all-start.5 = ((bf16[8,64,1792]{2,1,0:T(8,128)(2,1)}), bf16[8,64,1792]{2,1,0:T(8,128)(2,1)}, u32[]{:S(2)}, u32[]{:S(2)}) async-start(bf16[8,64,1792]{2,1,0:T(8,128)(2,1)} %broadcast_in_dim.51), calls=%async_computation.5 | async-start | bytes 3670016 | tf_op jit(solution)/shard_map/all_to_all | solution.py:63
  161.9 3.2 %copy-start.12 = (bf16[1024,896]{1,0:T(8,128)(2,1)S(1)}, bf16[1024,896]{1,0:T(8,128)(2,1)}, u32[]{:S(2)}) copy-start(bf16[1024,896]{1,0:T(8,128)(2,1)} %param.16) | copy-start | bytes 5505028
  209.3 5.8 %copy-start.9 = (pred[512]{0:T(512)(128)(4,1)S(1)}, pred[512]{0:T(512)(128)(4,1)}, u32[]{:S(2)}) copy-start(pred[512]{0:T(512)(128)(4,1)} %copy-done.8) | copy-start | bytes 1540
  209.3 43.5 %all-to-all-start.6 = ((bf16[16,64,1024]{2,1,0:T(8,128)(2,1)}), bf16[16,64,1024]{2,1,0:T(8,128)(2,1)}, u32[]{:S(2)}, u32[]{:S(2)}) async-start(bf16[16,64,1024]{2,1,0:T(8,128)(2,1)} %get-tuple-element.32), calls=%async_computation.6 | async-start | bytes 4194304 | tf_op jit(solution)/shard_map/all_to_all | solution.py:71
  215.1 4.6 %copy-start.3 = (bf16[16,32,1024]{2,1,0:T(8,128)(2,1)S(1)}, bf16[16,32,1024]{2,1,0:T(8,128)(2,1)}, u32[]{:S(2)}) copy-start(bf16[16,32,1024]{2,1,0:T(8,128)(2,1)} %copy-done.2) | copy-start | bytes 3145732
Sparse Core Ops, SparseCore 0:
  17.8 48.5 all-gather.1

commit v3 on v2

v3 whole, which is shorter than its diff:
```python
import functools

import jax
import jax.numpy as jnp
from jax import lax
from jax.sharding import PartitionSpec as P

MOST = 16


def deal_tables(doc_lengths, doc_dests):
    groups = doc_lengths.shape[0]
    starts = jnp.cumsum(doc_lengths, axis=1) - doc_lengths
    targets = jnp.arange(groups, dtype=jnp.int32)
    hits = (doc_dests[:, :, None] == targets[None, None, :]).astype(jnp.int32)
    loads = jnp.sum(doc_lengths[:, :, None] * hits, axis=1)
    firsts = jnp.sum(starts[:, :, None] * hits, axis=1)
    return (loads, firsts)


def token_rows(doc_lengths, doc_dests, loads, tok, recv):
    sources, ndoc = doc_lengths.shape
    starts = jnp.cumsum(doc_lengths, axis=1) - doc_lengths
    ends = starts + doc_lengths
    offsets = jnp.cumsum(loads, axis=0) - loads
    t = jnp.arange(tok, dtype=jnp.int32)
    doc_of = jnp.sum((ends[:, :, None] <= t[None, None, :]).astype(jnp.int32), axis=1)
    doc_of = jnp.minimum(doc_of, ndoc - 1)
    hit = (doc_of[:, :, None] == jnp.arange(ndoc, dtype=jnp.int32)[None, None, :]).astype(jnp.int32)
    dst = jnp.sum(hit * doc_dests[:, None, :], axis=2)
    st = jnp.sum(hit * starts[:, None, :], axis=2)
    to = (dst[:, :, None] == jnp.arange(sources, dtype=jnp.int32)[None, None, :]).astype(jnp.int32)
    off = jnp.sum(to * offsets[:, None, :], axis=2)
    row = dst * recv + off + t[None, :] - st
    return row.reshape(-1)


def settle(term):
    return lax.optimization_barrier(term.astype(jnp.bfloat16)).astype(jnp.float32)


def reduce_rows(part, axis, n):
    rows, cols = part.shape
    got = lax.all_to_all(part.astype(jnp.bfloat16).reshape(n, rows // n, cols), axis, 0, 0, tiled=True)
    return jnp.sum(got.astype(jnp.float32), axis=0)


def gather_rows(block, axis, n):
    rows, cols = block.shape
    got = lax.all_to_all(jnp.broadcast_to(block[None], (n, rows, cols)), axis, 0, 0, tiled=True)
    return got.reshape(n * rows, cols)


def reduce_dealt(part, pick, blocks):
    cols = part.shape[1]
    contract_rows = (((0,), (0,)), ((), ()))
    send = lax.dot_general(pick, part.astype(jnp.bfloat16), contract_rows, preferred_element_type=jnp.float32)
    send = send.astype(jnp.bfloat16).reshape(blocks, -1, cols)
    got = lax.all_to_all(send, "fsdp", 0, 0, tiled=True)
    return jnp.sum(got.astype(jnp.float32), axis=0).astype(jnp.bfloat16)


def per_device(n_dp, n_fsdp, x_src, doc_lengths, doc_dests, w_gate, w_up, w_down, basis, out_cotangent):
    hidden_width = w_gate.shape[1]
    tok = x_src.shape[0]
    recv = out_cotangent.shape[0]
    loads, firsts = deal_tables(doc_lengths, doc_dests)
    rows_of = token_rows(doc_lengths, doc_dests, loads, tok, recv)
    dealt_rows = jnp.arange(n_fsdp * recv, dtype=jnp.int32)
    pick = (rows_of[:, None] == dealt_rows[None, :]).astype(jnp.bfloat16)
    contract_rows = (((0,), (0,)), ((), ()))
    contract_cols = (((1,), (1,)), ((), ()))

    xall = gather_rows(x_src, "fsdp", n_fsdp)
    dy_dealt = lax.all_gather(out_cotangent, "fsdp", axis=0, tiled=True)
    dyall = jnp.dot(pick, dy_dealt, preferred_element_type=jnp.float32).astype(jnp.bfloat16)
    first = jnp.dot(xall, w_gate, preferred_element_type=jnp.float32)
    second = jnp.dot(xall, w_up, preferred_element_type=jnp.float32)
    keys_local = jnp.dot(xall, basis, preferred_element_type=jnp.float32)
    both = reduce_rows(jnp.concatenate([first, second, keys_local], axis=1), "dp", n_dp)
    gate = both[:, :hidden_width]
    up = both[:, hidden_width:2 * hidden_width]
    keys = both[:, 2 * hidden_width:].astype(jnp.bfloat16)
    sig = jax.nn.sigmoid(gate)
    hidden = (gate * sig * up).astype(jnp.bfloat16)
    gathered = gather_rows(jnp.concatenate([hidden, keys], axis=1), "dp", n_dp)
    hall = gathered[:, :hidden_width]
    keys_all = gathered[:, hidden_width:]
    out_part = jnp.dot(hall, w_down, preferred_element_type=jnp.float32)
    layer_out = reduce_dealt(out_part, pick, n_fsdp)

    hg_part = lax.dot_general(dyall, w_down, contract_cols, preferred_element_type=jnp.float32)
    hidden_grad = reduce_rows(hg_part, "dp", n_dp)
    gate_grad = (hidden_grad * up * sig * (1.0 + gate * (1.0 - sig))).astype(jnp.bfloat16)
    up_grad = (hidden_grad * gate * sig).astype(jnp.bfloat16)
    grads = gather_rows(jnp.concatenate([gate_grad, up_grad], axis=1), "dp", n_dp)
    gate_all = grads[:, :hidden_width]
    up_all = grads[:, hidden_width:]
    grad_down = lax.dot_general(hall, dyall, contract_rows, preferred_element_type=jnp.float32)
    total = lax.dot_general(gate_all, w_gate, contract_cols, preferred_element_type=jnp.float32)
    total = total + lax.dot_general(up_all, w_up, contract_cols, preferred_element_type=jnp.float32)
    input_grad = reduce_dealt(total, pick, n_fsdp)

    x_t = xall.T.astype(jnp.float32)
    keys_t = lax.dot_general(basis, keys_all, contract_cols, preferred_element_type=jnp.float32)
    xp_t = (x_t - keys_t).astype(jnp.bfloat16)
    grad_gate = jnp.dot(xp_t, gate_all, preferred_element_type=jnp.float32)
    grad_up = jnp.dot(xp_t, up_all, preferred_element_type=jnp.float32)
    return (layer_out, input_grad, grad_gate, grad_up, grad_down)


def solution(mesh):
    body = functools.partial(per_device, mesh.shape["dp"], mesh.shape["fsdp"])
    return jax.shard_map(
        body,
        mesh=mesh,
        in_specs=(
            P("fsdp", "dp"),
            P(),
            P(),
            P("dp", "fsdp"),
            P("dp", "fsdp"),
            P("fsdp", "dp"),
            P("dp", None),
            P("fsdp", "dp"),
        ),
        out_specs=(
            P("fsdp", "dp"),
            P("fsdp", "dp"),
            P("dp", "fsdp"),
            P("dp", "fsdp"),
            P("fsdp", "dp"),
        ),
        check_vma=False,
    )
```

time: 265 us -> 240 us (0.906)
  local copies, waits for them, and re-layouts: 47.1 us -> 6.47 us
  waiting for transfers between devices: 71.7 us -> 110 us
  blocking collectives: 32 us -> 24.3 us
  other arithmetic: 20.4 us -> 13.5 us
  starting transfers between devices: 35.7 us -> 31.7 us
    gather x11 -> x0, local copies, waits for them, and re-layouts: 28.8 us -> none  [the longest x2 10.7 us: reduce_dealt(): jnp.take(part.astype(jnp.bfloat16), index, axis=0)]
    all_to_all x1 -> x2, waiting for transfers between devices: 0.01 us -> 28.3 us  [reduce_dealt(): got = lax.all_to_all(send, 'fsdp', 0, 0, tiled=True)]
    all_to_all x2, waiting for transfers between devices: 14.5 us -> 37.8 us  [reduce_rows(): lax.all_to_all(part.astype(jnp.bfloat16).reshape(n, rows // n, cols), axi...]
    unnamed x28 -> x18, local copies, waits for them, and re-layouts: 12.3 us -> 2.86 us
    all_to_all x1, blocking collectives: 32 us -> 24.3 us  [gather_rows(): lax.all_to_all(jnp.broadcast_to(block[None], (n, rows, cols)), axis, 0, 0...]
    all_to_all x3 -> x2, waiting for transfers between devices: 48.2 us -> 40.9 us  [gather_rows(): lax.all_to_all(jnp.broadcast_to(block[None], (n, rows, cols)), axis, 0, 0...]
    all_gather x1, waiting for transfers between devices: 8.34 us -> 2.1 us  [per_device(): dy_dealt = lax.all_gather(out_cotangent, 'fsdp', axis=0, tiled=True)]
    all_to_all x1 -> x2, starting transfers between devices: 5.82 us -> 11.7 us  [reduce_dealt(): got = lax.all_to_all(send, 'fsdp', 0, 0, tiled=True)]
  transfers between devices with their start and end apart: 7 -> 7, of which waited for: 6 -> 7; matrix products, arithmetic and copies ran while one was open for 31% -> 20% of each run, Pallas kernels for 0% -> 0%
where the time goes in v3:
time: 240 us; the launch traced here: 239 us
  waiting for transfers between devices  110 us (46%)
  matrix products  39.1 us (16%)
  starting transfers between devices  31.7 us (13%)
  blocking collectives  24.3 us (10%)
  between operations  14.2 us (6%)
  other arithmetic  13.5 us (6%)
  local copies, waits for them, and re-layouts  6.47 us (3%)
    all_to_all x2, waiting for transfers between devices, gather_rows(): lax.all_to_all(jnp.broadcast_to(block[None], (n, rows, cols)), axis, 0, 0...  40.9 us
    all_to_all x2, waiting for transfers between devices, reduce_rows(): lax.all_to_all(part.astype(jnp.bfloat16).reshape(n, rows // n, cols), axi...  37.8 us
    all_to_all x2, waiting for transfers between devices, reduce_dealt(): got = lax.all_to_all(send, 'fsdp', 0, 0, tiled=True)  28.3 us
    all_to_all x1, blocking collectives, gather_rows(): lax.all_to_all(jnp.broadcast_to(block[None], (n, rows, cols)), axis, 0, 0...  24.3 us
    all_to_all x2, starting transfers between devices, reduce_dealt(): got = lax.all_to_all(send, 'fsdp', 0, 0, tiled=True)  11.7 us
    dot_general x2, matrix products, reduce_dealt(): lax.dot_general(pick, part.astype(jnp.bfloat16), contract_rows, preferred...  11.6 us
    all_to_all x2, starting transfers between devices, reduce_rows(): lax.all_to_all(part.astype(jnp.bfloat16).reshape(n, rows // n, cols), axi...  11.4 us
    all_to_all x2, starting transfers between devices, gather_rows(): lax.all_to_all(jnp.broadcast_to(block[None], (n, rows, cols)), axis, 0, 0...  8.61 us
  transfers between devices with their start and end apart: 7, of which 7 were waited for; matrix products, arithmetic and copies ran while one was open for 20% of the time, Pallas kernels for 0%

profile of v3, /device:TPU:33, one launch (start us, length us, event | category | flops | bytes accessed | tf_op | source)
XLA Modules:
  0.0 239.0 jit_solution(17484503428554494101)
XLA Ops:
  8.9 24.3 %all_to_all.35 = bf16[16,32,1024]{2,1,0:T(8,128)(2,1)S(1)} all-to-all(bf16[16,32,1024]{2,1,0:T(8,128)(2,1)S(1)} %broadcast_in_dim.6), channel_id=1, replica_groups=mesh['dp'=8,'fsdp'=16] {'fsdp'}, dimensions={0} | all-to-all | bytes 2097152 | tf_op jit(solution)/shard_map/all_to_all | solution.py:50
  34.6 1.3 fusion.16
  36.2 1.3 fusion.13
  37.4 1.6 pad_maximum_fusion
  39.0 7.1 %all-to-all-start.1 = ((bf16[8,64,2304]{2,1,0:T(8,128)(2,1)}), bf16[8,64,2304]{2,1,0:T(8,128)(2,1)}, u32[]{:S(2)}, u32[]{:S(2)}) async-start(bf16[8,64,2304]{2,1,0:T(8,128)(2,1)} %pad_maximum_fusion), calls=%async_computation.1 | async-start | bytes 4718592 | tf_op jit(solution)/shard_map/all_to_all | solution.py:44
  46.7 2.1 all-gather.2.cloned.1.call-done
  48.8 3.0 %fusion.12 = bf16[512,1024]{1,0:T(8,128)(2,1)S(1)} fusion(bf16[1024,1024]{1,0:T(8,128)(2,1)} %all-gather.2.cloned.1.call-done, s32[512]{0:T(512)S(1)} %sub.30), kind=kOutput, calls=%fused_computation.18 | convolution fusion | flops 1074790400 | bytes 3147776 | tf_op jit(solution)/shard_map/dot_general | solution.py:76
  52.8 2.2 convolution_convert_fusion.1
  55.0 26.2 %all-to-all-done.1 = bf16[8,64,2304]{2,1,0:T(8,128)(2,1)} async-done(((bf16[8,64,2304]{2,1,0:T(8,128)(2,1)}), bf16[8,64,2304]{2,1,0:T(8,128)(2,1)}, u32[]{:S(2)}, u32[]{:S(2)}) %all-to-all-start.1) | async-done | bytes 2359328 | tf_op jit(solution)/shard_map/all_to_all | solution.py:44
  81.2 4.3 %all-to-all-start.4 = ((bf16[8,64,896]{2,1,0:T(8,128)(2,1)}), bf16[8,64,896]{2,1,0:T(8,128)(2,1)}, u32[]{:S(2)}, u32[]{:S(2)}) async-start(bf16[8,64,896]{2,1,0:T(8,128)(2,1)} %bitcast.51), calls=%async_computation.4 | async-start | bytes 1835008 | tf_op jit(solution)/shard_map/all_to_all | solution.py:44
  85.5 2.1 convert_reduce_fusion
  88.4 11.6 %all-to-all-done.4 = bf16[8,64,896]{2,1,0:T(8,128)(2,1)} async-done(((bf16[8,64,896]{2,1,0:T(8,128)(2,1)}), bf16[8,64,896]{2,1,0:T(8,128)(2,1)}, u32[]{:S(2)}, u32[]{:S(2)}) %all-to-all-start.4) | async-done | bytes 917536 | tf_op jit(solution)/shard_map/all_to_all | solution.py:44
  100.0 1.3 convert_reduce_fusion.1
  101.3 1.8 multiply_convert_fusion.1
  104.4 4.3 %all-to-all-start.2 = ((bf16[8,64,1408]{2,1,0:T(8,128)(2,1)}), bf16[8,64,1408]{2,1,0:T(8,128)(2,1)}, u32[]{:S(2)}, u32[]{:S(2)}) async-start(bf16[8,64,1408]{2,1,0:T(8,128)(2,1)} %broadcast_in_dim.7), calls=%async_computation.2 | async-start | bytes 2883584 | tf_op jit(solution)/shard_map/all_to_all | solution.py:50
  109.6 20.2 %all-to-all-done.2 = bf16[8,64,1408]{2,1,0:T(8,128)(2,1)} async-done(((bf16[8,64,1408]{2,1,0:T(8,128)(2,1)}), bf16[8,64,1408]{2,1,0:T(8,128)(2,1)}, u32[]{:S(2)}, u32[]{:S(2)}) %all-to-all-start.2) | async-done | bytes 1441824 | tf_op jit(solution)/shard_map/all_to_all | solution.py:50
  129.8 1.4 broadcast_in_dim.8
  131.2 4.3 %all-to-all-start.5 = ((bf16[8,64,1792]{2,1,0:T(8,128)(2,1)}), bf16[8,64,1792]{2,1,0:T(8,128)(2,1)}, u32[]{:S(2)}, u32[]{:S(2)}) async-start(bf16[8,64,1792]{2,1,0:T(8,128)(2,1)} %broadcast_in_dim.8), calls=%async_computation.5 | async-start | bytes 3670016 | tf_op jit(solution)/shard_map/all_to_all | solution.py:50
  135.5 5.4 %fusion.6 = bf16[1024,1024]{1,0:T(8,128)(2,1)} fusion(s32[512]{0:T(512)S(1)} %sub.30, bf16[896,1024]{1,0:T(8,128)(2,1)} %param.13, bf16[512,1408]{1,0:T(8,128)(2,1)} %bitcast.4), kind=kOutput, calls=%fused_computation.11 | convolution fusion | flops 2015363072 | bytes 4851712 | tf_op jit(solution)/shard_map/dot_general | solution.py:57
  141.0 20.7 %all-to-all-done.5 = bf16[8,64,1792]{2,1,0:T(8,128)(2,1)} async-done(((bf16[8,64,1792]{2,1,0:T(8,128)(2,1)}), bf16[8,64,1792]{2,1,0:T(8,128)(2,1)}, u32[]{:S(2)}, u32[]{:S(2)}) %all-to-all-start.5) | async-done | bytes 1835040 | tf_op jit(solution)/shard_map/all_to_all | solution.py:50
  161.6 7.4 %all-to-all-start.3 = ((bf16[16,64,1024]{2,1,0:T(8,128)(2,1)}), bf16[16,64,1024]{2,1,0:T(8,128)(2,1)}, u32[]{:S(2)}, u32[]{:S(2)}) async-start(bf16[16,64,1024]{2,1,0:T(8,128)(2,1)} %bitcast.50), calls=%async_computation.3 | async-start | bytes 4194304 | tf_op jit(solution)/shard_map/all_to_all | solution.py:59
  169.0 4.4 %fusion.30 = f32[512,1024]{1,0:T(8,128)} fusion(bf16[1024,896]{1,0:T(8,128)(2,1)} %param.11, bf16[512,1792]{1,0:T(8,128)(2,1)} %bitcast.7), kind=kOutput, calls=%fused_computation.32 | convolution fusion | flops 939524096 | bytes 4849664 | tf_op jit(solution)/shard_map/dot_general | solution.py:100
  173.4 6.1 %fusion.7 = bf16[1024,1024]{1,0:T(8,128)(2,1)} fusion(s32[512]{0:T(512)S(1)} %sub.30, f32[512,1024]{1,0:T(8,128)} %fusion.30, bf16[1024,896]{1,0:T(8,128)(2,1)} %param.12, bf16[512,1792]{1,0:T(8,128)(2,1)} %bitcast.7), kind=kOutput, calls=%fused_computation.12 | convolution fusion | flops 2015887360 | bytes 6948864 | tf_op jit(solution)/shard_map/dot_general | solution.py:57
  179.5 17.7 %all-to-all-done.3 = bf16[16,64,1024]{2,1,0:T(8,128)(2,1)} async-done(((bf16[16,64,1024]{2,1,0:T(8,128)(2,1)}), bf16[16,64,1024]{2,1,0:T(8,128)(2,1)}, u32[]{:S(2)}, u32[]{:S(2)}) %all-to-all-start.3) | async-done | bytes 2097184 | tf_op jit(solution)/shard_map/all_to_all | solution.py:59
  197.2 4.3 %all-to-all-start.6 = ((bf16[16,64,1024]{2,1,0:T(8,128)(2,1)}), bf16[16,64,1024]{2,1,0:T(8,128)(2,1)}, u32[]{:S(2)}, u32[]{:S(2)}) async-start(bf16[16,64,1024]{2,1,0:T(8,128)(2,1)} %bitcast.49), calls=%async_computation.6 | async-start | bytes 4194304 | tf_op jit(solution)/shard_map/all_to_all | solution.py:59
  201.5 1.9 fusion
  203.4 4.2 %fusion.32 = f32[896,1024]{1,0:T(8,128)} fusion(bf16[512,1024]{1,0:T(8,128)(2,1)S(1)} %copy-done.3, bf16[512,1408]{1,0:T(8,128)(2,1)} %bitcast.4), kind=kOutput, calls=%fused_computation.34 | convolution fusion | flops 939524096 | bytes 5636096 | tf_op jit(solution)/shard_map/dot_general | solution.py:99
  207.6 4.3 %fusion.28 = f32[1024,896]{1,0:T(8,128)} fusion(bf16[512,1024]{1,0:T(8,128)(2,1)S(1)} %fusion, bf16[512,1792]{1,0:T(8,128)(2,1)} %bitcast.7), kind=kOutput, calls=%fused_computation.30 | convolution fusion | flops 939524096 | bytes 5636096 | tf_op jit(solution)/shard_map/dot_general | solution.py:107
  211.9 4.3 %fusion.25 = f32[1024,896]{1,0:T(8,128)} fusion(bf16[512,1024]{1,0:T(8,128)(2,1)S(1)} %fusion, bf16[512,1792]{1,0:T(8,128)(2,1)} %bitcast.7), kind=kOutput, calls=%fused_computation.27 | convolution fusion | flops 939524096 | bytes 5636096 | tf_op jit(solution)/shard_map/dot_general | solution.py:108
  216.2 2.7 %reduce_sum.93 = bf16[64,1024]{1,0:T(8,128)(2,1)} reduce(bf16[16,64,1024]{2,1,0:T(8,128)(2,1)} %all-to-all-done.3, bf16[]{:T(256)} %constant.22.clone.1), dimensions={0}, to_apply=%region_8.9 | reduce | flops 983040 | bytes 2228226 | tf_op jit(solution)/shard_map/reduce_sum | solution.py:60
  218.9 10.6 %all-to-all-done.6 = bf16[16,64,1024]{2,1,0:T(8,128)(2,1)} async-done(((bf16[16,64,1024]{2,1,0:T(8,128)(2,1)}), bf16[16,64,1024]{2,1,0:T(8,128)(2,1)}, u32[]{:S(2)}, u32[]{:S(2)}) %all-to-all-start.6) | async-done | bytes 2097184 | tf_op jit(solution)/shard_map/all_to_all | solution.py:59
  229.5 2.7 %reduce_sum.95 = bf16[64,1024]{1,0:T(8,128)(2,1)} reduce(bf16[16,64,1024]{2,1,0:T(8,128)(2,1)} %all-to-all-done.6, bf16[]{:T(256)} %constant.22.clone.1), dimensions={0}, to_apply=%region_10.11 | reduce | flops 983040 | bytes 2228226 | tf_op jit(solution)/shard_map/reduce_sum | solution.py:60
  (37 shorter events, 7.9 us)
Async XLA Ops:
  7.2 26.0 %copy-start = (f32[1024,512]{1,0:T(8,128)S(1)}, f32[1024,512]{1,0:T(8,128)}, u32[]{:S(2)}) copy-start(f32[1024,512]{1,0:T(8,128)} %param.14) | copy-start | bytes 6291460
  7.2 41.6 %all-gather.2.cloned.1.call-start = ((), (), s32[]{:S(2)}) async-start(), calls=%async_computation.7 | async-start | bytes 2228224 | tf_op jit(solution)/shard_map/all_gather | solution.py:75
  33.1 1.5 copy-start.8
  34.6 1.5 copy-start.7
  39.0 7.1 %copy-start.4 = (s32[16,4]{0,1:T(4,128)S(1)}, s32[16,4]{0,1:T(4,128)}, u32[]{:S(2)}) copy-start(s32[16,4]{0,1:T(4,128)} %param.9) | copy-start | bytes 772
  39.0 7.1 %copy-start.5 = (s32[16,4]{0,1:T(4,128)S(1)}, s32[16,4]{0,1:T(4,128)}, u32[]{:S(2)}) copy-start(s32[16,4]{0,1:T(4,128)} %param.10) | copy-start | bytes 772
  39.0 42.1 %all-to-all-start.1 = ((bf16[8,64,2304]{2,1,0:T(8,128)(2,1)}), bf16[8,64,2304]{2,1,0:T(8,128)(2,1)}, u32[]{:S(2)}, u32[]{:S(2)}) async-start(bf16[8,64,2304]{2,1,0:T(8,128)(2,1)} %pad_maximum_fusion), calls=%async_computation.1 | async-start | bytes 4718592 | tf_op jit(solution)/shard_map/all_to_all | solution.py:44
  48.8 4.0 %copy-start.6 = (bf16[896,1024]{1,0:T(8,128)(2,1)S(1)}, bf16[896,1024]{1,0:T(8,128)(2,1)}, u32[]{:S(2)}) copy-start(bf16[896,1024]{1,0:T(8,128)(2,1)} %param.13) | copy-start | bytes 5505028
  51.8 1.0 copy-start.2
  81.2 18.8 %all-to-all-start.4 = ((bf16[8,64,896]{2,1,0:T(8,128)(2,1)}), bf16[8,64,896]{2,1,0:T(8,128)(2,1)}, u32[]{:S(2)}, u32[]{:S(2)}) async-start(bf16[8,64,896]{2,1,0:T(8,128)(2,1)} %bitcast.51), calls=%async_computation.4 | async-start | bytes 1835008 | tf_op jit(solution)/shard_map/all_to_all | solution.py:44
  87.5 0.8 copy-start.1
  104.4 25.5 %all-to-all-start.2 = ((bf16[8,64,1408]{2,1,0:T(8,128)(2,1)}), bf16[8,64,1408]{2,1,0:T(8,128)(2,1)}, u32[]{:S(2)}, u32[]{:S(2)}) async-start(bf16[8,64,1408]{2,1,0:T(8,128)(2,1)} %broadcast_in_dim.7), calls=%async_computation.2 | async-start | bytes 2883584 | tf_op jit(solution)/shard_map/all_to_all | solution.py:50
  131.2 30.4 %all-to-all-start.5 = ((bf16[8,64,1792]{2,1,0:T(8,128)(2,1)}), bf16[8,64,1792]{2,1,0:T(8,128)(2,1)}, u32[]{:S(2)}, u32[]{:S(2)}) async-start(bf16[8,64,1792]{2,1,0:T(8,128)(2,1)} %broadcast_in_dim.8), calls=%async_computation.5 | async-start | bytes 3670016 | tf_op jit(solution)/shard_map/all_to_all | solution.py:50
  161.6 35.5 %all-to-all-start.3 = ((bf16[16,64,1024]{2,1,0:T(8,128)(2,1)}), bf16[16,64,1024]{2,1,0:T(8,128)(2,1)}, u32[]{:S(2)}, u32[]{:S(2)}) async-start(bf16[16,64,1024]{2,1,0:T(8,128)(2,1)} %bitcast.50), calls=%async_computation.3 | async-start | bytes 4194304 | tf_op jit(solution)/shard_map/all_to_all | solution.py:59
  197.2 32.4 %all-to-all-start.6 = ((bf16[16,64,1024]{2,1,0:T(8,128)(2,1)}), bf16[16,64,1024]{2,1,0:T(8,128)(2,1)}, u32[]{:S(2)}, u32[]{:S(2)}) async-start(bf16[16,64,1024]{2,1,0:T(8,128)(2,1)} %bitcast.49), calls=%async_computation.6 | async-start | bytes 4194304 | tf_op jit(solution)/shard_map/all_to_all | solution.py:59
  201.5 1.9 copy-start.3
Sparse Core Ops, SparseCore 0:
  9.7 39.0 all-gather.1

commit v4 on v3

--- a/solution.py
+++ b/solution.py
@@ -93,7 +93,7 @@
     hidden_grad = reduce_rows(hg_part, "dp", n_dp)
     gate_grad = (hidden_grad * up * sig * (1.0 + gate * (1.0 - sig))).astype(jnp.bfloat16)
     up_grad = (hidden_grad * gate * sig).astype(jnp.bfloat16)
-    grads = gather_rows(jnp.concatenate([gate_grad, up_grad], axis=1), "dp", n_dp)
+    grads = lax.all_gather(jnp.concatenate([gate_grad, up_grad], axis=1), "dp", axis=0, tiled=True)
     gate_all = grads[:, :hidden_width]
     up_all = grads[:, hidden_width:]
     grad_down = lax.dot_general(hall, dyall, contract_rows, preferred_element_type=jnp.float32)

time: 240 us -> 238 us (level)
  blocking collectives: 24.3 us -> 49.4 us
  waiting for transfers between devices: 110 us -> 91.6 us
  matrix products: 39.1 us -> 35.6 us
  starting transfers between devices: 31.7 us -> 28.8 us
    all_to_all x2 -> x0, waiting for transfers between devices: 40.9 us -> none  [gather_rows(): lax.all_to_all(jnp.broadcast_to(block[None], (n, rows, cols)), axis, 0, 0...]
    all_gather x0 -> x1, waiting for transfers between devices: none -> 36.8 us  [per_device(): lax.all_gather(jnp.concatenate([gate_grad, up_grad], axis=1), 'dp', axis=...]
    all_to_all x1 -> x2, blocking collectives: 24.3 us -> 49.4 us  [gather_rows(): lax.all_to_all(jnp.broadcast_to(block[None], (n, rows, cols)), axis, 0, 0...]
    all_to_all x2, waiting for transfers between devices: 28.3 us -> 14.1 us  [reduce_dealt(): got = lax.all_to_all(send, 'fsdp', 0, 0, tiled=True)]
    all_to_all x2 -> x0, starting transfers between devices: 8.61 us -> none  [gather_rows(): lax.all_to_all(jnp.broadcast_to(block[None], (n, rows, cols)), axis, 0, 0...]
    all_to_all x2, starting transfers between devices: 11.7 us -> 17.4 us  [reduce_dealt(): got = lax.all_to_all(send, 'fsdp', 0, 0, tiled=True)]
    broadcast_in_dim x3 -> x2, local copies, waits for them, and re-layouts: 3.53 us -> 1.07 us  [gather_rows(): jnp.broadcast_to(block[None], (n, rows, cols))]
  transfers between devices with their start and end apart: 7 -> 6, of which waited for: 7 -> 5; matrix products, arithmetic and copies ran while one was open for 20% -> 19% of each run, Pallas kernels for 0% -> 0%
where the time goes in v4:
time: 238 us; the launch traced here: 237 us
  waiting for transfers between devices  91.6 us (38%)
  blocking collectives  49.4 us (21%)
  matrix products  35.6 us (15%)
  starting transfers between devices  28.8 us (12%)
  between operations  14.2 us (6%)
  other arithmetic  13.5 us (6%)
  local copies, waits for them, and re-layouts  4.12 us (2%)
    all_to_all x2, blocking collectives, gather_rows(): lax.all_to_all(jnp.broadcast_to(block[None], (n, rows, cols)), axis, 0, 0...  49.4 us
    all_to_all x2, waiting for transfers between devices, reduce_rows(): lax.all_to_all(part.astype(jnp.bfloat16).reshape(n, rows // n, cols), axi...  37.8 us
    all_gather x1, waiting for transfers between devices, per_device(): lax.all_gather(jnp.concatenate([gate_grad, up_grad], axis=1), 'dp', axis=...  36.8 us
    all_to_all x2, starting transfers between devices, reduce_dealt(): got = lax.all_to_all(send, 'fsdp', 0, 0, tiled=True)  17.4 us
    all_to_all x2, waiting for transfers between devices, reduce_dealt(): got = lax.all_to_all(send, 'fsdp', 0, 0, tiled=True)  14.1 us
    dot_general x2, matrix products, reduce_dealt(): lax.dot_general(pick, part.astype(jnp.bfloat16), contract_rows, preferred...  11.6 us
    all_to_all x2, starting transfers between devices, reduce_rows(): lax.all_to_all(part.astype(jnp.bfloat16).reshape(n, rows // n, cols), axi...  11.4 us
    reduce_sum x2, other arithmetic, reduce_dealt(): return jnp.sum(got.astype(jnp.float32), axis=0).astype(jnp.bfloat16)  5.34 us
  transfers between devices with their start and end apart: 6, of which 5 were waited for; matrix products, arithmetic and copies ran while one was open for 19% of the time, Pallas kernels for 0%

profile of v4, /device:TPU:33, one launch (start us, length us, event | category | flops | bytes accessed | tf_op | source)
XLA Modules:
  0.0 237.1 jit_solution(16623951701506676709)
XLA Ops:
  7.9 1.0 broadcast_in_dim.4
  8.9 24.3 %all_to_all.30 = bf16[16,32,1024]{2,1,0:T(8,128)(2,1)S(1)} all-to-all(bf16[16,32,1024]{2,1,0:T(8,128)(2,1)S(1)} %broadcast_in_dim.4), channel_id=1, replica_groups=mesh['dp'=8,'fsdp'=16] {'fsdp'}, dimensions={0} | all-to-all | bytes 2097152 | tf_op jit(solution)/shard_map/all_to_all | solution.py:50
  33.9 0.8 copy-done.9
  34.6 1.3 fusion.16
  36.2 1.3 fusion.13
  37.4 1.6 pad_maximum_fusion
  39.0 7.1 %all-to-all-start.1 = ((bf16[8,64,2304]{2,1,0:T(8,128)(2,1)}), bf16[8,64,2304]{2,1,0:T(8,128)(2,1)}, u32[]{:S(2)}, u32[]{:S(2)}) async-start(bf16[8,64,2304]{2,1,0:T(8,128)(2,1)} %pad_maximum_fusion), calls=%async_computation.1 | async-start | bytes 4718592 | tf_op jit(solution)/shard_map/all_to_all | solution.py:44
  46.7 2.1 all-gather.3.cloned.1.call-done
  48.8 3.0 %fusion.12 = bf16[512,1024]{1,0:T(8,128)(2,1)S(1)} fusion(bf16[1024,1024]{1,0:T(8,128)(2,1)} %all-gather.3.cloned.1.call-done, s32[512]{0:T(512)S(1)} %sub.30), kind=kOutput, calls=%fused_computation.18 | convolution fusion | flops 1074790400 | bytes 3147776 | tf_op jit(solution)/shard_map/dot_general | solution.py:76
  51.8 1.0 copy-done.3
  52.8 2.2 convolution_convert_fusion.1
  55.0 26.2 %all-to-all-done.1 = bf16[8,64,2304]{2,1,0:T(8,128)(2,1)} async-done(((bf16[8,64,2304]{2,1,0:T(8,128)(2,1)}), bf16[8,64,2304]{2,1,0:T(8,128)(2,1)}, u32[]{:S(2)}, u32[]{:S(2)}) %all-to-all-start.1) | async-done | bytes 2359328 | tf_op jit(solution)/shard_map/all_to_all | solution.py:44
  81.2 4.3 %all-to-all-start.4 = ((bf16[8,64,896]{2,1,0:T(8,128)(2,1)}), bf16[8,64,896]{2,1,0:T(8,128)(2,1)}, u32[]{:S(2)}, u32[]{:S(2)}) async-start(bf16[8,64,896]{2,1,0:T(8,128)(2,1)} %bitcast.53), calls=%async_computation.4 | async-start | bytes 1835008 | tf_op jit(solution)/shard_map/all_to_all | solution.py:44
  85.5 2.9 %convert_reduce_fusion = f32[64,2304]{1,0:T(8,128)} fusion(bf16[8,64,2304]{2,1,0:T(8,128)(2,1)} %all-to-all-done.1), kind=kLoop, calls=%fused_computation | loop fusion | flops 2211840 | bytes 2949120 | tf_op jit(solution)/shard_map/reduce_sum | solution.py:45
  88.4 11.6 %all-to-all-done.4 = bf16[8,64,896]{2,1,0:T(8,128)(2,1)} async-done(((bf16[8,64,896]{2,1,0:T(8,128)(2,1)}), bf16[8,64,896]{2,1,0:T(8,128)(2,1)}, u32[]{:S(2)}, u32[]{:S(2)}) %all-to-all-start.4) | async-done | bytes 917536 | tf_op jit(solution)/shard_map/all_to_all | solution.py:44
  100.0 1.3 convert_reduce_fusion.1
  101.3 1.2 multiply_convert_fusion.1
  103.2 0.9 slice.60
  104.3 25.1 %all_to_all.31 = bf16[8,64,1408]{2,1,0:T(8,128)(2,1)} all-to-all(bf16[8,64,1408]{2,1,0:T(8,128)(2,1)S(1)} %broadcast_in_dim.5), channel_id=1, replica_groups=mesh['dp'=8,'fsdp'=16] {'dp'}, dimensions={0} | all-to-all | bytes 2883584 | tf_op jit(solution)/shard_map/all_to_all | solution.py:50
  129.4 5.5 %fusion.6 = bf16[1024,1024]{1,0:T(8,128)(2,1)} fusion(s32[512]{0:T(512)S(1)} %sub.30, bf16[896,1024]{1,0:T(8,128)(2,1)} %param.13, bf16[512,1408]{1,0:T(8,128)(2,1)} %bitcast.48), kind=kOutput, calls=%fused_computation.11 | convolution fusion | flops 2015363072 | bytes 4851712 | tf_op jit(solution)/shard_map/dot_general | solution.py:57
  134.9 9.6 %all-to-all-start.3 = ((bf16[16,64,1024]{2,1,0:T(8,128)(2,1)}), bf16[16,64,1024]{2,1,0:T(8,128)(2,1)}, u32[]{:S(2)}, u32[]{:S(2)}) async-start(bf16[16,64,1024]{2,1,0:T(8,128)(2,1)} %bitcast.52), calls=%async_computation.3 | async-start | bytes 4194304 | tf_op jit(solution)/shard_map/all_to_all | solution.py:59
  144.5 36.8 %all-gather.5.cloned.1.call-done = bf16[512,1792]{1,0:T(8,128)(2,1)} async-done(((bf16[64,1792]{1,0:T(8,128)(2,1)}), bf16[512,1792]{1,0:T(8,128)(2,1)}) %all-gather.5.cloned.1.call-update) | async-done | bytes 1835024 | tf_op jit(solution)/shard_map/all_gather | solution.py:96
  181.3 4.4 %fusion.30 = f32[512,1024]{1,0:T(8,128)} fusion(bf16[1024,896]{1,0:T(8,128)(2,1)} %param.11, bf16[512,1792]{1,0:T(8,128)(2,1)} %all-gather.5.cloned.1.call-done), kind=kOutput, calls=%fused_computation.32 | convolution fusion | flops 939524096 | bytes 4849664 | tf_op jit(solution)/shard_map/dot_general | solution.py:100
  185.7 6.1 %fusion.7 = bf16[1024,1024]{1,0:T(8,128)(2,1)} fusion(s32[512]{0:T(512)S(1)} %sub.30, f32[512,1024]{1,0:T(8,128)} %fusion.30, bf16[1024,896]{1,0:T(8,128)(2,1)} %param.12, bf16[512,1792]{1,0:T(8,128)(2,1)} %all-gather.5.cloned.1.call-done), kind=kOutput, calls=%fused_computation.12 | convolution fusion | flops 2015887360 | bytes 6948864 | tf_op jit(solution)/shard_map/dot_general | solution.py:57
  191.8 7.8 %all-to-all-start.5 = ((bf16[16,64,1024]{2,1,0:T(8,128)(2,1)}), bf16[16,64,1024]{2,1,0:T(8,128)(2,1)}, u32[]{:S(2)}, u32[]{:S(2)}) async-start(bf16[16,64,1024]{2,1,0:T(8,128)(2,1)} %bitcast.51), calls=%async_computation.5 | async-start | bytes 4194304 | tf_op jit(solution)/shard_map/all_to_all | solution.py:59
  199.6 1.9 fusion
  201.5 3.0 %fusion.32 = f32[896,1024]{1,0:T(8,128)} fusion(bf16[512,1024]{1,0:T(8,128)(2,1)S(1)} %copy-done.4, bf16[512,1408]{1,0:T(8,128)(2,1)S(1)} %bitcast.50), kind=kOutput, calls=%fused_computation.34 | convolution fusion | flops 939524096 | bytes 5636096 | tf_op jit(solution)/shard_map/dot_general | solution.py:99
  204.5 3.1 %fusion.28 = f32[1024,896]{1,0:T(8,128)} fusion(bf16[512,1024]{1,0:T(8,128)(2,1)S(1)} %fusion, bf16[512,1792]{1,0:T(8,128)(2,1)S(1)} %copy-done.2), kind=kOutput, calls=%fused_computation.30 | convolution fusion | flops 939524096 | bytes 5636096 | tf_op jit(solution)/shard_map/dot_general | solution.py:107
  207.6 3.1 %fusion.25 = f32[1024,896]{1,0:T(8,128)} fusion(bf16[512,1024]{1,0:T(8,128)(2,1)S(1)} %fusion, bf16[512,1792]{1,0:T(8,128)(2,1)S(1)} %copy-done.2), kind=kOutput, calls=%fused_computation.27 | convolution fusion | flops 939524096 | bytes 5636096 | tf_op jit(solution)/shard_map/dot_general | solution.py:108
  210.8 2.7 %reduce_sum.93 = bf16[64,1024]{1,0:T(8,128)(2,1)} reduce(bf16[16,64,1024]{2,1,0:T(8,128)(2,1)} %all-to-all-done.3, bf16[]{:T(256)} %constant.22.clone.1), dimensions={0}, to_apply=%region_8.9 | reduce | flops 983040 | bytes 2228226 | tf_op jit(solution)/shard_map/reduce_sum | solution.py:60
  213.4 14.1 %all-to-all-done.5 = bf16[16,64,1024]{2,1,0:T(8,128)(2,1)} async-done(((bf16[16,64,1024]{2,1,0:T(8,128)(2,1)}), bf16[16,64,1024]{2,1,0:T(8,128)(2,1)}, u32[]{:S(2)}, u32[]{:S(2)}) %all-to-all-start.5) | async-done | bytes 2097184 | tf_op jit(solution)/shard_map/all_to_all | solution.py:59
  227.6 2.7 %reduce_sum.95 = bf16[64,1024]{1,0:T(8,128)(2,1)} reduce(bf16[16,64,1024]{2,1,0:T(8,128)(2,1)} %all-to-all-done.5, bf16[]{:T(256)} %constant.22.clone.1), dimensions={0}, to_apply=%region_10.11 | reduce | flops 983040 | bytes 2228226 | tf_op jit(solution)/shard_map/reduce_sum | solution.py:60
  (38 shorter events, 3.2 us)
Async XLA Ops:
  7.2 26.0 %copy-start = (f32[1024,512]{1,0:T(8,128)S(1)}, f32[1024,512]{1,0:T(8,128)}, u32[]{:S(2)}) copy-start(f32[1024,512]{1,0:T(8,128)} %param.14) | copy-start | bytes 6291460
  7.2 41.6 %all-gather.3.cloned.1.call-start = ((), (), s32[]{:S(2)}) async-start(), calls=%async_computation.6 | async-start | bytes 2228224 | tf_op jit(solution)/shard_map/all_gather | solution.py:75
  33.1 1.5 copy-start.9
  34.6 1.5 copy-start.8
  39.0 7.1 %copy-start.5 = (s32[16,4]{0,1:T(4,128)S(1)}, s32[16,4]{0,1:T(4,128)}, u32[]{:S(2)}) copy-start(s32[16,4]{0,1:T(4,128)} %param.9) | copy-start | bytes 772
  39.0 7.1 %copy-start.6 = (s32[16,4]{0,1:T(4,128)S(1)}, s32[16,4]{0,1:T(4,128)}, u32[]{:S(2)}) copy-start(s32[16,4]{0,1:T(4,128)} %param.10) | copy-start | bytes 772
  39.0 42.1 %all-to-all-start.1 = ((bf16[8,64,2304]{2,1,0:T(8,128)(2,1)}), bf16[8,64,2304]{2,1,0:T(8,128)(2,1)}, u32[]{:S(2)}, u32[]{:S(2)}) async-start(bf16[8,64,2304]{2,1,0:T(8,128)(2,1)} %pad_maximum_fusion), calls=%async_computation.1 | async-start | bytes 4718592 | tf_op jit(solution)/shard_map/all_to_all | solution.py:44
  48.8 4.0 %copy-start.7 = (bf16[896,1024]{1,0:T(8,128)(2,1)S(1)}, bf16[896,1024]{1,0:T(8,128)(2,1)}, u32[]{:S(2)}) copy-start(bf16[896,1024]{1,0:T(8,128)(2,1)} %param.13) | copy-start | bytes 5505028
  51.8 1.0 copy-start.3
  81.2 18.8 %all-to-all-start.4 = ((bf16[8,64,896]{2,1,0:T(8,128)(2,1)}), bf16[8,64,896]{2,1,0:T(8,128)(2,1)}, u32[]{:S(2)}, u32[]{:S(2)}) async-start(bf16[8,64,896]{2,1,0:T(8,128)(2,1)} %bitcast.53), calls=%async_computation.4 | async-start | bytes 1835008 | tf_op jit(solution)/shard_map/all_to_all | solution.py:44
  85.5 95.8 %all-gather.5.cloned.1.call-start = ((), (), s32[]{:S(2)}) async-start(), calls=%async_computation.7 | async-start | bytes 2064384 | tf_op jit(solution)/shard_map/all_gather | solution.py:96
  134.9 56.9 %all-to-all-start.3 = ((bf16[16,64,1024]{2,1,0:T(8,128)(2,1)}), bf16[16,64,1024]{2,1,0:T(8,128)(2,1)}, u32[]{:S(2)}, u32[]{:S(2)}) async-start(bf16[16,64,1024]{2,1,0:T(8,128)(2,1)} %bitcast.52), calls=%async_computation.3 | async-start | bytes 4194304 | tf_op jit(solution)/shard_map/all_to_all | solution.py:59
  191.8 35.8 %all-to-all-start.5 = ((bf16[16,64,1024]{2,1,0:T(8,128)(2,1)}), bf16[16,64,1024]{2,1,0:T(8,128)(2,1)}, u32[]{:S(2)}, u32[]{:S(2)}) async-start(bf16[16,64,1024]{2,1,0:T(8,128)(2,1)} %bitcast.51), calls=%async_computation.5 | async-start | bytes 4194304 | tf_op jit(solution)/shard_map/all_to_all | solution.py:59
  199.5 2.0 copy-start.1
  199.5 2.0 copy-start.4
  201.5 3.0 %copy-start.2 = (bf16[512,1792]{1,0:T(8,128)(2,1)S(1)}, bf16[512,1792]{1,0:T(8,128)(2,1)}, u32[]{:S(2)}) copy-start(bf16[512,1792]{1,0:T(8,128)(2,1)} %all-gather.5.cloned.1.call-done) | copy-start | bytes 5505028
Sparse Core Ops, SparseCore 0:
  9.7 39.0 all-gather.2
  103.4 77.8 all-gather.4

commit v5 on v3

--- a/solution.py
+++ b/solution.py
@@ -74,18 +74,19 @@
     xall = gather_rows(x_src, "fsdp", n_fsdp)
     dy_dealt = lax.all_gather(out_cotangent, "fsdp", axis=0, tiled=True)
     dyall = jnp.dot(pick, dy_dealt, preferred_element_type=jnp.float32).astype(jnp.bfloat16)
+    keys_part = jnp.dot(x_src, basis, preferred_element_type=jnp.float32).astype(jnp.bfloat16)
+    keys_dp = lax.all_gather(keys_part, "dp", axis=0, tiled=False)
+    keys_src = jnp.sum(keys_dp.astype(jnp.float32), axis=0).astype(jnp.bfloat16)
+    keys_all = lax.all_gather(keys_src, "fsdp", axis=0, tiled=True)
+
     first = jnp.dot(xall, w_gate, preferred_element_type=jnp.float32)
     second = jnp.dot(xall, w_up, preferred_element_type=jnp.float32)
-    keys_local = jnp.dot(xall, basis, preferred_element_type=jnp.float32)
-    both = reduce_rows(jnp.concatenate([first, second, keys_local], axis=1), "dp", n_dp)
+    both = reduce_rows(jnp.concatenate([first, second], axis=1), "dp", n_dp)
     gate = both[:, :hidden_width]
-    up = both[:, hidden_width:2 * hidden_width]
-    keys = both[:, 2 * hidden_width:].astype(jnp.bfloat16)
+    up = both[:, hidden_width:]
     sig = jax.nn.sigmoid(gate)
     hidden = (gate * sig * up).astype(jnp.bfloat16)
-    gathered = gather_rows(jnp.concatenate([hidden, keys], axis=1), "dp", n_dp)
-    hall = gathered[:, :hidden_width]
-    keys_all = gathered[:, hidden_width:]
+    hall = gather_rows(hidden, "dp", n_dp)
     out_part = jnp.dot(hall, w_down, preferred_element_type=jnp.float32)
     layer_out = reduce_dealt(out_part, pick, n_fsdp)
 

time: 240 us -> 284 us (1.18); the launches traced: 239 us -> 280 us
  blocking collectives: 24.3 us -> 94.7 us
  waiting for transfers between devices: 110 us -> 87.2 us
  other arithmetic: 13.5 us -> 9.95 us
    all_gather x0 -> x2, blocking collectives: none -> 70.1 us  [the longest x1 43.5 us: per_device(): keys_dp = lax.all_gather(keys_part, 'dp', axis=0, tiled=False)]
    all_to_all x2, waiting for transfers between devices: 28.3 us -> 17.7 us  [reduce_dealt(): got = lax.all_to_all(send, 'fsdp', 0, 0, tiled=True)]
    all_to_all x2, waiting for transfers between devices: 37.8 us -> 29.8 us  [reduce_rows(): lax.all_to_all(part.astype(jnp.bfloat16).reshape(n, rows // n, cols), axi...]
    all_to_all x2, waiting for transfers between devices: 40.9 us -> 35.4 us  [gather_rows(): lax.all_to_all(jnp.broadcast_to(block[None], (n, rows, cols)), axis, 0, 0...]
  transfers between devices with their start and end apart: 7 -> 7, of which waited for: 7 -> 6; matrix products, arithmetic and copies ran while one was open for 20% -> 16% of each run, Pallas kernels for 0% -> 0%
where the time goes in v5:
time: 284 us; the launch traced here: 280 us
  blocking collectives  94.7 us (33%)
  waiting for transfers between devices  87.2 us (31%)
  matrix products  37.4 us (13%)
  starting transfers between devices  30.8 us (11%)
  between operations  14.2 us (5%)
  other arithmetic  9.95 us (4%)
  local copies, waits for them, and re-layouts  5.27 us (2%)
    all_gather x1, blocking collectives, per_device(): keys_dp = lax.all_gather(keys_part, 'dp', axis=0, tiled=False)  43.5 us
    all_to_all x2, waiting for transfers between devices, gather_rows(): lax.all_to_all(jnp.broadcast_to(block[None], (n, rows, cols)), axis, 0, 0...  35.4 us
    all_to_all x2, waiting for transfers between devices, reduce_rows(): lax.all_to_all(part.astype(jnp.bfloat16).reshape(n, rows // n, cols), axi...  29.8 us
    all_gather x1, blocking collectives, per_device(): keys_all = lax.all_gather(keys_src, 'fsdp', axis=0, tiled=True)  26.6 us
    all_to_all x1, blocking collectives, gather_rows(): lax.all_to_all(jnp.broadcast_to(block[None], (n, rows, cols)), axis, 0, 0...  24.6 us
    all_to_all x2, waiting for transfers between devices, reduce_dealt(): got = lax.all_to_all(send, 'fsdp', 0, 0, tiled=True)  17.7 us
    all_to_all x2, starting transfers between devices, reduce_dealt(): got = lax.all_to_all(send, 'fsdp', 0, 0, tiled=True)  12.3 us
    dot_general x2, matrix products, reduce_dealt(): lax.dot_general(pick, part.astype(jnp.bfloat16), contract_rows, preferred...  11.3 us
  transfers between devices with their start and end apart: 7, of which 6 were waited for; matrix products, arithmetic and copies ran while one was open for 16% of the time, Pallas kernels for 0%

profile of v5, /device:TPU:33, one launch (start us, length us, event | category | flops | bytes accessed | tf_op | source)
XLA Modules:
  0.0 279.5 jit_solution(4151959067863245574)
XLA Ops:
  7.9 1.1 broadcast_in_dim.6
  9.0 24.6 %all_to_all.35 = bf16[16,32,1024]{2,1,0:T(8,128)(2,1)S(1)} all-to-all(bf16[16,32,1024]{2,1,0:T(8,128)(2,1)S(1)} %broadcast_in_dim.6), channel_id=1, replica_groups=mesh['dp'=8,'fsdp'=16] {'fsdp'}, dimensions={0} | all-to-all | bytes 2097152 | tf_op jit(solution)/shard_map/all_to_all | solution.py:50
  33.6 1.2 fusion.14
  35.5 1.2 fusion.11
  36.8 1.4 pad_maximum_fusion
  38.1 6.8 %all-to-all-start.1 = ((bf16[8,64,1792]{2,1,0:T(8,128)(2,1)}), bf16[8,64,1792]{2,1,0:T(8,128)(2,1)}, u32[]{:S(2)}, u32[]{:S(2)}) async-start(bf16[8,64,1792]{2,1,0:T(8,128)(2,1)} %pad_maximum_fusion), calls=%async_computation.1 | async-start | bytes 3670016 | tf_op jit(solution)/shard_map/all_to_all | solution.py:44
  45.5 3.6 %all-gather.3.cloned.1.call-done = bf16[1024,1024]{1,0:T(8,128)(2,1)} async-done(((bf16[64,1024]{1,0:T(8,128)(2,1)}), bf16[1024,1024]{1,0:T(8,128)(2,1)}) %all-gather.3.cloned.1.call-update) | async-done | bytes 2097168 | tf_op jit(solution)/shard_map/all_gather | solution.py:75
  49.1 3.0 %fusion.10 = bf16[512,1024]{1,0:T(8,128)(2,1)S(1)} fusion(bf16[1024,1024]{1,0:T(8,128)(2,1)} %all-gather.3.cloned.1.call-done, s32[512]{0:T(512)S(1)} %sub.30), kind=kOutput, calls=%fused_computation.16 | convolution fusion | flops 1074790400 | bytes 3147776 | tf_op jit(solution)/shard_map/dot_general | solution.py:76
  53.2 2.2 convolution_convert_fusion.1
  55.4 17.4 %all-to-all-done.1 = bf16[8,64,1792]{2,1,0:T(8,128)(2,1)} async-done(((bf16[8,64,1792]{2,1,0:T(8,128)(2,1)}), bf16[8,64,1792]{2,1,0:T(8,128)(2,1)}, u32[]{:S(2)}, u32[]{:S(2)}) %all-to-all-start.1) | async-done | bytes 1835040 | tf_op jit(solution)/shard_map/all_to_all | solution.py:44
  72.8 3.6 %all-to-all-start.4 = ((bf16[8,64,896]{2,1,0:T(8,128)(2,1)}), bf16[8,64,896]{2,1,0:T(8,128)(2,1)S(1)}, u32[]{:S(2)}, u32[]{:S(2)}) async-start(bf16[8,64,896]{2,1,0:T(8,128)(2,1)} %bitcast.44), calls=%async_computation.4 | async-start | bytes 1835008 | tf_op jit(solution)/shard_map/all_to_all | solution.py:44
  76.3 1.8 convert_reduce_fusion
  78.1 12.4 %all-to-all-done.4 = bf16[8,64,896]{2,1,0:T(8,128)(2,1)S(1)} async-done(((bf16[8,64,896]{2,1,0:T(8,128)(2,1)}), bf16[8,64,896]{2,1,0:T(8,128)(2,1)S(1)}, u32[]{:S(2)}, u32[]{:S(2)}) %all-to-all-start.4) | async-done | bytes 917536 | tf_op jit(solution)/shard_map/all_to_all | solution.py:44
  92.5 3.9 %all-to-all-start.2 = ((bf16[8,64,896]{2,1,0:T(8,128)(2,1)}), bf16[8,64,896]{2,1,0:T(8,128)(2,1)S(1)}, u32[]{:S(2)}, u32[]{:S(2)}) async-start(bf16[8,64,896]{2,1,0:T(8,128)(2,1)} %broadcast_in_dim.7), calls=%async_computation.2 | async-start | bytes 1835008 | tf_op jit(solution)/shard_map/all_to_all | solution.py:50
  96.5 14.1 %all-to-all-done.2 = bf16[8,64,896]{2,1,0:T(8,128)(2,1)S(1)} async-done(((bf16[8,64,896]{2,1,0:T(8,128)(2,1)}), bf16[8,64,896]{2,1,0:T(8,128)(2,1)S(1)}, u32[]{:S(2)}, u32[]{:S(2)}) %all-to-all-start.2) | async-done | bytes 917536 | tf_op jit(solution)/shard_map/all_to_all | solution.py:50
  110.6 1.4 broadcast_in_dim.8
  111.9 4.3 %all-to-all-start.5 = ((bf16[8,64,1792]{2,1,0:T(8,128)(2,1)}), bf16[8,64,1792]{2,1,0:T(8,128)(2,1)}, u32[]{:S(2)}, u32[]{:S(2)}) async-start(bf16[8,64,1792]{2,1,0:T(8,128)(2,1)} %broadcast_in_dim.8), calls=%async_computation.5 | async-start | bytes 3670016 | tf_op jit(solution)/shard_map/all_to_all | solution.py:50
  116.3 5.2 %fusion.4 = bf16[1024,1024]{1,0:T(8,128)(2,1)} fusion(s32[512]{0:T(512)S(1)} %sub.30, bf16[512,896]{1,0:T(8,128)(2,1)S(1)} %bitcast.36, bf16[896,1024]{1,0:T(8,128)(2,1)} %param.13), kind=kOutput, calls=%fused_computation.8 | convolution fusion | flops 2015363072 | bytes 4851712 | tf_op jit(solution)/shard_map/dot_general | solution.py:57
  121.4 21.2 %all-to-all-done.5 = bf16[8,64,1792]{2,1,0:T(8,128)(2,1)} async-done(((bf16[8,64,1792]{2,1,0:T(8,128)(2,1)}), bf16[8,64,1792]{2,1,0:T(8,128)(2,1)}, u32[]{:S(2)}, u32[]{:S(2)}) %all-to-all-start.5) | async-done | bytes 1835040 | tf_op jit(solution)/shard_map/all_to_all | solution.py:50
  142.7 7.7 %all-to-all-start.3 = ((bf16[16,64,1024]{2,1,0:T(8,128)(2,1)}), bf16[16,64,1024]{2,1,0:T(8,128)(2,1)}, u32[]{:S(2)}, u32[]{:S(2)}) async-start(bf16[16,64,1024]{2,1,0:T(8,128)(2,1)} %bitcast.42), calls=%async_computation.3 | async-start | bytes 4194304 | tf_op jit(solution)/shard_map/all_to_all | solution.py:59
  150.4 4.4 %fusion.25 = f32[512,1024]{1,0:T(8,128)} fusion(bf16[1024,896]{1,0:T(8,128)(2,1)} %param.11, bf16[512,1792]{1,0:T(8,128)(2,1)} %bitcast.6), kind=kOutput, calls=%fused_computation.30 | convolution fusion | flops 939524096 | bytes 4849664 | tf_op jit(solution)/shard_map/dot_general | solution.py:101
  154.8 6.1 %fusion.5 = bf16[1024,1024]{1,0:T(8,128)(2,1)} fusion(s32[512]{0:T(512)S(1)} %sub.30, f32[512,1024]{1,0:T(8,128)} %fusion.25, bf16[1024,896]{1,0:T(8,128)(2,1)} %param.12, bf16[512,1792]{1,0:T(8,128)(2,1)} %bitcast.6), kind=kOutput, calls=%fused_computation.9 | convolution fusion | flops 2015887360 | bytes 6948864 | tf_op jit(solution)/shard_map/dot_general | solution.py:57
  160.9 17.7 %all-to-all-done.3 = bf16[16,64,1024]{2,1,0:T(8,128)(2,1)} async-done(((bf16[16,64,1024]{2,1,0:T(8,128)(2,1)}), bf16[16,64,1024]{2,1,0:T(8,128)(2,1)}, u32[]{:S(2)}, u32[]{:S(2)}) %all-to-all-start.3) | async-done | bytes 2097184 | tf_op jit(solution)/shard_map/all_to_all | solution.py:59
  178.6 4.6 %all-to-all-start.6 = ((bf16[16,64,1024]{2,1,0:T(8,128)(2,1)}), bf16[16,64,1024]{2,1,0:T(8,128)(2,1)}, u32[]{:S(2)}, u32[]{:S(2)}) async-start(bf16[16,64,1024]{2,1,0:T(8,128)(2,1)} %bitcast.41), calls=%async_computation.6 | async-start | bytes 4194304 | tf_op jit(solution)/shard_map/all_to_all | solution.py:59
  183.4 43.5 %all-gather = bf16[256,512]{1,0:T(8,128)(2,1)S(1)} all-gather(bf16[32,512]{1,0:T(8,128)(2,1)S(1)} %fusion.30), channel_id=2, replica_groups=mesh['dp'=8,'fsdp'=16] {'dp'}, dimensions={0}, use_global_device_ids=true | all-gather | bytes 294912 | tf_op jit(solution)/shard_map/all_gather | solution.py:78
  227.0 26.6 %all_gather.15 = bf16[512,512]{1,0:T(8,128)(2,1)S(1)} all-gather(bf16[32,512]{1,0:T(8,128)(2,1)S(1)} %reduce_sum.108), channel_id=1, replica_groups=mesh['dp'=8,'fsdp'=16] {'fsdp'}, dimensions={0}, use_global_device_ids=true | all-gather | bytes 557056 | tf_op jit(solution)/shard_map/all_gather | solution.py:80
  253.6 2.1 fusion
  255.7 3.0 %fusion.29 = f32[896,1024]{1,0:T(8,128)} fusion(bf16[512,896]{1,0:T(8,128)(2,1)S(1)} %bitcast.37, bf16[512,1024]{1,0:T(8,128)(2,1)S(1)} %copy-done.3), kind=kOutput, calls=%fused_computation.48 | convolution fusion | flops 939524096 | bytes 5636096 | tf_op jit(solution)/shard_map/dot_general | solution.py:100
  258.7 4.3 %fusion.23 = f32[1024,896]{1,0:T(8,128)} fusion(bf16[512,1024]{1,0:T(8,128)(2,1)S(1)} %fusion, bf16[512,1792]{1,0:T(8,128)(2,1)} %bitcast.6), kind=kOutput, calls=%fused_computation.28 | convolution fusion | flops 939524096 | bytes 5636096 | tf_op jit(solution)/shard_map/dot_general | solution.py:108
  263.0 4.3 %fusion.20 = f32[1024,896]{1,0:T(8,128)} fusion(bf16[512,1024]{1,0:T(8,128)(2,1)S(1)} %fusion, bf16[512,1792]{1,0:T(8,128)(2,1)} %bitcast.6), kind=kOutput, calls=%fused_computation.25 | convolution fusion | flops 939524096 | bytes 5636096 | tf_op jit(solution)/shard_map/dot_general | solution.py:109
  267.3 2.7 reduce_sum.105
  270.0 2.7 reduce_sum.107
  (44 shorter events, 5.3 us)
Async XLA Ops:
  7.2 175.9 %copy-start = (f32[1024,512]{1,0:T(8,128)S(1)}, f32[1024,512]{1,0:T(8,128)}, u32[]{:S(2)}) copy-start(f32[1024,512]{1,0:T(8,128)} %param.14) | copy-start | bytes 6291460
  7.2 41.9 %all-gather.3.cloned.1.call-start = ((), (), s32[]{:S(2)}) async-start(), calls=%async_computation.7 | async-start | bytes 2228224 | tf_op jit(solution)/shard_map/all_gather | solution.py:75
  7.9 25.7 %copy-start.11 = (bf16[1024,896]{1,0:T(8,128)(2,1)S(1)}, bf16[1024,896]{1,0:T(8,128)(2,1)}, u32[]{:S(2)}) copy-start(bf16[1024,896]{1,0:T(8,128)(2,1)} %param.12) | copy-start | bytes 5505028
  33.6 1.3 copy-start.1
  33.6 1.9 copy-start.10
  38.1 6.8 %copy-start.7 = (s32[16,4]{0,1:T(4,128)S(1)}, s32[16,4]{0,1:T(4,128)}, u32[]{:S(2)}) copy-start(s32[16,4]{0,1:T(4,128)} %param.9) | copy-start | bytes 772
  38.1 6.8 %copy-start.8 = (s32[16,4]{0,1:T(4,128)S(1)}, s32[16,4]{0,1:T(4,128)}, u32[]{:S(2)}) copy-start(s32[16,4]{0,1:T(4,128)} %param.10) | copy-start | bytes 772
  38.1 34.6 %all-to-all-start.1 = ((bf16[8,64,1792]{2,1,0:T(8,128)(2,1)}), bf16[8,64,1792]{2,1,0:T(8,128)(2,1)}, u32[]{:S(2)}, u32[]{:S(2)}) async-start(bf16[8,64,1792]{2,1,0:T(8,128)(2,1)} %pad_maximum_fusion), calls=%async_computation.1 | async-start | bytes 3670016 | tf_op jit(solution)/shard_map/all_to_all | solution.py:44
  49.1 4.1 %copy-start.9 = (bf16[896,1024]{1,0:T(8,128)(2,1)S(1)}, bf16[896,1024]{1,0:T(8,128)(2,1)}, u32[]{:S(2)}) copy-start(bf16[896,1024]{1,0:T(8,128)(2,1)} %param.13) | copy-start | bytes 5505028
  52.1 1.0 copy-start.2
  72.8 17.8 %all-to-all-start.4 = ((bf16[8,64,896]{2,1,0:T(8,128)(2,1)}), bf16[8,64,896]{2,1,0:T(8,128)(2,1)S(1)}, u32[]{:S(2)}, u32[]{:S(2)}) async-start(bf16[8,64,896]{2,1,0:T(8,128)(2,1)} %bitcast.44), calls=%async_computation.4 | async-start | bytes 1835008 | tf_op jit(solution)/shard_map/all_to_all | solution.py:44
  91.5 4.9 %copy-start.4 = (bf16[64,896]{1,0:T(8,128)(2,1)S(1)}, bf16[64,896]{1,0:T(8,128)(2,1)}, u32[]{:S(2)}) copy-start(bf16[64,896]{1,0:T(8,128)(2,1)} %get-tuple-element.7) | copy-start | bytes 344068
  91.5 4.9 %copy-start.5 = (bf16[64,896]{1,0:T(8,128)(2,1)S(1)}, bf16[64,896]{1,0:T(8,128)(2,1)}, u32[]{:S(2)}) copy-start(bf16[64,896]{1,0:T(8,128)(2,1)} %get-tuple-element.8) | copy-start | bytes 344068
  92.5 18.1 %all-to-all-start.2 = ((bf16[8,64,896]{2,1,0:T(8,128)(2,1)}), bf16[8,64,896]{2,1,0:T(8,128)(2,1)S(1)}, u32[]{:S(2)}, u32[]{:S(2)}) async-start(bf16[8,64,896]{2,1,0:T(8,128)(2,1)} %broadcast_in_dim.7), calls=%async_computation.2 | async-start | bytes 1835008 | tf_op jit(solution)/shard_map/all_to_all | solution.py:50
  111.9 30.7 %all-to-all-start.5 = ((bf16[8,64,1792]{2,1,0:T(8,128)(2,1)}), bf16[8,64,1792]{2,1,0:T(8,128)(2,1)}, u32[]{:S(2)}, u32[]{:S(2)}) async-start(bf16[8,64,1792]{2,1,0:T(8,128)(2,1)} %broadcast_in_dim.8), calls=%async_computation.5 | async-start | bytes 3670016 | tf_op jit(solution)/shard_map/all_to_all | solution.py:50
  142.7 35.9 %all-to-all-start.3 = ((bf16[16,64,1024]{2,1,0:T(8,128)(2,1)}), bf16[16,64,1024]{2,1,0:T(8,128)(2,1)}, u32[]{:S(2)}, u32[]{:S(2)}) async-start(bf16[16,64,1024]{2,1,0:T(8,128)(2,1)} %bitcast.42), calls=%async_computation.3 | async-start | bytes 4194304 | tf_op jit(solution)/shard_map/all_to_all | solution.py:59
  178.5 4.6 %copy-start.6 = (bf16[32,1024]{1,0:T(8,128)(2,1)S(1)}, bf16[32,1024]{1,0:T(8,128)(2,1)}, u32[]{:S(2)}) copy-start(bf16[32,1024]{1,0:T(8,128)(2,1)} %param.8) | copy-start | bytes 196612
  178.6 91.5 %all-to-all-start.6 = ((bf16[16,64,1024]{2,1,0:T(8,128)(2,1)}), bf16[16,64,1024]{2,1,0:T(8,128)(2,1)}, u32[]{:S(2)}, u32[]{:S(2)}) async-start(bf16[16,64,1024]{2,1,0:T(8,128)(2,1)} %bitcast.41), calls=%async_computation.6 | async-start | bytes 4194304 | tf_op jit(solution)/shard_map/all_to_all | solution.py:59
  253.6 2.1 copy-start.3
Sparse Core Ops, SparseCore 0:
  9.7 39.3 all-gather.2

commit v6 on v4

--- a/solution.py
+++ b/solution.py
@@ -83,23 +83,24 @@
     keys = both[:, 2 * hidden_width:].astype(jnp.bfloat16)
     sig = jax.nn.sigmoid(gate)
     hidden = (gate * sig * up).astype(jnp.bfloat16)
-    gathered = gather_rows(jnp.concatenate([hidden, keys], axis=1), "dp", n_dp)
-    hall = gathered[:, :hidden_width]
-    keys_all = gathered[:, hidden_width:]
-    out_part = jnp.dot(hall, w_down, preferred_element_type=jnp.float32)
-    layer_out = reduce_dealt(out_part, pick, n_fsdp)
 
     hg_part = lax.dot_general(dyall, w_down, contract_cols, preferred_element_type=jnp.float32)
     hidden_grad = reduce_rows(hg_part, "dp", n_dp)
     gate_grad = (hidden_grad * up * sig * (1.0 + gate * (1.0 - sig))).astype(jnp.bfloat16)
     up_grad = (hidden_grad * gate * sig).astype(jnp.bfloat16)
-    grads = lax.all_gather(jnp.concatenate([gate_grad, up_grad], axis=1), "dp", axis=0, tiled=True)
-    gate_all = grads[:, :hidden_width]
-    up_all = grads[:, hidden_width:]
+    gathered = gather_rows(jnp.concatenate([hidden, gate_grad, up_grad, keys], axis=1), "dp", n_dp)
+    hall = gathered[:, :hidden_width]
+    gate_all = gathered[:, hidden_width:2 * hidden_width]
+    up_all = gathered[:, 2 * hidden_width:3 * hidden_width]
+    keys_all = gathered[:, 3 * hidden_width:]
+    out_part = jnp.dot(hall, w_down, preferred_element_type=jnp.float32)
     grad_down = lax.dot_general(hall, dyall, contract_rows, preferred_element_type=jnp.float32)
     total = lax.dot_general(gate_all, w_gate, contract_cols, preferred_element_type=jnp.float32)
     total = total + lax.dot_general(up_all, w_up, contract_cols, preferred_element_type=jnp.float32)
-    input_grad = reduce_dealt(total, pick, n_fsdp)
+    model_width = out_part.shape[1]
+    dealt = reduce_dealt(jnp.concatenate([out_part, total], axis=1), pick, n_fsdp)
+    layer_out = dealt[:, :model_width]
+    input_grad = dealt[:, model_width:]
 
     x_t = xall.T.astype(jnp.float32)
     keys_t = lax.dot_general(basis, keys_all, contract_cols, preferred_element_type=jnp.float32)

time: 238 us -> 234 us (0.983)
  blocking collectives: 49.4 us -> 66.9 us
  starting transfers between devices: 28.8 us -> 20.1 us
  matrix products: 35.6 us -> 27.9 us
  waiting for transfers between devices: 91.6 us -> 86.5 us
  other arithmetic: 13.5 us -> 9.61 us
  local copies, waits for them, and re-layouts: 4.12 us -> 7.02 us
    all_gather x1 -> x0, waiting for transfers between devices: 36.8 us -> none  [per_device(): lax.all_gather(jnp.concatenate([gate_grad, up_grad], axis=1), 'dp', axis=...]
    all_to_all x2 -> x1, waiting for transfers between devices: 14.1 us -> 45.9 us  [reduce_dealt(): got = lax.all_to_all(send, 'fsdp', 0, 0, tiled=True)]
    all_to_all x2, blocking collectives: 49.4 us -> 66.9 us  [gather_rows(): lax.all_to_all(jnp.broadcast_to(block[None], (n, rows, cols)), axis, 0, 0...]
    all_to_all x2 -> x1, starting transfers between devices: 17.4 us -> 8.66 us  [reduce_dealt(): got = lax.all_to_all(send, 'fsdp', 0, 0, tiled=True)]
    dot_general x2 -> x1, matrix products: 11.6 us -> 4.49 us  [reduce_dealt(): lax.dot_general(pick, part.astype(jnp.bfloat16), contract_rows, preferred...]
    dot_general x1, matrix products: 4.38 us -> 1.28 us  [per_device(): lax.dot_general(gate_all, w_gate, contract_cols, preferred_element_type=j...]
    unnamed x20 -> x28, local copies, waits for them, and re-layouts: 2.05 us -> 4.87 us
    dot_general x0 -> x2, matrix products: none -> 2.55 us  [the longest x1 1.28 us: per_device(): lax.dot_general(up_all, w_up, contract_cols, preferred_element_type=jnp.f...]
  transfers between devices with their start and end apart: 6 -> 4, of which waited for: 5 -> 4; matrix products, arithmetic and copies ran while one was open for 19% -> 11% of each run, Pallas kernels for 0% -> 0%
where the time goes in v6:
time: 234 us; the launch traced here: 232 us
  waiting for transfers between devices  86.5 us (37%)
  blocking collectives  66.9 us (29%)
  matrix products  27.9 us (12%)
  starting transfers between devices  20.1 us (9%)
  between operations  14.2 us (6%)
  other arithmetic  9.61 us (4%)
  local copies, waits for them, and re-layouts  7.02 us (3%)
    all_to_all x2, blocking collectives, gather_rows(): lax.all_to_all(jnp.broadcast_to(block[None], (n, rows, cols)), axis, 0, 0...  66.9 us
    all_to_all x1, waiting for transfers between devices, reduce_dealt(): got = lax.all_to_all(send, 'fsdp', 0, 0, tiled=True)  45.9 us
    all_to_all x2, waiting for transfers between devices, reduce_rows(): lax.all_to_all(part.astype(jnp.bfloat16).reshape(n, rows // n, cols), axi...  37.8 us
    all_to_all x2, starting transfers between devices, reduce_rows(): lax.all_to_all(part.astype(jnp.bfloat16).reshape(n, rows // n, cols), axi...  11.4 us
    all_to_all x1, starting transfers between devices, reduce_dealt(): got = lax.all_to_all(send, 'fsdp', 0, 0, tiled=True)  8.66 us
    unnamed x28, local copies, waits for them, and re-layouts  4.87 us
  transfers between devices with their start and end apart: 4, of which 4 were waited for; matrix products, arithmetic and copies ran while one was open for 11% of the time, Pallas kernels for 0%

profile of v6, /device:TPU:33, one launch (start us, length us, event | category | flops | bytes accessed | tf_op | source)
XLA Modules:
  0.0 232.2 jit_solution(16560645817300790128)
XLA Ops:
  7.9 1.0 broadcast_in_dim.4
  8.9 24.3 %all_to_all.25 = bf16[16,32,1024]{2,1,0:T(8,128)(2,1)S(1)} all-to-all(bf16[16,32,1024]{2,1,0:T(8,128)(2,1)S(1)} %broadcast_in_dim.4), channel_id=1, replica_groups=mesh['dp'=8,'fsdp'=16] {'fsdp'}, dimensions={0} | all-to-all | bytes 2097152 | tf_op jit(solution)/shard_map/all_to_all | solution.py:50
  33.9 0.8 copy-done.12
  34.6 1.3 fusion.15
  36.2 1.3 fusion.12
  37.4 1.6 pad_maximum_fusion
  39.0 7.1 %all-to-all-start.1 = ((bf16[8,64,2304]{2,1,0:T(8,128)(2,1)}), bf16[8,64,2304]{2,1,0:T(8,128)(2,1)}, u32[]{:S(2)}, u32[]{:S(2)}) async-start(bf16[8,64,2304]{2,1,0:T(8,128)(2,1)} %pad_maximum_fusion), calls=%async_computation.1 | async-start | bytes 4718592 | tf_op jit(solution)/shard_map/all_to_all | solution.py:44
  46.7 2.1 all-gather.2.cloned.1.call-done
  48.8 3.0 %fusion.11 = bf16[512,1024]{1,0:T(8,128)(2,1)S(1)} fusion(bf16[1024,1024]{1,0:T(8,128)(2,1)} %all-gather.2.cloned.1.call-done, s32[512]{0:T(512)S(1)} %sub.30), kind=kOutput, calls=%fused_computation.18 | convolution fusion | flops 1074790400 | bytes 3147776 | tf_op jit(solution)/shard_map/dot_general | solution.py:76
  51.8 1.0 copy-done.4
  52.8 2.2 convolution_convert_fusion.2
  55.0 26.2 %all-to-all-done.1 = bf16[8,64,2304]{2,1,0:T(8,128)(2,1)} async-done(((bf16[8,64,2304]{2,1,0:T(8,128)(2,1)}), bf16[8,64,2304]{2,1,0:T(8,128)(2,1)}, u32[]{:S(2)}, u32[]{:S(2)}) %all-to-all-start.1) | async-done | bytes 2359328 | tf_op jit(solution)/shard_map/all_to_all | solution.py:44
  81.2 4.3 %all-to-all-start.2 = ((bf16[8,64,896]{2,1,0:T(8,128)(2,1)}), bf16[8,64,896]{2,1,0:T(8,128)(2,1)}, u32[]{:S(2)}, u32[]{:S(2)}) async-start(bf16[8,64,896]{2,1,0:T(8,128)(2,1)} %bitcast.55), calls=%async_computation.2 | async-start | bytes 1835008 | tf_op jit(solution)/shard_map/all_to_all | solution.py:44
  85.5 2.1 convert_reduce_fusion
  87.5 0.8 copy-done.3
  88.4 11.6 %all-to-all-done.2 = bf16[8,64,896]{2,1,0:T(8,128)(2,1)} async-done(((bf16[8,64,896]{2,1,0:T(8,128)(2,1)}), bf16[8,64,896]{2,1,0:T(8,128)(2,1)}, u32[]{:S(2)}, u32[]{:S(2)}) %all-to-all-start.2) | async-done | bytes 917536 | tf_op jit(solution)/shard_map/all_to_all | solution.py:44
  100.0 1.3 convert_reduce_fusion.1
  101.3 1.2 multiply_convert_fusion.1
  103.0 42.6 %all_to_all.26 = bf16[8,64,3200]{2,1,0:T(8,128)(2,1)S(1)} all-to-all(bf16[8,64,3200]{2,1,0:T(8,128)(2,1)S(1)} %broadcast_in_dim.5), channel_id=1, replica_groups=mesh['dp'=8,'fsdp'=16] {'dp'}, dimensions={0} | all-to-all | bytes 6553600 | tf_op jit(solution)/shard_map/all_to_all | solution.py:50
  145.6 1.3 convolution_convert_fusion.1
  146.8 1.4 copy-done.11
  148.2 1.3 fusion.28
  149.7 1.3 add_convert_fusion
  151.0 4.5 %convolution_convert_fusion = bf16[1024,2048]{1,0:T(8,128)(2,1)} fusion(bf16[512,1024]{1,0:T(8,128)(2,1)S(1)} %add_convert_fusion, bf16[512,1024]{1,0:T(8,128)(2,1)S(1)} %convolution_convert_fusion.1, s32[512]{0:T(512)S(1)} %sub.30), kind=kOutput, calls=%fused_computation.1 | convolution fusion | flops 2154299392 | bytes 6293504 | tf_op jit(solution)/shard_map/dot_general | solution.py:57
  155.5 8.7 %all-to-all-start.4 = ((bf16[16,64,2048]{2,1,0:T(8,128)(2,1)}), bf16[16,64,2048]{2,1,0:T(8,128)(2,1)}, u32[]{:S(2)}, u32[]{:S(2)}) async-start(bf16[16,64,2048]{2,1,0:T(8,128)(2,1)} %bitcast.54), calls=%async_computation.4 | async-start | bytes 8388608 | tf_op jit(solution)/shard_map/all_to_all | solution.py:59
  164.2 1.9 fusion.3
  166.6 3.0 %fusion.30 = f32[896,1024]{1,0:T(8,128)} fusion(bf16[512,1024]{1,0:T(8,128)(2,1)S(1)} %copy-done.5, bf16[512,3200]{1,0:T(8,128)(2,1)S(1)} %bitcast.47), kind=kOutput, calls=%fused_computation.33 | convolution fusion | flops 939524096 | bytes 5636096 | tf_op jit(solution)/shard_map/dot_general | solution.py:97
  169.5 3.1 %fusion.23 = f32[1024,896]{1,0:T(8,128)} fusion(bf16[512,1024]{1,0:T(8,128)(2,1)S(1)} %fusion.3, bf16[512,3200]{1,0:T(8,128)(2,1)S(1)} %bitcast.48), kind=kOutput, calls=%fused_computation.26 | convolution fusion | flops 939524096 | bytes 5636096 | tf_op jit(solution)/shard_map/dot_general | solution.py:109
  172.6 3.1 %fusion.26 = f32[1024,896]{1,0:T(8,128)} fusion(bf16[512,1024]{1,0:T(8,128)(2,1)S(1)} %fusion.3, bf16[512,3200]{1,0:T(8,128)(2,1)S(1)} %bitcast.49), kind=kOutput, calls=%fused_computation.29 | convolution fusion | flops 939524096 | bytes 5636096 | tf_op jit(solution)/shard_map/dot_general | solution.py:108
  175.8 45.9 %all-to-all-done.4 = bf16[16,64,2048]{2,1,0:T(8,128)(2,1)} async-done(((bf16[16,64,2048]{2,1,0:T(8,128)(2,1)}), bf16[16,64,2048]{2,1,0:T(8,128)(2,1)}, u32[]{:S(2)}, u32[]{:S(2)}) %all-to-all-start.4) | async-done | bytes 4194336 | tf_op jit(solution)/shard_map/all_to_all | solution.py:59
  221.7 3.0 %reduce_sum.82 = bf16[64,2048]{1,0:T(8,128)(2,1)S(1)} reduce(bf16[16,64,2048]{2,1,0:T(8,128)(2,1)} %all-to-all-done.4, bf16[]{:T(256)} %constant.21.clone.1), dimensions={0}, to_apply=%region_9.10 | reduce | flops 1966080 | bytes 4456450 | tf_op jit(solution)/shard_map/reduce_sum | solution.py:60
  224.7 0.7 fusion.36
  (41 shorter events, 3.3 us)
Async XLA Ops:
  7.2 26.0 %copy-start = (f32[1024,512]{1,0:T(8,128)S(1)}, f32[1024,512]{1,0:T(8,128)}, u32[]{:S(2)}) copy-start(f32[1024,512]{1,0:T(8,128)} %param.14) | copy-start | bytes 6291460
  7.2 41.6 %all-gather.2.cloned.1.call-start = ((), (), s32[]{:S(2)}) async-start(), calls=%async_computation.5 | async-start | bytes 2228224 | tf_op jit(solution)/shard_map/all_gather | solution.py:75
  33.1 1.5 copy-start.12
  34.6 1.5 copy-start.10
  39.0 7.1 %copy-start.6 = (s32[16,4]{0,1:T(4,128)S(1)}, s32[16,4]{0,1:T(4,128)}, u32[]{:S(2)}) copy-start(s32[16,4]{0,1:T(4,128)} %param.9) | copy-start | bytes 772
  39.0 7.1 %copy-start.7 = (s32[16,4]{0,1:T(4,128)S(1)}, s32[16,4]{0,1:T(4,128)}, u32[]{:S(2)}) copy-start(s32[16,4]{0,1:T(4,128)} %param.10) | copy-start | bytes 772
  39.0 42.1 %all-to-all-start.1 = ((bf16[8,64,2304]{2,1,0:T(8,128)(2,1)}), bf16[8,64,2304]{2,1,0:T(8,128)(2,1)}, u32[]{:S(2)}, u32[]{:S(2)}) async-start(bf16[8,64,2304]{2,1,0:T(8,128)(2,1)} %pad_maximum_fusion), calls=%async_computation.1 | async-start | bytes 4718592 | tf_op jit(solution)/shard_map/all_to_all | solution.py:44
  48.8 4.0 %copy-start.8 = (bf16[896,1024]{1,0:T(8,128)(2,1)S(1)}, bf16[896,1024]{1,0:T(8,128)(2,1)}, u32[]{:S(2)}) copy-start(bf16[896,1024]{1,0:T(8,128)(2,1)} %param.13) | copy-start | bytes 5505028
  51.8 1.0 copy-start.4
  81.2 18.8 %all-to-all-start.2 = ((bf16[8,64,896]{2,1,0:T(8,128)(2,1)}), bf16[8,64,896]{2,1,0:T(8,128)(2,1)}, u32[]{:S(2)}, u32[]{:S(2)}) async-start(bf16[8,64,896]{2,1,0:T(8,128)(2,1)} %bitcast.55), calls=%async_computation.2 | async-start | bytes 1835008 | tf_op jit(solution)/shard_map/all_to_all | solution.py:44
  87.5 0.8 copy-start.3
  102.9 42.6 %copy-start.9 = (bf16[896,1024]{1,0:T(8,128)(2,1)S(1)}, bf16[896,1024]{1,0:T(8,128)(2,1)}, u32[]{:S(2)}) copy-start(bf16[896,1024]{1,0:T(8,128)(2,1)} %param.13) | copy-start | bytes 5505028
  145.6 4.0 %copy-start.1 = (bf16[8,64,3200]{2,1,0:T(8,128)(2,1)}, bf16[8,64,3200]{2,1,0:T(8,128)(2,1)S(1)}, u32[]{:S(2)}) copy-start(bf16[8,64,3200]{2,1,0:T(8,128)(2,1)S(1)} %all_to_all.26) | copy-start | bytes 9830404
  145.6 2.7 %copy-start.11 = (bf16[1024,896]{1,0:T(8,128)(2,1)S(1)}, bf16[1024,896]{1,0:T(8,128)(2,1)}, u32[]{:S(2)}) copy-start(bf16[1024,896]{1,0:T(8,128)(2,1)} %param.11) | copy-start | bytes 5505028
  148.2 1.5 copy-start.13
  155.5 66.2 %all-to-all-start.4 = ((bf16[16,64,2048]{2,1,0:T(8,128)(2,1)}), bf16[16,64,2048]{2,1,0:T(8,128)(2,1)}, u32[]{:S(2)}, u32[]{:S(2)}) async-start(bf16[16,64,2048]{2,1,0:T(8,128)(2,1)} %bitcast.54), calls=%async_computation.4 | async-start | bytes 8388608 | tf_op jit(solution)/shard_map/all_to_all | solution.py:59
  164.2 2.1 copy-start.2
  164.2 2.4 %copy-start.5 = (bf16[512,1024]{1,0:T(8,128)(2,1)S(1)}, bf16[512,1024]{1,0:T(8,128)(2,1)}, u32[]{:S(2)}) copy-start(bf16[512,1024]{1,0:T(8,128)(2,1)} %copy-done.4) | copy-start | bytes 3145732
Sparse Core Ops, SparseCore 0:
  9.7 39.0 all-gather.1

commit v7 on v6

--- a/solution.py
+++ b/solution.py
@@ -55,9 +55,15 @@
     cols = part.shape[1]
     contract_rows = (((0,), (0,)), ((), ()))
     send = lax.dot_general(pick, part.astype(jnp.bfloat16), contract_rows, preferred_element_type=jnp.float32)
-    send = send.astype(jnp.bfloat16).reshape(blocks, -1, cols)
-    got = lax.all_to_all(send, "fsdp", 0, 0, tiled=True)
-    return jnp.sum(got.astype(jnp.float32), axis=0).astype(jnp.bfloat16)
+    send = send.astype(jnp.bfloat16).reshape(blocks, 2, -1, cols)
+    odd = lax.axis_index("fsdp") % 2 == 1
+    keep = jnp.where(odd, send[:, 1], send[:, 0])
+    give = jnp.where(odd, send[:, 0], send[:, 1])
+    got = lax.ppermute(give, "fsdp", [(f, f ^ 1) for f in range(blocks)])
+    pair = (keep.astype(jnp.float32) + got.astype(jnp.float32)).astype(jnp.bfloat16)
+    came = lax.all_to_all(pair, "fsdp", 0, 0, tiled=True)
+    halves = jnp.sum(came.astype(jnp.float32).reshape(blocks // 2, 2, -1, cols), axis=0)
+    return halves.reshape(-1, cols).astype(jnp.bfloat16)
 
 
 def per_device(n_dp, n_fsdp, x_src, doc_lengths, doc_dests, w_gate, w_up, w_down, basis, out_cotangent):

time: 234 us -> 219 us (0.936)
  blocking collectives: 66.9 us -> 24.3 us
  waiting for transfers between devices: 86.5 us -> 104 us
  matrix products: 27.9 us -> 33.9 us
  starting transfers between devices: 20.1 us -> 23.5 us
    all_to_all x2 -> x1, blocking collectives: 66.9 us -> 24.3 us  [gather_rows(): lax.all_to_all(jnp.broadcast_to(block[None], (n, rows, cols)), axis, 0, 0...]
    all_to_all x1 -> x2, waiting for transfers between devices: 45.9 us -> 60 us  [the longest x1 46.5 us: gather_rows(): lax.all_to_all(jnp.broadcast_to(block[None], (n, rows, cols)), axis, 0, 0...]
    ppermute x0 -> x1, waiting for transfers between devices: none -> 3.79 us  [reduce_dealt(): got = lax.ppermute(give, 'fsdp', [(f, f ^ 1) for f in range(blocks)])]
    convert_element_type x0 -> x1, other arithmetic: none -> 2.69 us  [reduce_dealt(): (keep.astype(jnp.float32) + got.astype(jnp.float32)).astype(jnp.bfloat16)]
    unnamed x28 -> x22, local copies, waits for them, and re-layouts: 4.87 us -> 2.86 us
    all_to_all x1 -> x2, starting transfers between devices: 8.66 us -> 10.4 us  [the longest x1 5.8 us: reduce_dealt(): came = lax.all_to_all(pair, 'fsdp', 0, 0, tiled=True)]
  transfers between devices with their start and end apart: 4 -> 6, of which waited for: 4 -> 6; matrix products, arithmetic and copies ran while one was open for 11% -> 13% of each run, Pallas kernels for 0% -> 0%
where the time goes in v7:
time: 219 us
  waiting for transfers between devices  104 us (47%)
  matrix products  33.9 us (15%)
  blocking collectives  24.3 us (11%)
  starting transfers between devices  23.5 us (11%)
  between operations  14.3 us (7%)
  other arithmetic  11.5 us (5%)
  local copies, waits for them, and re-layouts  6.73 us (3%)
    all_to_all x1, waiting for transfers between devices, gather_rows(): lax.all_to_all(jnp.broadcast_to(block[None], (n, rows, cols)), axis, 0, 0...  46.5 us
    all_to_all x2, waiting for transfers between devices, reduce_rows(): lax.all_to_all(part.astype(jnp.bfloat16).reshape(n, rows // n, cols), axi...  37.8 us
    all_to_all x1, blocking collectives, gather_rows(): lax.all_to_all(jnp.broadcast_to(block[None], (n, rows, cols)), axis, 0, 0...  24.3 us
    all_to_all x1, waiting for transfers between devices, reduce_dealt(): came = lax.all_to_all(pair, 'fsdp', 0, 0, tiled=True)  13.4 us
    all_to_all x2, starting transfers between devices, reduce_rows(): lax.all_to_all(part.astype(jnp.bfloat16).reshape(n, rows // n, cols), axi...  11.4 us
    all_to_all x1, starting transfers between devices, reduce_dealt(): came = lax.all_to_all(pair, 'fsdp', 0, 0, tiled=True)  5.8 us
    all_to_all x1, starting transfers between devices, gather_rows(): lax.all_to_all(jnp.broadcast_to(block[None], (n, rows, cols)), axis, 0, 0...  4.62 us
  transfers between devices with their start and end apart: 6, of which 6 were waited for; matrix products, arithmetic and copies ran while one was open for 13% of the time, Pallas kernels for 0%

profile of v7, /device:TPU:33, one launch (start us, length us, event | category | flops | bytes accessed | tf_op | source)
XLA Modules:
  0.0 218.6 jit_solution(15720473858049844930)
XLA Ops:
  8.9 24.3 %all_to_all.25 = bf16[16,32,1024]{2,1,0:T(8,128)(2,1)S(1)} all-to-all(bf16[16,32,1024]{2,1,0:T(8,128)(2,1)S(1)} %broadcast_in_dim.4), channel_id=1, replica_groups=mesh['dp'=8,'fsdp'=16] {'fsdp'}, dimensions={0} | all-to-all | bytes 2097152 | tf_op jit(solution)/shard_map/all_to_all | solution.py:50
  34.6 1.3 fusion.18
  36.2 1.3 fusion.15
  37.4 1.6 pad_maximum_fusion
  39.0 7.1 %all-to-all-start.1 = ((bf16[8,64,2304]{2,1,0:T(8,128)(2,1)}), bf16[8,64,2304]{2,1,0:T(8,128)(2,1)}, u32[]{:S(2)}, u32[]{:S(2)}) async-start(bf16[8,64,2304]{2,1,0:T(8,128)(2,1)} %pad_maximum_fusion), calls=%async_computation.1 | async-start | bytes 4718592 | tf_op jit(solution)/shard_map/all_to_all | solution.py:44
  46.7 2.1 all-gather.2.cloned.1.call-done
  48.8 3.0 %fusion.14 = bf16[512,1024]{1,0:T(8,128)(2,1)S(1)} fusion(bf16[1024,1024]{1,0:T(8,128)(2,1)} %all-gather.2.cloned.1.call-done, s32[512]{0:T(512)S(1)} %sub.30), kind=kOutput, calls=%fused_computation.24 | convolution fusion | flops 1074790400 | bytes 3147776 | tf_op jit(solution)/shard_map/dot_general | solution.py:82
  51.8 1.0 copy-done.2
  52.8 2.2 %convolution_convert_fusion.2 = bf16[512,896]{1,0:T(8,128)(2,1)} fusion(bf16[512,1024]{1,0:T(8,128)(2,1)S(1)} %fusion.14, bf16[896,1024]{1,0:T(8,128)(2,1)S(1)} %copy-done.6), kind=kOutput, calls=%fused_computation.28 | convolution fusion | flops 939982848 | bytes 3801088 | tf_op jit(solution)/shard_map/dot_general | solution.py:93
  55.0 26.2 %all-to-all-done.1 = bf16[8,64,2304]{2,1,0:T(8,128)(2,1)} async-done(((bf16[8,64,2304]{2,1,0:T(8,128)(2,1)}), bf16[8,64,2304]{2,1,0:T(8,128)(2,1)}, u32[]{:S(2)}, u32[]{:S(2)}) %all-to-all-start.1) | async-done | bytes 2359328 | tf_op jit(solution)/shard_map/all_to_all | solution.py:44
  81.2 4.3 %all-to-all-start.2 = ((bf16[8,64,896]{2,1,0:T(8,128)(2,1)}), bf16[8,64,896]{2,1,0:T(8,128)(2,1)}, u32[]{:S(2)}, u32[]{:S(2)}) async-start(bf16[8,64,896]{2,1,0:T(8,128)(2,1)} %bitcast.73), calls=%async_computation.2 | async-start | bytes 1835008 | tf_op jit(solution)/shard_map/all_to_all | solution.py:44
  85.5 2.1 convert_reduce_fusion
  88.4 11.6 %all-to-all-done.2 = bf16[8,64,896]{2,1,0:T(8,128)(2,1)} async-done(((bf16[8,64,896]{2,1,0:T(8,128)(2,1)}), bf16[8,64,896]{2,1,0:T(8,128)(2,1)}, u32[]{:S(2)}, u32[]{:S(2)}) %all-to-all-start.2) | async-done | bytes 917536 | tf_op jit(solution)/shard_map/all_to_all | solution.py:44
  100.0 1.3 convert_reduce_fusion.1
  101.3 1.2 multiply_convert_fusion.1
  102.5 2.1 broadcast_in_dim.5
  104.7 4.6 %all-to-all-start.3 = ((bf16[8,64,3200]{2,1,0:T(8,128)(2,1)}), bf16[8,64,3200]{2,1,0:T(8,128)(2,1)}, u32[]{:S(2)}, u32[]{:S(2)}) async-start(bf16[8,64,3200]{2,1,0:T(8,128)(2,1)} %broadcast_in_dim.5), calls=%async_computation.3 | async-start | bytes 6553600 | tf_op jit(solution)/shard_map/all_to_all | solution.py:50
  109.3 46.5 %all-to-all-done.3 = bf16[8,64,3200]{2,1,0:T(8,128)(2,1)} async-done(((bf16[8,64,3200]{2,1,0:T(8,128)(2,1)}), bf16[8,64,3200]{2,1,0:T(8,128)(2,1)}, u32[]{:S(2)}, u32[]{:S(2)}) %all-to-all-start.3) | async-done | bytes 3276832 | tf_op jit(solution)/shard_map/all_to_all | solution.py:50
  155.8 3.2 %convolution_convert_fusion.1 = bf16[512,1024]{1,0:T(8,128)(2,1)S(1)} fusion(bf16[896,1024]{1,0:T(8,128)(2,1)} %param.13, bf16[512,3200]{1,0:T(8,128)(2,1)} %bitcast.5), kind=kOutput, calls=%fused_computation.25 | convolution fusion | flops 940048384 | bytes 3801088 | tf_op jit(solution)/shard_map/dot_general | solution.py:102
  159.0 2.6 %fusion.31 = f32[512,1024]{1,0:T(8,128)S(1)} fusion(bf16[1024,896]{1,0:T(8,128)(2,1)S(1)} %copy-done.8, bf16[512,3200]{1,0:T(8,128)(2,1)} %bitcast.5), kind=kOutput, calls=%fused_computation.37 | convolution fusion | flops 939524096 | bytes 4849664 | tf_op jit(solution)/shard_map/dot_general | solution.py:104
  161.7 2.5 %add_convert_fusion = bf16[512,1024]{1,0:T(8,128)(2,1)S(1)} fusion(f32[512,1024]{1,0:T(8,128)S(1)} %fusion.31, bf16[1024,896]{1,0:T(8,128)(2,1)S(1)} %copy-done.10, bf16[512,3200]{1,0:T(8,128)(2,1)} %bitcast.5), kind=kOutput, calls=%fused_computation.16 | convolution fusion | flops 940572672 | bytes 5898240 | tf_op jit(solution)/shard_map/dot_general | solution.py:105
  164.1 2.5 %convolution_convert_fusion = bf16[1024,2048]{1,0:T(8,128)(2,1)S(1)} fusion(bf16[512,1024]{1,0:T(8,128)(2,1)S(1)} %add_convert_fusion, bf16[512,1024]{1,0:T(8,128)(2,1)S(1)} %convolution_convert_fusion.1, s32[512]{0:T(512)S(1)} %sub.30), kind=kOutput, calls=%fused_computation.4 | convolution fusion | flops 2154299392 | bytes 6293504 | tf_op jit(solution)/shard_map/dot_general | solution.py:57
  166.9 1.7 collective-permute-start
  168.6 3.8 %collective-permute-done = bf16[16,32,2048]{2,1,0:T(8,128)(2,1)S(1)} collective-permute-done((bf16[16,32,2048]{2,1,0:T(8,128)(2,1)S(1)}, bf16[16,32,2048]{2,1,0:T(8,128)(2,1)S(1)}, u32[]{:S(2)}, u32[]{:S(2)}) %collective-permute-start) | collective-permute-done | bytes 2097184 | tf_op jit(solution)/shard_map/ppermute | solution.py:62
  172.4 2.7 %fusion = bf16[16,32,2048]{2,1,0:T(8,128)(2,1)} fusion(bf16[16,32,2048]{2,1,0:T(8,128)(2,1)S(1)} %collective-permute-done, pred[]{:T(512)S(6)} %eq.27, bf16[16,2,32,2048]{3,2,1,0:T(8,128)(2,1)S(1)} %bitcast.67), kind=kLoop, calls=%fused_computation.2 | loop fusion | flops 5242880 | bytes 8388609 | tf_op jit(solution)/shard_map/convert_element_type | solution.py:63
  175.1 5.8 %all-to-all-start.4 = ((bf16[16,32,2048]{2,1,0:T(8,128)(2,1)}), bf16[16,32,2048]{2,1,0:T(8,128)(2,1)}, u32[]{:S(2)}, u32[]{:S(2)}) async-start(bf16[16,32,2048]{2,1,0:T(8,128)(2,1)} %fusion), calls=%async_computation.4 | async-start | bytes 4194304 | tf_op jit(solution)/shard_map/all_to_all | solution.py:64
  180.9 1.9 fusion.6
  182.8 4.2 %fusion.33 = f32[896,1024]{1,0:T(8,128)} fusion(bf16[512,1024]{1,0:T(8,128)(2,1)S(1)} %copy-done.3, bf16[512,3200]{1,0:T(8,128)(2,1)} %bitcast.5), kind=kOutput, calls=%fused_computation.39 | convolution fusion | flops 939524096 | bytes 5636096 | tf_op jit(solution)/shard_map/dot_general | solution.py:103
  186.9 4.3 %fusion.26 = f32[1024,896]{1,0:T(8,128)} fusion(bf16[512,1024]{1,0:T(8,128)(2,1)S(1)} %fusion.6, bf16[512,3200]{1,0:T(8,128)(2,1)} %bitcast.5), kind=kOutput, calls=%fused_computation.32 | convolution fusion | flops 939524096 | bytes 5636096 | tf_op jit(solution)/shard_map/dot_general | solution.py:115
  191.3 4.3 %fusion.29 = f32[1024,896]{1,0:T(8,128)} fusion(bf16[512,1024]{1,0:T(8,128)(2,1)S(1)} %fusion.6, bf16[512,3200]{1,0:T(8,128)(2,1)} %bitcast.5), kind=kOutput, calls=%fused_computation.35 | convolution fusion | flops 939524096 | bytes 5636096 | tf_op jit(solution)/shard_map/dot_general | solution.py:114
  195.6 13.4 %all-to-all-done.4 = bf16[16,32,2048]{2,1,0:T(8,128)(2,1)} async-done(((bf16[16,32,2048]{2,1,0:T(8,128)(2,1)}), bf16[16,32,2048]{2,1,0:T(8,128)(2,1)}, u32[]{:S(2)}, u32[]{:S(2)}) %all-to-all-start.4) | async-done | bytes 2097184 | tf_op jit(solution)/shard_map/all_to_all | solution.py:64
  209.0 2.0 reduce
  (40 shorter events, 5.8 us)
Async XLA Ops:
  7.2 26.0 %copy-start = (f32[1024,512]{1,0:T(8,128)S(1)}, f32[1024,512]{1,0:T(8,128)}, u32[]{:S(2)}) copy-start(f32[1024,512]{1,0:T(8,128)} %param.14) | copy-start | bytes 6291460
  7.2 41.6 %all-gather.2.cloned.1.call-start = ((), (), s32[]{:S(2)}) async-start(), calls=%async_computation.5 | async-start | bytes 2228224 | tf_op jit(solution)/shard_map/all_gather | solution.py:81
  33.1 1.5 copy-start.9
  34.6 1.5 copy-start.7
  39.0 7.1 %copy-start.4 = (s32[16,4]{0,1:T(4,128)S(1)}, s32[16,4]{0,1:T(4,128)}, u32[]{:S(2)}) copy-start(s32[16,4]{0,1:T(4,128)} %param.9) | copy-start | bytes 772
  39.0 7.1 %copy-start.5 = (s32[16,4]{0,1:T(4,128)S(1)}, s32[16,4]{0,1:T(4,128)}, u32[]{:S(2)}) copy-start(s32[16,4]{0,1:T(4,128)} %param.10) | copy-start | bytes 772
  39.0 42.1 %all-to-all-start.1 = ((bf16[8,64,2304]{2,1,0:T(8,128)(2,1)}), bf16[8,64,2304]{2,1,0:T(8,128)(2,1)}, u32[]{:S(2)}, u32[]{:S(2)}) async-start(bf16[8,64,2304]{2,1,0:T(8,128)(2,1)} %pad_maximum_fusion), calls=%async_computation.1 | async-start | bytes 4718592 | tf_op jit(solution)/shard_map/all_to_all | solution.py:44
  48.8 4.0 %copy-start.6 = (bf16[896,1024]{1,0:T(8,128)(2,1)S(1)}, bf16[896,1024]{1,0:T(8,128)(2,1)}, u32[]{:S(2)}) copy-start(bf16[896,1024]{1,0:T(8,128)(2,1)} %param.13) | copy-start | bytes 5505028
  51.8 1.0 copy-start.2
  81.2 18.8 %all-to-all-start.2 = ((bf16[8,64,896]{2,1,0:T(8,128)(2,1)}), bf16[8,64,896]{2,1,0:T(8,128)(2,1)}, u32[]{:S(2)}, u32[]{:S(2)}) async-start(bf16[8,64,896]{2,1,0:T(8,128)(2,1)} %bitcast.73), calls=%async_computation.2 | async-start | bytes 1835008 | tf_op jit(solution)/shard_map/all_to_all | solution.py:44
  87.5 0.8 copy-start.1
  104.7 51.2 %all-to-all-start.3 = ((bf16[8,64,3200]{2,1,0:T(8,128)(2,1)}), bf16[8,64,3200]{2,1,0:T(8,128)(2,1)}, u32[]{:S(2)}, u32[]{:S(2)}) async-start(bf16[8,64,3200]{2,1,0:T(8,128)(2,1)} %broadcast_in_dim.5), calls=%async_computation.3 | async-start | bytes 6553600 | tf_op jit(solution)/shard_map/all_to_all | solution.py:50
  155.8 3.2 %copy-start.8 = (bf16[1024,896]{1,0:T(8,128)(2,1)S(1)}, bf16[1024,896]{1,0:T(8,128)(2,1)}, u32[]{:S(2)}) copy-start(bf16[1024,896]{1,0:T(8,128)(2,1)} %param.11) | copy-start | bytes 5505028
  159.0 2.6 %copy-start.10 = (bf16[1024,896]{1,0:T(8,128)(2,1)S(1)}, bf16[1024,896]{1,0:T(8,128)(2,1)}, u32[]{:S(2)}) copy-start(bf16[1024,896]{1,0:T(8,128)(2,1)} %param.12) | copy-start | bytes 5505028
  166.9 5.5 %collective-permute-start = (bf16[16,32,2048]{2,1,0:T(8,128)(2,1)S(1)}, bf16[16,32,2048]{2,1,0:T(8,128)(2,1)S(1)}, u32[]{:S(2)}, u32[]{:S(2)}) collective-permute-start(bf16[16,32,2048]{2,1,0:T(8,128)(2,1)S(1)} %fusion.1), channel_id=1, source_target_pairs={{0,1},{1,0},{2,3},{3,2},{4,5},{5,4},{6,7},{7,6},{8,9},{9,8},{10,11... | collective-permute-start | bytes 6291464 | tf_op jit(solution)/shard_map/ppermute | solution.py:62
  175.1 34.0 %all-to-all-start.4 = ((bf16[16,32,2048]{2,1,0:T(8,128)(2,1)}), bf16[16,32,2048]{2,1,0:T(8,128)(2,1)}, u32[]{:S(2)}, u32[]{:S(2)}) async-start(bf16[16,32,2048]{2,1,0:T(8,128)(2,1)} %fusion), calls=%async_computation.4 | async-start | bytes 4194304 | tf_op jit(solution)/shard_map/all_to_all | solution.py:64
  180.9 1.9 copy-start.3
Sparse Core Ops, SparseCore 0:
  9.7 39.0 all-gather.1

commit v8 on v7

--- a/solution.py
+++ b/solution.py
@@ -77,8 +77,19 @@
     contract_rows = (((0,), (0,)), ((), ()))
     contract_cols = (((1,), (1,)), ((), ()))
 
-    xall = gather_rows(x_src, "fsdp", n_fsdp)
-    dy_dealt = lax.all_gather(out_cotangent, "fsdp", axis=0, tiled=True)
+    half_x = tok // 2
+    half_dy = recv // 2
+    halves = jnp.stack([
+        jnp.concatenate([x_src[:half_x], out_cotangent[:half_dy]], axis=0),
+        jnp.concatenate([x_src[half_x:], out_cotangent[half_dy:]], axis=0),
+    ])
+    came = lax.all_to_all(jnp.tile(halves, (n_fsdp // 2, 1, 1)), "fsdp", 0, 0, tiled=True)
+    other = lax.ppermute(came, "fsdp", [(f, f ^ 1) for f in range(n_fsdp)])
+    odd = lax.axis_index("fsdp") % 2 == 1
+    low = jnp.where(odd, other, came)
+    high = jnp.where(odd, came, other)
+    xall = jnp.concatenate([low[:, :half_x], high[:, :half_x]], axis=1).reshape(-1, x_src.shape[1])
+    dy_dealt = jnp.concatenate([low[:, half_x:], high[:, half_x:]], axis=1).reshape(-1, x_src.shape[1])
     dyall = jnp.dot(pick, dy_dealt, preferred_element_type=jnp.float32).astype(jnp.bfloat16)
     first = jnp.dot(xall, w_gate, preferred_element_type=jnp.float32)
     second = jnp.dot(xall, w_up, preferred_element_type=jnp.float32)

time: 219 us -> 200 us (0.913)
  blocking collectives: 24.3 us -> 67.9 us
  waiting for transfers between devices: 104 us -> 63.4 us
  between operations: 14.3 us -> 0.95 us
  matrix products: 33.9 us -> 24.2 us
  starting transfers between devices: 23.5 us -> 20.5 us
  other arithmetic: 11.5 us -> 14.2 us
    all_to_all x1 -> x0, waiting for transfers between devices: 46.5 us -> none  [gather_rows(): lax.all_to_all(jnp.broadcast_to(block[None], (n, rows, cols)), axis, 0, 0...]
    all_to_all x0 -> x1, blocking collectives: none -> 26.6 us  [per_device(): lax.all_to_all(jnp.tile(halves, (n_fsdp // 2, 1, 1)), 'fsdp', 0, 0, tiled...]
    all_to_all x1, blocking collectives: 24.3 us -> 41.3 us  [gather_rows(): lax.all_to_all(jnp.broadcast_to(block[None], (n, rows, cols)), axis, 0, 0...]
    all_to_all x1 -> x0, starting transfers between devices: 4.62 us -> none  [gather_rows(): lax.all_to_all(jnp.broadcast_to(block[None], (n, rows, cols)), axis, 0, 0...]
    slice x0 -> x6, local copies, waits for them, and re-layouts: none -> 3.66 us  [the longest x1 0.93 us: per_device(): x_src[:half_x]]
    all_to_all x1, waiting for transfers between devices: 13.4 us -> 16.6 us  [reduce_dealt(): came = lax.all_to_all(pair, 'fsdp', 0, 0, tiled=True)]
    ppermute x0 -> x1, waiting for transfers between devices: none -> 3.07 us  [per_device(): other = lax.ppermute(came, 'fsdp', [(f, f ^ 1) for f in range(n_fsdp)])]
    broadcast_in_dim x2 -> x1, local copies, waits for them, and re-layouts: 3.06 us -> 0.39 us  [gather_rows(): jnp.broadcast_to(block[None], (n, rows, cols))]
  transfers between devices with their start and end apart: 6 -> 5, of which waited for: 6 -> 5; matrix products, arithmetic and copies ran while one was open for 13% -> 10% of each run, Pallas kernels for 0% -> 0%
where the time goes in v8:
time: 200 us
  blocking collectives  67.9 us (34%)
  waiting for transfers between devices  63.4 us (32%)
  matrix products  24.2 us (12%)
  starting transfers between devices  20.5 us (10%)
  other arithmetic  14.2 us (7%)
  local copies, waits for them, and re-layouts  8.41 us (4%)
    all_to_all x1, blocking collectives, gather_rows(): lax.all_to_all(jnp.broadcast_to(block[None], (n, rows, cols)), axis, 0, 0...  41.3 us
    all_to_all x2, waiting for transfers between devices, reduce_rows(): lax.all_to_all(part.astype(jnp.bfloat16).reshape(n, rows // n, cols), axi...  40 us
    all_to_all x1, blocking collectives, per_device(): lax.all_to_all(jnp.tile(halves, (n_fsdp // 2, 1, 1)), 'fsdp', 0, 0, tiled...  26.6 us
    all_to_all x1, waiting for transfers between devices, reduce_dealt(): came = lax.all_to_all(pair, 'fsdp', 0, 0, tiled=True)  16.6 us
    all_to_all x2, starting transfers between devices, reduce_rows(): lax.all_to_all(part.astype(jnp.bfloat16).reshape(n, rows // n, cols), axi...  11 us
    all_to_all x1, starting transfers between devices, reduce_dealt(): came = lax.all_to_all(pair, 'fsdp', 0, 0, tiled=True)  6.15 us
  transfers between devices with their start and end apart: 5, of which 5 were waited for; matrix products, arithmetic and copies ran while one was open for 10% of the time, Pallas kernels for 0%

profile of v8, /device:TPU:33, one launch (start us, length us, event | category | flops | bytes accessed | tf_op | source)
XLA Modules:
  0.0 199.6 jit_solution(1650588092956032890)
XLA Ops:
  0.6 0.9 fusion.44
  2.7 26.6 %all_to_all.25 = bf16[16,48,1024]{2,1,0:T(8,128)(2,1)} all-to-all(bf16[16,48,1024]{2,1,0:T(8,128)(2,1)S(1)} %bitcast.85), channel_id=1, replica_groups=mesh['dp'=8,'fsdp'=16] {'fsdp'}, dimensions={0} | all-to-all | bytes 3145728 | tf_op jit(solution)/shard_map/all_to_all | solution.py:86
  30.1 3.1 %collective-permute-done = bf16[16,48,1024]{2,1,0:T(8,128)(2,1)} collective-permute-done((bf16[16,48,1024]{2,1,0:T(8,128)(2,1)}, bf16[16,48,1024]{2,1,0:T(8,128)(2,1)}, u32[]{:S(2)}, u32[]{:S(2)}) %collective-permute-start) | collective-permute-done | bytes 1572896 | tf_op jit(solution)/shard_map/ppermute | solution.py:87
  33.1 2.1 %broadcast_select_fusion.1 = (bf16[16,48,1024]{2,1,0:T(8,128)(2,1)S(1)}, bf16[16,48,1024]{2,1,0:T(8,128)(2,1)S(1)}) fusion(bf16[16,48,1024]{2,1,0:T(8,128)(2,1)} %collective-permute-done, bf16[16,48,1024]{2,1,0:T(8,128)(2,1)} %all_to_all.25, pred[]{:T(512)S(6)} %eq.28), kind=kLoop, calls=%fused_computation.26 | loop fusion | flops 1572864 | bytes 6291457 | tf_op jit(solution)/shard_map/jit(_where)/select_n | solution.py:89
  37.3 1.3 fusion.14
  38.8 2.2 %convolution_convert_fusion.2 = bf16[512,896]{1,0:T(8,128)(2,1)} fusion(bf16[512,1024]{1,0:T(8,128)(2,1)S(1)} %fusion.14, bf16[896,1024]{1,0:T(8,128)(2,1)S(1)} %copy-done.7), kind=kOutput, calls=%fused_computation.31 | convolution fusion | flops 939982848 | bytes 3801088 | tf_op jit(solution)/shard_map/dot_general | solution.py:104
  41.0 6.6 %all-to-all-start.2 = ((bf16[8,64,896]{2,1,0:T(8,128)(2,1)}), bf16[8,64,896]{2,1,0:T(8,128)(2,1)}, u32[]{:S(2)}, u32[]{:S(2)}) async-start(bf16[8,64,896]{2,1,0:T(8,128)(2,1)} %bitcast.8), calls=%async_computation.2 | async-start | bytes 1835008 | tf_op jit(solution)/shard_map/all_to_all | solution.py:44
  47.6 1.4 pad_maximum_fusion.2
  49.5 1.3 fusion.18
  52.2 1.3 fusion.15
  53.5 1.6 pad_maximum_fusion
  55.1 7.1 %all-to-all-done.2 = bf16[8,64,896]{2,1,0:T(8,128)(2,1)} async-done(((bf16[8,64,896]{2,1,0:T(8,128)(2,1)}), bf16[8,64,896]{2,1,0:T(8,128)(2,1)}, u32[]{:S(2)}, u32[]{:S(2)}) %all-to-all-start.2) | async-done | bytes 917536 | tf_op jit(solution)/shard_map/all_to_all | solution.py:44
  62.2 4.4 %all-to-all-start.1 = ((bf16[8,64,2304]{2,1,0:T(8,128)(2,1)}), bf16[8,64,2304]{2,1,0:T(8,128)(2,1)}, u32[]{:S(2)}, u32[]{:S(2)}) async-start(bf16[8,64,2304]{2,1,0:T(8,128)(2,1)} %pad_maximum_fusion), calls=%async_computation.1 | async-start | bytes 4718592 | tf_op jit(solution)/shard_map/all_to_all | solution.py:44
  66.6 1.3 convert_reduce_fusion.1
  67.9 32.9 %all-to-all-done.1 = bf16[8,64,2304]{2,1,0:T(8,128)(2,1)} async-done(((bf16[8,64,2304]{2,1,0:T(8,128)(2,1)}), bf16[8,64,2304]{2,1,0:T(8,128)(2,1)}, u32[]{:S(2)}, u32[]{:S(2)}) %all-to-all-start.1) | async-done | bytes 2359328 | tf_op jit(solution)/shard_map/all_to_all | solution.py:44
  100.8 2.1 %convert_reduce_fusion = f32[64,2304]{1,0:T(8,128)S(1)} fusion(bf16[8,64,2304]{2,1,0:T(8,128)(2,1)} %all-to-all-done.1), kind=kLoop, calls=%fused_computation | loop fusion | flops 2211840 | bytes 2949120 | tf_op jit(solution)/shard_map/reduce_sum | solution.py:45
  103.5 41.3 %all_to_all.26 = bf16[8,64,3200]{2,1,0:T(8,128)(2,1)S(1)} all-to-all(bf16[8,64,3200]{2,1,0:T(8,128)(2,1)S(1)} %broadcast_in_dim.2), channel_id=1, replica_groups=mesh['dp'=8,'fsdp'=16] {'dp'}, dimensions={0} | all-to-all | bytes 6553600 | tf_op jit(solution)/shard_map/all_to_all | solution.py:50
  144.7 1.3 convolution_convert_fusion.1
  146.0 1.4 copy-done.10
  147.4 1.3 fusion.31
  148.9 1.3 add_convert_fusion
  150.2 2.5 %convolution_convert_fusion = bf16[1024,2048]{1,0:T(8,128)(2,1)S(1)} fusion(bf16[512,1024]{1,0:T(8,128)(2,1)S(1)} %add_convert_fusion, bf16[512,1024]{1,0:T(8,128)(2,1)S(1)} %convolution_convert_fusion.1, s32[512]{0:T(512)S(1)} %sub.30), kind=kOutput, calls=%fused_computation.4 | convolution fusion | flops 2154299392 | bytes 6293504 | tf_op jit(solution)/shard_map/dot_general | solution.py:57
  152.9 3.3 %collective-permute-start.1 = (bf16[16,32,2048]{2,1,0:T(8,128)(2,1)S(1)}, bf16[16,32,2048]{2,1,0:T(8,128)(2,1)S(1)}, u32[]{:S(2)}, u32[]{:S(2)}) collective-permute-start(bf16[16,32,2048]{2,1,0:T(8,128)(2,1)S(1)} %fusion.1), channel_id=1, source_target_pairs={{0,1},{1,0},{2,3},{3,2},{4,5},{5,4},{6,7},{7,6},{8,9},{9,8},{10,11... | collective-permute-start | bytes 6291464 | tf_op jit(solution)/shard_map/ppermute | solution.py:62
  156.2 3.8 %collective-permute-done.1 = bf16[16,32,2048]{2,1,0:T(8,128)(2,1)S(1)} collective-permute-done((bf16[16,32,2048]{2,1,0:T(8,128)(2,1)S(1)}, bf16[16,32,2048]{2,1,0:T(8,128)(2,1)S(1)}, u32[]{:S(2)}, u32[]{:S(2)}) %collective-permute-start.1) | collective-permute-done | bytes 2097184 | tf_op jit(solution)/shard_map/ppermute | solution.py:62
  160.0 2.6 %fusion = bf16[16,32,2048]{2,1,0:T(8,128)(2,1)} fusion(bf16[16,32,2048]{2,1,0:T(8,128)(2,1)S(1)} %collective-permute-done.1, pred[]{:T(512)S(6)} %eq.28, bf16[16,2,32,2048]{3,2,1,0:T(8,128)(2,1)S(1)} %bitcast.74), kind=kLoop, calls=%fused_computation.2 | loop fusion | flops 5242880 | bytes 8388609 | tf_op jit(solution)/shard_map/convert_element_type | solution.py:63
  162.6 6.1 %all-to-all-start.4 = ((bf16[16,32,2048]{2,1,0:T(8,128)(2,1)}), bf16[16,32,2048]{2,1,0:T(8,128)(2,1)}, u32[]{:S(2)}, u32[]{:S(2)}) async-start(bf16[16,32,2048]{2,1,0:T(8,128)(2,1)} %fusion), calls=%async_computation.4 | async-start | bytes 4194304 | tf_op jit(solution)/shard_map/all_to_all | solution.py:64
  168.8 1.9 fusion.6
  171.1 3.0 %fusion.33 = f32[896,1024]{1,0:T(8,128)} fusion(bf16[512,1024]{1,0:T(8,128)(2,1)S(1)} %copy-done.4, bf16[512,3200]{1,0:T(8,128)(2,1)S(1)} %bitcast.79), kind=kOutput, calls=%fused_computation.43 | convolution fusion | flops 939524096 | bytes 5636096 | tf_op jit(solution)/shard_map/dot_general | solution.py:114
  174.1 3.1 %fusion.26 = f32[1024,896]{1,0:T(8,128)} fusion(bf16[512,1024]{1,0:T(8,128)(2,1)S(1)} %fusion.6, bf16[512,3200]{1,0:T(8,128)(2,1)S(1)} %bitcast.80), kind=kOutput, calls=%fused_computation.36 | convolution fusion | flops 939524096 | bytes 5636096 | tf_op jit(solution)/shard_map/dot_general | solution.py:126
  177.2 3.1 %fusion.29 = f32[1024,896]{1,0:T(8,128)} fusion(bf16[512,1024]{1,0:T(8,128)(2,1)S(1)} %fusion.6, bf16[512,3200]{1,0:T(8,128)(2,1)S(1)} %bitcast.81), kind=kOutput, calls=%fused_computation.39 | convolution fusion | flops 939524096 | bytes 5636096 | tf_op jit(solution)/shard_map/dot_general | solution.py:125
  180.4 16.6 %all-to-all-done.4 = bf16[16,32,2048]{2,1,0:T(8,128)(2,1)} async-done(((bf16[16,32,2048]{2,1,0:T(8,128)(2,1)}), bf16[16,32,2048]{2,1,0:T(8,128)(2,1)}, u32[]{:S(2)}, u32[]{:S(2)}) %all-to-all-start.4) | async-done | bytes 2097184 | tf_op jit(solution)/shard_map/all_to_all | solution.py:64
  196.9 2.0 reduce
  (53 shorter events, 8.0 us)
Async XLA Ops:
  0.6 50.1 %copy-start = (f32[1024,512]{1,0:T(8,128)S(1)}, f32[1024,512]{1,0:T(8,128)}, u32[]{:S(2)}) copy-start(f32[1024,512]{1,0:T(8,128)} %param.14) | copy-start | bytes 6291460
  2.5 27.0 %copy-start.5 = (s32[16,4]{0,1:T(4,128)S(1)}, s32[16,4]{0,1:T(4,128)}, u32[]{:S(2)}) copy-start(s32[16,4]{0,1:T(4,128)} %param.9) | copy-start | bytes 772
  2.5 27.0 %copy-start.6 = (s32[16,4]{0,1:T(4,128)S(1)}, s32[16,4]{0,1:T(4,128)}, u32[]{:S(2)}) copy-start(s32[16,4]{0,1:T(4,128)} %param.10) | copy-start | bytes 772
  29.4 3.8 %collective-permute-start = (bf16[16,48,1024]{2,1,0:T(8,128)(2,1)}, bf16[16,48,1024]{2,1,0:T(8,128)(2,1)}, u32[]{:S(2)}, u32[]{:S(2)}) collective-permute-start(bf16[16,48,1024]{2,1,0:T(8,128)(2,1)} %all_to_all.25), channel_id=1, source_target_pairs={{0,1},{1,0},{2,3},{3,2},{4,5},{5,4},{6,7},{7,6},{8,9},{9,8},{10,11... | collective-permute-start | bytes 4718600 | tf_op jit(solution)/shard_map/ppermute | solution.py:87
  37.3 1.5 copy-start.7
  38.8 2.2 %copy-start.3 = (bf16[512,1024]{1,0:T(8,128)(2,1)}, bf16[512,1024]{1,0:T(8,128)(2,1)S(1)}, u32[]{:S(2)}) copy-start(bf16[512,1024]{1,0:T(8,128)(2,1)S(1)} %fusion.14) | copy-start | bytes 3145732
  41.0 21.2 %all-to-all-start.2 = ((bf16[8,64,896]{2,1,0:T(8,128)(2,1)}), bf16[8,64,896]{2,1,0:T(8,128)(2,1)}, u32[]{:S(2)}, u32[]{:S(2)}) async-start(bf16[8,64,896]{2,1,0:T(8,128)(2,1)} %bitcast.8), calls=%async_computation.2 | async-start | bytes 1835008 | tf_op jit(solution)/shard_map/all_to_all | solution.py:44
  47.6 1.8 copy-start.11
  50.7 1.5 copy-start.9
  62.2 38.6 %all-to-all-start.1 = ((bf16[8,64,2304]{2,1,0:T(8,128)(2,1)}), bf16[8,64,2304]{2,1,0:T(8,128)(2,1)}, u32[]{:S(2)}, u32[]{:S(2)}) async-start(bf16[8,64,2304]{2,1,0:T(8,128)(2,1)} %pad_maximum_fusion), calls=%async_computation.1 | async-start | bytes 4718592 | tf_op jit(solution)/shard_map/all_to_all | solution.py:44
  103.5 41.3 %copy-start.8 = (bf16[896,1024]{1,0:T(8,128)(2,1)S(1)}, bf16[896,1024]{1,0:T(8,128)(2,1)}, u32[]{:S(2)}) copy-start(bf16[896,1024]{1,0:T(8,128)(2,1)} %param.13) | copy-start | bytes 5505028
  144.7 4.0 %copy-start.1 = (bf16[8,64,3200]{2,1,0:T(8,128)(2,1)}, bf16[8,64,3200]{2,1,0:T(8,128)(2,1)S(1)}, u32[]{:S(2)}) copy-start(bf16[8,64,3200]{2,1,0:T(8,128)(2,1)S(1)} %all_to_all.26) | copy-start | bytes 9830404
  144.7 2.7 %copy-start.10 = (bf16[1024,896]{1,0:T(8,128)(2,1)S(1)}, bf16[1024,896]{1,0:T(8,128)(2,1)}, u32[]{:S(2)}) copy-start(bf16[1024,896]{1,0:T(8,128)(2,1)} %param.11) | copy-start | bytes 5505028
  147.4 1.5 copy-start.12
  152.9 7.1 %collective-permute-start.1 = (bf16[16,32,2048]{2,1,0:T(8,128)(2,1)S(1)}, bf16[16,32,2048]{2,1,0:T(8,128)(2,1)S(1)}, u32[]{:S(2)}, u32[]{:S(2)}) collective-permute-start(bf16[16,32,2048]{2,1,0:T(8,128)(2,1)S(1)} %fusion.1), channel_id=1, source_target_pairs={{0,1},{1,0},{2,3},{3,2},{4,5},{5,4},{6,7},{7,6},{8,9},{9,8},{10,11... | collective-permute-start | bytes 6291464 | tf_op jit(solution)/shard_map/ppermute | solution.py:62
  162.6 34.3 %all-to-all-start.4 = ((bf16[16,32,2048]{2,1,0:T(8,128)(2,1)}), bf16[16,32,2048]{2,1,0:T(8,128)(2,1)}, u32[]{:S(2)}, u32[]{:S(2)}) async-start(bf16[16,32,2048]{2,1,0:T(8,128)(2,1)} %fusion), calls=%async_computation.4 | async-start | bytes 4194304 | tf_op jit(solution)/shard_map/all_to_all | solution.py:64
  168.8 2.1 %copy-start.2 = (bf16[8,64,3200]{2,1,0:T(8,128)(2,1)S(1)}, bf16[8,64,3200]{2,1,0:T(8,128)(2,1)}, u32[]{:S(2)}) copy-start(bf16[8,64,3200]{2,1,0:T(8,128)(2,1)} %copy-done.1) | copy-start | bytes 9830404
  168.8 2.4 %copy-start.4 = (bf16[512,1024]{1,0:T(8,128)(2,1)S(1)}, bf16[512,1024]{1,0:T(8,128)(2,1)}, u32[]{:S(2)}) copy-start(bf16[512,1024]{1,0:T(8,128)(2,1)} %copy-done.3) | copy-start | bytes 3145732

commit v9 on v8

--- a/solution.py
+++ b/solution.py
@@ -93,7 +93,9 @@
     dyall = jnp.dot(pick, dy_dealt, preferred_element_type=jnp.float32).astype(jnp.bfloat16)
     first = jnp.dot(xall, w_gate, preferred_element_type=jnp.float32)
     second = jnp.dot(xall, w_up, preferred_element_type=jnp.float32)
-    keys_local = jnp.dot(xall, basis, preferred_element_type=jnp.float32)
+    key_half = basis.shape[1] // 2
+    basis_half = lax.dynamic_slice_in_dim(basis, (lax.axis_index("fsdp") % 2) * key_half, key_half, 1)
+    keys_local = jnp.dot(xall, basis_half, preferred_element_type=jnp.float32)
     both = reduce_rows(jnp.concatenate([first, second, keys_local], axis=1), "dp", n_dp)
     gate = both[:, :hidden_width]
     up = both[:, hidden_width:2 * hidden_width]
@@ -109,7 +111,13 @@
     hall = gathered[:, :hidden_width]
     gate_all = gathered[:, hidden_width:2 * hidden_width]
     up_all = gathered[:, 2 * hidden_width:3 * hidden_width]
-    keys_all = gathered[:, 3 * hidden_width:]
+    keys_mine = gathered[:, 3 * hidden_width:]
+    keys_other = lax.ppermute(keys_mine, "fsdp", [(f, f ^ 1) for f in range(n_fsdp)])
+    keys_all = jnp.where(
+        odd,
+        jnp.concatenate([keys_other, keys_mine], axis=1),
+        jnp.concatenate([keys_mine, keys_other], axis=1),
+    )
     out_part = jnp.dot(hall, w_down, preferred_element_type=jnp.float32)
     grad_down = lax.dot_general(hall, dyall, contract_rows, preferred_element_type=jnp.float32)
     total = lax.dot_general(gate_all, w_gate, contract_cols, preferred_element_type=jnp.float32)

time: 200 us -> 193 us (0.965)
  waiting for transfers between devices: 63.4 us -> 59.8 us
  blocking collectives: 67.9 us -> 65.2 us
    all_to_all x1, blocking collectives: 41.3 us -> 38.5 us  [gather_rows(): lax.all_to_all(jnp.broadcast_to(block[None], (n, rows, cols)), axis, 0, 0...]
    all_to_all x1, waiting for transfers between devices: 16.6 us -> 14.4 us  [reduce_dealt(): came = lax.all_to_all(pair, 'fsdp', 0, 0, tiled=True)]
  transfers between devices with their start and end apart: 5 -> 6, of which waited for: 5 -> 5; matrix products, arithmetic and copies ran while one was open for 10% -> 10% of each run, Pallas kernels for 0% -> 0%
where the time goes in v9:
time: 193 us; the launch traced here: 192 us
  blocking collectives  65.2 us (34%)
  waiting for transfers between devices  59.8 us (31%)
  matrix products  24 us (12%)
  starting transfers between devices  21 us (11%)
  other arithmetic  12.8 us (7%)
  local copies, waits for them, and re-layouts  8.36 us (4%)
    all_to_all x1, blocking collectives, gather_rows(): lax.all_to_all(jnp.broadcast_to(block[None], (n, rows, cols)), axis, 0, 0...  38.5 us
    all_to_all x2, waiting for transfers between devices, reduce_rows(): lax.all_to_all(part.astype(jnp.bfloat16).reshape(n, rows // n, cols), axi...  38.5 us
    all_to_all x1, blocking collectives, per_device(): lax.all_to_all(jnp.tile(halves, (n_fsdp // 2, 1, 1)), 'fsdp', 0, 0, tiled...  26.6 us
    all_to_all x1, waiting for transfers between devices, reduce_dealt(): came = lax.all_to_all(pair, 'fsdp', 0, 0, tiled=True)  14.4 us
    all_to_all x2, starting transfers between devices, reduce_rows(): lax.all_to_all(part.astype(jnp.bfloat16).reshape(n, rows // n, cols), axi...  10.9 us
    all_to_all x1, starting transfers between devices, reduce_dealt(): came = lax.all_to_all(pair, 'fsdp', 0, 0, tiled=True)  6.27 us
    dot_general x1, matrix products, per_device(): lax.dot_general(hall, dyall, contract_rows, preferred_element_type=jnp.fl...  4.16 us
  transfers between devices with their start and end apart: 6, of which 5 were waited for; matrix products, arithmetic and copies ran while one was open for 10% of the time, Pallas kernels for 0%

profile of v9, /device:TPU:33, one launch (start us, length us, event | category | flops | bytes accessed | tf_op | source)
XLA Modules:
  0.0 192.1 jit_solution(9495909389891030809)
XLA Ops:
  0.6 0.9 fusion.44
  2.7 26.6 %all_to_all.25 = bf16[16,48,1024]{2,1,0:T(8,128)(2,1)} all-to-all(bf16[16,48,1024]{2,1,0:T(8,128)(2,1)S(1)} %bitcast.70), channel_id=1, replica_groups=mesh['dp'=8,'fsdp'=16] {'fsdp'}, dimensions={0} | all-to-all | bytes 3145728 | tf_op jit(solution)/shard_map/all_to_all | solution.py:86
  30.1 3.1 %collective-permute-done = bf16[16,48,1024]{2,1,0:T(8,128)(2,1)} collective-permute-done((bf16[16,48,1024]{2,1,0:T(8,128)(2,1)}, bf16[16,48,1024]{2,1,0:T(8,128)(2,1)}, u32[]{:S(2)}, u32[]{:S(2)}) %collective-permute-start) | collective-permute-done | bytes 1572896 | tf_op jit(solution)/shard_map/ppermute | solution.py:87
  33.1 2.1 %broadcast_select_fusion.1 = (bf16[16,48,1024]{2,1,0:T(8,128)(2,1)S(1)}, bf16[16,48,1024]{2,1,0:T(8,128)(2,1)S(1)}) fusion(bf16[16,48,1024]{2,1,0:T(8,128)(2,1)} %collective-permute-done, bf16[16,48,1024]{2,1,0:T(8,128)(2,1)} %all_to_all.25, pred[]{:T(512)S(6)} %eq.30), kind=kLoop, calls=%fused_computation.24 | loop fusion | flops 1572864 | bytes 6291457 | tf_op jit(solution)/shard_map/jit(_where)/select_n | solution.py:89
  36.5 1.3 fusion.12
  38.0 2.2 %convolution_convert_fusion.2 = bf16[512,896]{1,0:T(8,128)(2,1)} fusion(bf16[512,1024]{1,0:T(8,128)(2,1)S(1)} %fusion.12, bf16[896,1024]{1,0:T(8,128)(2,1)S(1)} %copy-done.9), kind=kOutput, calls=%fused_computation.29 | convolution fusion | flops 939982848 | bytes 3801088 | tf_op jit(solution)/shard_map/dot_general | solution.py:106
  40.3 6.6 %all-to-all-start.2 = ((bf16[8,64,896]{2,1,0:T(8,128)(2,1)}), bf16[8,64,896]{2,1,0:T(8,128)(2,1)S(1)}, u32[]{:S(2)}, u32[]{:S(2)}) async-start(bf16[8,64,896]{2,1,0:T(8,128)(2,1)} %bitcast.77), calls=%async_computation.2 | async-start | bytes 1835008 | tf_op jit(solution)/shard_map/all_to_all | solution.py:44
  46.9 1.3 pad_maximum_fusion.2
  48.5 1.2 fusion.16
  50.3 1.2 fusion.13
  51.5 1.6 pad_maximum_fusion
  53.1 8.2 %all-to-all-done.2 = bf16[8,64,896]{2,1,0:T(8,128)(2,1)S(1)} async-done(((bf16[8,64,896]{2,1,0:T(8,128)(2,1)}), bf16[8,64,896]{2,1,0:T(8,128)(2,1)S(1)}, u32[]{:S(2)}, u32[]{:S(2)}) %all-to-all-start.2) | async-done | bytes 917536 | tf_op jit(solution)/shard_map/all_to_all | solution.py:44
  61.3 4.3 %all-to-all-start.1 = ((bf16[8,64,2048]{2,1,0:T(8,128)(2,1)}), bf16[8,64,2048]{2,1,0:T(8,128)(2,1)}, u32[]{:S(2)}, u32[]{:S(2)}) async-start(bf16[8,64,2048]{2,1,0:T(8,128)(2,1)} %pad_maximum_fusion), calls=%async_computation.1 | async-start | bytes 4194304 | tf_op jit(solution)/shard_map/all_to_all | solution.py:44
  65.8 30.3 %all-to-all-done.1 = bf16[8,64,2048]{2,1,0:T(8,128)(2,1)} async-done(((bf16[8,64,2048]{2,1,0:T(8,128)(2,1)}), bf16[8,64,2048]{2,1,0:T(8,128)(2,1)}, u32[]{:S(2)}, u32[]{:S(2)}) %all-to-all-start.1) | async-done | bytes 2097184 | tf_op jit(solution)/shard_map/all_to_all | solution.py:44
  96.1 2.0 %convert_reduce_fusion = f32[64,2048]{1,0:T(8,128)S(1)} fusion(bf16[8,64,2048]{2,1,0:T(8,128)(2,1)} %all-to-all-done.1), kind=kLoop, calls=%fused_computation.2 | loop fusion | flops 1966080 | bytes 2621440 | tf_op jit(solution)/shard_map/reduce_sum | solution.py:45
  98.8 38.5 %all_to_all.26 = bf16[8,64,2944]{2,1,0:T(8,128)(2,1)S(1)} all-to-all(bf16[8,64,2944]{2,1,0:T(8,128)(2,1)S(1)} %broadcast_in_dim.2), channel_id=1, replica_groups=mesh['dp'=8,'fsdp'=16] {'dp'}, dimensions={0} | all-to-all | bytes 6029312 | tf_op jit(solution)/shard_map/all_to_all | solution.py:50
  137.3 1.3 convolution_convert_fusion.1
  138.6 1.3 copy-done.12
  139.9 1.3 fusion.28
  141.4 1.3 add_convert_fusion
  142.7 2.5 %convolution_convert_fusion = bf16[1024,2048]{1,0:T(8,128)(2,1)S(1)} fusion(bf16[512,1024]{1,0:T(8,128)(2,1)S(1)} %add_convert_fusion, bf16[512,1024]{1,0:T(8,128)(2,1)S(1)} %convolution_convert_fusion.1, s32[512]{0:T(512)S(1)} %sub.30), kind=kOutput, calls=%fused_computation.4 | convolution fusion | flops 2154299392 | bytes 6293504 | tf_op jit(solution)/shard_map/dot_general | solution.py:57
  145.4 3.2 %collective-permute-start.1 = (bf16[16,32,2048]{2,1,0:T(8,128)(2,1)S(1)}, bf16[16,32,2048]{2,1,0:T(8,128)(2,1)S(1)}, u32[]{:S(2)}, u32[]{:S(2)}) collective-permute-start(bf16[16,32,2048]{2,1,0:T(8,128)(2,1)S(1)} %fusion.1), channel_id=1, source_target_pairs={{0,1},{1,0},{2,3},{3,2},{4,5},{5,4},{6,7},{7,6},{8,9},{9,8},{10,11... | collective-permute-start | bytes 6291464 | tf_op jit(solution)/shard_map/ppermute | solution.py:62
  148.6 3.8 %collective-permute-done.1 = bf16[16,32,2048]{2,1,0:T(8,128)(2,1)S(1)} collective-permute-done((bf16[16,32,2048]{2,1,0:T(8,128)(2,1)S(1)}, bf16[16,32,2048]{2,1,0:T(8,128)(2,1)S(1)}, u32[]{:S(2)}, u32[]{:S(2)}) %collective-permute-start.1) | collective-permute-done | bytes 2097184 | tf_op jit(solution)/shard_map/ppermute | solution.py:62
  152.4 2.6 %fusion = bf16[16,32,2048]{2,1,0:T(8,128)(2,1)} fusion(bf16[16,32,2048]{2,1,0:T(8,128)(2,1)S(1)} %collective-permute-done.1, pred[]{:T(512)S(6)} %eq.30, bf16[16,2,32,2048]{3,2,1,0:T(8,128)(2,1)S(1)} %bitcast.62), kind=kLoop, calls=%fused_computation.1 | loop fusion | flops 5242880 | bytes 8388609 | tf_op jit(solution)/shard_map/convert_element_type | solution.py:63
  155.0 6.3 %all-to-all-start.4 = ((bf16[16,32,2048]{2,1,0:T(8,128)(2,1)}), bf16[16,32,2048]{2,1,0:T(8,128)(2,1)}, u32[]{:S(2)}, u32[]{:S(2)}) async-start(bf16[16,32,2048]{2,1,0:T(8,128)(2,1)} %fusion), calls=%async_computation.4 | async-start | bytes 4194304 | tf_op jit(solution)/shard_map/all_to_all | solution.py:64
  161.3 1.0 slice.93
  162.7 4.2 %fusion.30 = f32[896,1024]{1,0:T(8,128)} fusion(bf16[512,1024]{1,0:T(8,128)(2,1)S(1)} %copy-done.6, bf16[512,2944]{1,0:T(8,128)(2,1)} %bitcast.67), kind=kOutput, calls=%fused_computation.43 | convolution fusion | flops 939524096 | bytes 5636096 | tf_op jit(solution)/shard_map/dot_general | solution.py:122
  167.7 1.1 copy-done.2
  168.8 3.1 %fusion.23 = f32[1024,896]{1,0:T(8,128)} fusion(bf16[512,1024]{1,0:T(8,128)(2,1)S(1)} %fusion.6, bf16[512,2944]{1,0:T(8,128)(2,1)S(1)} %bitcast.68), kind=kOutput, calls=%fused_computation.36 | convolution fusion | flops 939524096 | bytes 5636096 | tf_op jit(solution)/shard_map/dot_general | solution.py:134
  171.9 3.1 %fusion.26 = f32[1024,896]{1,0:T(8,128)} fusion(bf16[512,1024]{1,0:T(8,128)(2,1)S(1)} %fusion.6, bf16[512,2944]{1,0:T(8,128)(2,1)S(1)} %bitcast.69), kind=kOutput, calls=%fused_computation.39 | convolution fusion | flops 939524096 | bytes 5636096 | tf_op jit(solution)/shard_map/dot_general | solution.py:133
  175.0 14.4 %all-to-all-done.4 = bf16[16,32,2048]{2,1,0:T(8,128)(2,1)} async-done(((bf16[16,32,2048]{2,1,0:T(8,128)(2,1)}), bf16[16,32,2048]{2,1,0:T(8,128)(2,1)}, u32[]{:S(2)}, u32[]{:S(2)}) %all-to-all-start.4) | async-done | bytes 2097184 | tf_op jit(solution)/shard_map/all_to_all | solution.py:64
  189.4 2.0 %reduce = bf16[2,32,2048]{2,1,0:T(8,128)(2,1)S(1)} reduce(bf16[8,2,32,2048]{3,2,1,0:T(8,128)(2,1)} %bitcast.16, bf16[]{:T(256)} %constant.45), dimensions={0}, to_apply=%region_9.10.clone | reduce | flops 917504 | bytes 2359298 | tf_op jit(solution)/shard_map/reduce_sum | solution.py:65
  (60 shorter events, 7.2 us)
Async XLA Ops:
  0.6 49.1 %copy-start = (f32[1024,512]{1,0:T(8,128)S(1)}, f32[1024,512]{1,0:T(8,128)}, u32[]{:S(2)}) copy-start(f32[1024,512]{1,0:T(8,128)} %param.14) | copy-start | bytes 6291460
  2.5 27.0 %copy-start.7 = (s32[16,4]{0,1:T(4,128)S(1)}, s32[16,4]{0,1:T(4,128)}, u32[]{:S(2)}) copy-start(s32[16,4]{0,1:T(4,128)} %param.9) | copy-start | bytes 772
  2.5 27.0 %copy-start.8 = (s32[16,4]{0,1:T(4,128)S(1)}, s32[16,4]{0,1:T(4,128)}, u32[]{:S(2)}) copy-start(s32[16,4]{0,1:T(4,128)} %param.10) | copy-start | bytes 772
  29.4 3.8 %collective-permute-start = (bf16[16,48,1024]{2,1,0:T(8,128)(2,1)}, bf16[16,48,1024]{2,1,0:T(8,128)(2,1)}, u32[]{:S(2)}, u32[]{:S(2)}) collective-permute-start(bf16[16,48,1024]{2,1,0:T(8,128)(2,1)} %all_to_all.25), channel_id=1, source_target_pairs={{0,1},{1,0},{2,3},{3,2},{4,5},{5,4},{6,7},{7,6},{8,9},{9,8},{10,11... | collective-permute-start | bytes 4718600 | tf_op jit(solution)/shard_map/ppermute | solution.py:87
  36.5 1.5 copy-start.9
  38.0 2.2 %copy-start.5 = (bf16[512,1024]{1,0:T(8,128)(2,1)}, bf16[512,1024]{1,0:T(8,128)(2,1)S(1)}, u32[]{:S(2)}) copy-start(bf16[512,1024]{1,0:T(8,128)(2,1)S(1)} %fusion.12) | copy-start | bytes 3145732
  40.3 21.1 %all-to-all-start.2 = ((bf16[8,64,896]{2,1,0:T(8,128)(2,1)}), bf16[8,64,896]{2,1,0:T(8,128)(2,1)S(1)}, u32[]{:S(2)}, u32[]{:S(2)}) async-start(bf16[8,64,896]{2,1,0:T(8,128)(2,1)} %bitcast.77), calls=%async_computation.2 | async-start | bytes 1835008 | tf_op jit(solution)/shard_map/all_to_all | solution.py:44
  46.9 1.7 copy-start.13
  48.1 2.1 %copy-start.3 = (bf16[16,32,1024]{2,1,0:T(8,128)(2,1)}, bf16[16,32,1024]{2,1,0:T(8,128)(2,1)S(1)}, u32[]{:S(2)}) copy-start(bf16[16,32,1024]{2,1,0:T(8,128)(2,1)S(1)} %pad_maximum_fusion.2) | copy-start | bytes 3145732
  48.5 1.7 copy-start.11
  61.3 34.8 %all-to-all-start.1 = ((bf16[8,64,2048]{2,1,0:T(8,128)(2,1)}), bf16[8,64,2048]{2,1,0:T(8,128)(2,1)}, u32[]{:S(2)}, u32[]{:S(2)}) async-start(bf16[8,64,2048]{2,1,0:T(8,128)(2,1)} %pad_maximum_fusion), calls=%async_computation.1 | async-start | bytes 4194304 | tf_op jit(solution)/shard_map/all_to_all | solution.py:44
  98.7 38.5 %copy-start.10 = (bf16[896,1024]{1,0:T(8,128)(2,1)S(1)}, bf16[896,1024]{1,0:T(8,128)(2,1)}, u32[]{:S(2)}) copy-start(bf16[896,1024]{1,0:T(8,128)(2,1)} %param.13) | copy-start | bytes 5505028
  137.3 3.9 %copy-start.1 = (bf16[8,64,2944]{2,1,0:T(8,128)(2,1)}, bf16[8,64,2944]{2,1,0:T(8,128)(2,1)S(1)}, u32[]{:S(2)}) copy-start(bf16[8,64,2944]{2,1,0:T(8,128)(2,1)S(1)} %all_to_all.26) | copy-start | bytes 9043972
  137.3 2.6 %copy-start.12 = (bf16[1024,896]{1,0:T(8,128)(2,1)S(1)}, bf16[1024,896]{1,0:T(8,128)(2,1)}, u32[]{:S(2)}) copy-start(bf16[1024,896]{1,0:T(8,128)(2,1)} %param.11) | copy-start | bytes 5505028
  139.9 1.5 copy-start.14
  145.4 7.0 %collective-permute-start.1 = (bf16[16,32,2048]{2,1,0:T(8,128)(2,1)S(1)}, bf16[16,32,2048]{2,1,0:T(8,128)(2,1)S(1)}, u32[]{:S(2)}, u32[]{:S(2)}) collective-permute-start(bf16[16,32,2048]{2,1,0:T(8,128)(2,1)S(1)} %fusion.1), channel_id=1, source_target_pairs={{0,1},{1,0},{2,3},{3,2},{4,5},{5,4},{6,7},{7,6},{8,9},{9,8},{10,11... | collective-permute-start | bytes 6291464 | tf_op jit(solution)/shard_map/ppermute | solution.py:62
  155.0 7.7 %copy-start.6 = (bf16[512,1024]{1,0:T(8,128)(2,1)S(1)}, bf16[512,1024]{1,0:T(8,128)(2,1)}, u32[]{:S(2)}) copy-start(bf16[512,1024]{1,0:T(8,128)(2,1)} %copy-done.5) | copy-start | bytes 3145732
  155.0 34.4 %all-to-all-start.4 = ((bf16[16,32,2048]{2,1,0:T(8,128)(2,1)}), bf16[16,32,2048]{2,1,0:T(8,128)(2,1)}, u32[]{:S(2)}, u32[]{:S(2)}) async-start(bf16[16,32,2048]{2,1,0:T(8,128)(2,1)} %fusion), calls=%async_computation.4 | async-start | bytes 4194304 | tf_op jit(solution)/shard_map/all_to_all | solution.py:64
  162.2 4.7 %copy-start.4 = (bf16[16,32,1024]{2,1,0:T(8,128)(2,1)S(1)}, bf16[16,32,1024]{2,1,0:T(8,128)(2,1)}, u32[]{:S(2)}) copy-start(bf16[16,32,1024]{2,1,0:T(8,128)(2,1)} %copy-done.3) | copy-start | bytes 3145732
  162.3 4.6 %collective-permute-start.2 = (bf16[512,256]{1,0:T(8,128)(2,1)S(1)}, bf16[512,256]{1,0:T(8,128)(2,1)S(1)}, u32[]{:S(2)}, u32[]{:S(2)}) collective-permute-start(bf16[512,256]{1,0:T(8,128)(2,1)S(1)} %slice.93), channel_id=1, source_target_pairs={{0,1},{1,0},{2,3},{3,2},{4,5},{5,4},{6,7},{7,6},{8,9},{9,8},{10,11... | collective-permute-start | bytes 786440 | tf_op jit(solution)/shard_map/ppermute | solution.py:115
  166.9 1.9 copy-start.2

commit v10 on v9

--- a/solution.py
+++ b/solution.py
@@ -96,15 +96,15 @@
     key_half = basis.shape[1] // 2
     basis_half = lax.dynamic_slice_in_dim(basis, (lax.axis_index("fsdp") % 2) * key_half, key_half, 1)
     keys_local = jnp.dot(xall, basis_half, preferred_element_type=jnp.float32)
-    both = reduce_rows(jnp.concatenate([first, second, keys_local], axis=1), "dp", n_dp)
+    hg_part = lax.dot_general(dyall, w_down, contract_cols, preferred_element_type=jnp.float32)
+    both = reduce_rows(jnp.concatenate([first, second, keys_local, hg_part], axis=1), "dp", n_dp)
     gate = both[:, :hidden_width]
     up = both[:, hidden_width:2 * hidden_width]
-    keys = both[:, 2 * hidden_width:].astype(jnp.bfloat16)
+    keys = both[:, 2 * hidden_width:2 * hidden_width + key_half].astype(jnp.bfloat16)
+    hidden_grad = both[:, 2 * hidden_width + key_half:]
     sig = jax.nn.sigmoid(gate)
     hidden = (gate * sig * up).astype(jnp.bfloat16)
 
-    hg_part = lax.dot_general(dyall, w_down, contract_cols, preferred_element_type=jnp.float32)
-    hidden_grad = reduce_rows(hg_part, "dp", n_dp)
     gate_grad = (hidden_grad * up * sig * (1.0 + gate * (1.0 - sig))).astype(jnp.bfloat16)
     up_grad = (hidden_grad * gate * sig).astype(jnp.bfloat16)
     gathered = gather_rows(jnp.concatenate([hidden, gate_grad, up_grad, keys], axis=1), "dp", n_dp)

time: 193 us -> 181 us (0.938)
  blocking collectives: 65.2 us -> 109 us
  waiting for transfers between devices: 59.8 us -> 21 us
  starting transfers between devices: 21 us -> 9.57 us
  other arithmetic: 12.8 us -> 8.59 us
    all_to_all x0 -> x1, blocking collectives: none -> 43.8 us  [reduce_rows(): lax.all_to_all(part.astype(jnp.bfloat16).reshape(n, rows // n, cols), axi...]
    all_to_all x2 -> x0, waiting for transfers between devices: 38.5 us -> none  [reduce_rows(): lax.all_to_all(part.astype(jnp.bfloat16).reshape(n, rows // n, cols), axi...]
    all_to_all x2 -> x0, starting transfers between devices: 10.9 us -> none  [reduce_rows(): lax.all_to_all(part.astype(jnp.bfloat16).reshape(n, rows // n, cols), axi...]
  transfers between devices with their start and end apart: 6 -> 4, of which waited for: 5 -> 3; matrix products, arithmetic and copies ran while one was open for 10% -> 7% of each run, Pallas kernels for 0% -> 0%
where the time goes in v10:
time: 181 us; the launch traced here: 180 us
  blocking collectives  109 us (60%)
  matrix products  23.5 us (13%)
  waiting for transfers between devices  21 us (12%)
  starting transfers between devices  9.57 us (5%)
  other arithmetic  8.59 us (5%)
  local copies, waits for them, and re-layouts  7.04 us (4%)
    all_to_all x1, blocking collectives, reduce_rows(): lax.all_to_all(part.astype(jnp.bfloat16).reshape(n, rows // n, cols), axi...  43.8 us
    all_to_all x1, blocking collectives, gather_rows(): lax.all_to_all(jnp.broadcast_to(block[None], (n, rows, cols)), axis, 0, 0...  38.9 us
    all_to_all x1, blocking collectives, per_device(): lax.all_to_all(jnp.tile(halves, (n_fsdp // 2, 1, 1)), 'fsdp', 0, 0, tiled...  26.6 us
    all_to_all x1, waiting for transfers between devices, reduce_dealt(): came = lax.all_to_all(pair, 'fsdp', 0, 0, tiled=True)  14.1 us
    all_to_all x1, starting transfers between devices, reduce_dealt(): came = lax.all_to_all(pair, 'fsdp', 0, 0, tiled=True)  5.99 us
    dot_general x1, matrix products, per_device(): lax.dot_general(hall, dyall, contract_rows, preferred_element_type=jnp.fl...  4.49 us
    ppermute x1, waiting for transfers between devices, reduce_dealt(): got = lax.ppermute(give, 'fsdp', [(f, f ^ 1) for f in range(blocks)])  3.79 us
  transfers between devices with their start and end apart: 4, of which 3 were waited for; matrix products, arithmetic and copies ran while one was open for 7% of the time, Pallas kernels for 0%

profile of v10, /device:TPU:33, one launch (start us, length us, event | category | flops | bytes accessed | tf_op | source)
XLA Modules:
  0.0 180.0 jit_solution(17554359876574666313)
XLA Ops:
  0.6 0.9 fusion.44
  1.6 0.9 fusion.43
  2.7 26.6 %all_to_all.20 = bf16[16,48,1024]{2,1,0:T(8,128)(2,1)} all-to-all(bf16[16,48,1024]{2,1,0:T(8,128)(2,1)S(1)} %bitcast.70), channel_id=1, replica_groups=mesh['dp'=8,'fsdp'=16] {'fsdp'}, dimensions={0} | all-to-all | bytes 3145728 | tf_op jit(solution)/shard_map/all_to_all | solution.py:86
  30.1 3.1 %collective-permute-done = bf16[16,48,1024]{2,1,0:T(8,128)(2,1)} collective-permute-done((bf16[16,48,1024]{2,1,0:T(8,128)(2,1)}, bf16[16,48,1024]{2,1,0:T(8,128)(2,1)}, u32[]{:S(2)}, u32[]{:S(2)}) %collective-permute-start) | collective-permute-done | bytes 1572896 | tf_op jit(solution)/shard_map/ppermute | solution.py:87
  33.1 2.1 %broadcast_select_fusion.1 = (bf16[16,48,1024]{2,1,0:T(8,128)(2,1)S(1)}, bf16[16,48,1024]{2,1,0:T(8,128)(2,1)S(1)}) fusion(bf16[16,48,1024]{2,1,0:T(8,128)(2,1)} %collective-permute-done, bf16[16,48,1024]{2,1,0:T(8,128)(2,1)} %all_to_all.20, pred[]{:T(512)S(6)} %eq.30), kind=kLoop, calls=%fused_computation.23 | loop fusion | flops 1572864 | bytes 6291457 | tf_op jit(solution)/shard_map/jit(_where)/select_n | solution.py:89
  35.6 1.3 copy-done.8
  36.9 1.3 fusion.16
  38.4 1.3 fusion.13
  39.9 1.3 fusion.12
  41.3 0.5 convolution_convert_fusion.3
  41.8 1.3 convolution_convert_fusion.2
  43.4 43.8 %all_to_all.21 = bf16[8,64,2944]{2,1,0:T(8,128)(2,1)S(1)} all-to-all(bf16[8,64,2944]{2,1,0:T(8,128)(2,1)S(1)} %pad_maximum_fusion), channel_id=1, replica_groups=mesh['dp'=8,'fsdp'=16] {'dp'}, dimensions={0} | all-to-all | bytes 6029312 | tf_op jit(solution)/shard_map/all_to_all | solution.py:44
  87.2 0.4 convert_reduce_fusion
  88.2 38.9 %all_to_all.22 = bf16[8,64,2944]{2,1,0:T(8,128)(2,1)S(1)} all-to-all(bf16[8,64,2944]{2,1,0:T(8,128)(2,1)S(1)} %broadcast_in_dim.2), channel_id=1, replica_groups=mesh['dp'=8,'fsdp'=16] {'dp'}, dimensions={0} | all-to-all | bytes 6029312 | tf_op jit(solution)/shard_map/all_to_all | solution.py:50
  127.1 1.3 convolution_convert_fusion.1
  128.4 1.3 fusion.28
  129.7 1.3 add_convert_fusion
  131.0 2.5 %convolution_convert_fusion = bf16[1024,2048]{1,0:T(8,128)(2,1)S(1)} fusion(bf16[512,1024]{1,0:T(8,128)(2,1)S(1)} %add_convert_fusion, bf16[512,1024]{1,0:T(8,128)(2,1)S(1)} %convolution_convert_fusion.1, s32[512]{0:T(512)S(1)} %sub.30), kind=kOutput, calls=%fused_computation.4 | convolution fusion | flops 2154299392 | bytes 6293504 | tf_op jit(solution)/shard_map/dot_general | solution.py:57
  133.8 3.0 %collective-permute-start.1 = (bf16[16,32,2048]{2,1,0:T(8,128)(2,1)S(1)}, bf16[16,32,2048]{2,1,0:T(8,128)(2,1)S(1)}, u32[]{:S(2)}, u32[]{:S(2)}) collective-permute-start(bf16[16,32,2048]{2,1,0:T(8,128)(2,1)S(1)} %fusion.1), channel_id=1, source_target_pairs={{0,1},{1,0},{2,3},{3,2},{4,5},{5,4},{6,7},{7,6},{8,9},{9,8},{10,11... | collective-permute-start | bytes 6291464 | tf_op jit(solution)/shard_map/ppermute | solution.py:62
  136.8 3.8 %collective-permute-done.1 = bf16[16,32,2048]{2,1,0:T(8,128)(2,1)S(1)} collective-permute-done((bf16[16,32,2048]{2,1,0:T(8,128)(2,1)S(1)}, bf16[16,32,2048]{2,1,0:T(8,128)(2,1)S(1)}, u32[]{:S(2)}, u32[]{:S(2)}) %collective-permute-start.1) | collective-permute-done | bytes 2097184 | tf_op jit(solution)/shard_map/ppermute | solution.py:62
  140.5 2.6 %fusion = bf16[16,32,2048]{2,1,0:T(8,128)(2,1)} fusion(bf16[16,32,2048]{2,1,0:T(8,128)(2,1)S(1)} %collective-permute-done.1, pred[]{:T(512)S(6)} %eq.30, bf16[16,2,32,2048]{3,2,1,0:T(8,128)(2,1)S(1)} %bitcast.62), kind=kLoop, calls=%fused_computation.2 | loop fusion | flops 5242880 | bytes 8388609 | tf_op jit(solution)/shard_map/convert_element_type | solution.py:63
  143.2 6.0 %all-to-all-start.3 = ((bf16[16,32,2048]{2,1,0:T(8,128)(2,1)}), bf16[16,32,2048]{2,1,0:T(8,128)(2,1)}, u32[]{:S(2)}, u32[]{:S(2)}) async-start(bf16[16,32,2048]{2,1,0:T(8,128)(2,1)} %fusion), calls=%async_computation.3 | async-start | bytes 4194304 | tf_op jit(solution)/shard_map/all_to_all | solution.py:64
  149.2 1.0 slice.98
  150.1 0.5 collective-permute-start.2
  150.6 4.5 %fusion.30 = f32[896,1024]{1,0:T(8,128)} fusion(bf16[512,1024]{1,0:T(8,128)(2,1)} %copy-done.3, bf16[512,2944]{1,0:T(8,128)(2,1)} %bitcast.67), kind=kOutput, calls=%fused_computation.42 | convolution fusion | flops 939524096 | bytes 5636096 | tf_op jit(solution)/shard_map/dot_general | solution.py:122
  155.1 0.8 fusion.6
  155.9 1.1 copy-done.2
  156.9 3.1 %fusion.23 = f32[1024,896]{1,0:T(8,128)} fusion(bf16[512,1024]{1,0:T(8,128)(2,1)S(1)} %fusion.6, bf16[512,2944]{1,0:T(8,128)(2,1)S(1)} %bitcast.68), kind=kOutput, calls=%fused_computation.35 | convolution fusion | flops 939524096 | bytes 5636096 | tf_op jit(solution)/shard_map/dot_general | solution.py:134
  160.1 3.1 %fusion.26 = f32[1024,896]{1,0:T(8,128)} fusion(bf16[512,1024]{1,0:T(8,128)(2,1)S(1)} %fusion.6, bf16[512,2944]{1,0:T(8,128)(2,1)S(1)} %bitcast.69), kind=kOutput, calls=%fused_computation.38 | convolution fusion | flops 939524096 | bytes 5636096 | tf_op jit(solution)/shard_map/dot_general | solution.py:133
  163.2 14.1 %all-to-all-done.3 = bf16[16,32,2048]{2,1,0:T(8,128)(2,1)} async-done(((bf16[16,32,2048]{2,1,0:T(8,128)(2,1)}), bf16[16,32,2048]{2,1,0:T(8,128)(2,1)}, u32[]{:S(2)}, u32[]{:S(2)}) %all-to-all-start.3) | async-done | bytes 2097184 | tf_op jit(solution)/shard_map/all_to_all | solution.py:64
  177.3 2.0 %reduce = bf16[2,32,2048]{2,1,0:T(8,128)(2,1)S(1)} reduce(bf16[8,2,32,2048]{3,2,1,0:T(8,128)(2,1)} %bitcast.16, bf16[]{:T(256)} %constant.45), dimensions={0}, to_apply=%region_8.9.clone | reduce | flops 917504 | bytes 2359298 | tf_op jit(solution)/shard_map/reduce_sum | solution.py:65
  179.3 0.7 fusion.42
  (44 shorter events, 2.8 us)
Async XLA Ops:
  0.6 40.6 %copy-start = (f32[1024,512]{1,0:T(8,128)S(1)}, f32[1024,512]{1,0:T(8,128)}, u32[]{:S(2)}) copy-start(f32[1024,512]{1,0:T(8,128)} %param.14) | copy-start | bytes 6291460
  2.5 27.0 %copy-start.4 = (s32[16,4]{0,1:T(4,128)S(1)}, s32[16,4]{0,1:T(4,128)}, u32[]{:S(2)}) copy-start(s32[16,4]{0,1:T(4,128)} %param.9) | copy-start | bytes 772
  2.5 27.0 %copy-start.5 = (s32[16,4]{0,1:T(4,128)S(1)}, s32[16,4]{0,1:T(4,128)}, u32[]{:S(2)}) copy-start(s32[16,4]{0,1:T(4,128)} %param.10) | copy-start | bytes 772
  29.4 3.8 %collective-permute-start = (bf16[16,48,1024]{2,1,0:T(8,128)(2,1)}, bf16[16,48,1024]{2,1,0:T(8,128)(2,1)}, u32[]{:S(2)}, u32[]{:S(2)}) collective-permute-start(bf16[16,48,1024]{2,1,0:T(8,128)(2,1)} %all_to_all.20), channel_id=1, source_target_pairs={{0,1},{1,0},{2,3},{3,2},{4,5},{5,4},{6,7},{7,6},{8,9},{9,8},{10,11... | collective-permute-start | bytes 4718600 | tf_op jit(solution)/shard_map/ppermute | solution.py:87
  35.4 1.5 copy-start.8
  36.9 1.5 copy-start.7
  39.9 1.8 %copy-start.6 = (bf16[896,1024]{1,0:T(8,128)(2,1)S(1)}, bf16[896,1024]{1,0:T(8,128)(2,1)}, u32[]{:S(2)}) copy-start(bf16[896,1024]{1,0:T(8,128)(2,1)} %param.13) | copy-start | bytes 5505028
  41.3 1.8 %copy-start.3 = (bf16[512,1024]{1,0:T(8,128)(2,1)}, bf16[512,1024]{1,0:T(8,128)(2,1)S(1)}, u32[]{:S(2)}) copy-start(bf16[512,1024]{1,0:T(8,128)(2,1)S(1)} %fusion.12) | copy-start | bytes 3145732
  127.1 2.6 %copy-start.1 = (bf16[8,64,2944]{2,1,0:T(8,128)(2,1)}, bf16[8,64,2944]{2,1,0:T(8,128)(2,1)S(1)}, u32[]{:S(2)}) copy-start(bf16[8,64,2944]{2,1,0:T(8,128)(2,1)S(1)} %all_to_all.22) | copy-start | bytes 9043972
  133.8 6.8 %collective-permute-start.1 = (bf16[16,32,2048]{2,1,0:T(8,128)(2,1)S(1)}, bf16[16,32,2048]{2,1,0:T(8,128)(2,1)S(1)}, u32[]{:S(2)}, u32[]{:S(2)}) collective-permute-start(bf16[16,32,2048]{2,1,0:T(8,128)(2,1)S(1)} %fusion.1), channel_id=1, source_target_pairs={{0,1},{1,0},{2,3},{3,2},{4,5},{5,4},{6,7},{7,6},{8,9},{9,8},{10,11... | collective-permute-start | bytes 6291464 | tf_op jit(solution)/shard_map/ppermute | solution.py:62
  143.2 34.1 %all-to-all-start.3 = ((bf16[16,32,2048]{2,1,0:T(8,128)(2,1)}), bf16[16,32,2048]{2,1,0:T(8,128)(2,1)}, u32[]{:S(2)}, u32[]{:S(2)}) async-start(bf16[16,32,2048]{2,1,0:T(8,128)(2,1)} %fusion), calls=%async_computation.3 | async-start | bytes 4194304 | tf_op jit(solution)/shard_map/all_to_all | solution.py:64
  150.1 5.0 %collective-permute-start.2 = (bf16[512,256]{1,0:T(8,128)(2,1)S(1)}, bf16[512,256]{1,0:T(8,128)(2,1)S(1)}, u32[]{:S(2)}, u32[]{:S(2)}) collective-permute-start(bf16[512,256]{1,0:T(8,128)(2,1)S(1)} %slice.98), channel_id=1, source_target_pairs={{0,1},{1,0},{2,3},{3,2},{4,5},{5,4},{6,7},{7,6},{8,9},{9,8},{10,11... | collective-permute-start | bytes 786440 | tf_op jit(solution)/shard_map/ppermute | solution.py:115
  155.1 1.9 %copy-start.2 = (bf16[8,64,2944]{2,1,0:T(8,128)(2,1)S(1)}, bf16[8,64,2944]{2,1,0:T(8,128)(2,1)}, u32[]{:S(2)}) copy-start(bf16[8,64,2944]{2,1,0:T(8,128)(2,1)} %copy-done.1) | copy-start | bytes 9043972

commit v11 on v9

--- a/solution.py
+++ b/solution.py
@@ -43,6 +43,18 @@
     rows, cols = part.shape
     got = lax.all_to_all(part.astype(jnp.bfloat16).reshape(n, rows // n, cols), axis, 0, 0, tiled=True)
     return jnp.sum(got.astype(jnp.float32), axis=0)
+
+
+def reduce_rows_permuted(part, axis, n):
+    rows, cols = part.shape
+    blocks = part.astype(jnp.bfloat16).reshape(n, rows // n, cols)
+    me = lax.axis_index(axis)
+    total = lax.dynamic_index_in_dim(blocks, me, 0, keepdims=False).astype(jnp.float32)
+    for k in range(1, n):
+        chunk = lax.dynamic_index_in_dim(blocks, (me + k) % n, 0, keepdims=False)
+        moved = lax.ppermute(chunk, axis, [(i, (i + k) % n) for i in range(n)])
+        total = total + moved.astype(jnp.float32)
+    return total
 
 
 def gather_rows(block, axis, n):
@@ -96,6 +108,8 @@
     key_half = basis.shape[1] // 2
     basis_half = lax.dynamic_slice_in_dim(basis, (lax.axis_index("fsdp") % 2) * key_half, key_half, 1)
     keys_local = jnp.dot(xall, basis_half, preferred_element_type=jnp.float32)
+    hg_part = lax.dot_general(dyall, w_down, contract_cols, preferred_element_type=jnp.float32)
+    hidden_grad = reduce_rows_permuted(hg_part, "dp", n_dp)
     both = reduce_rows(jnp.concatenate([first, second, keys_local], axis=1), "dp", n_dp)
     gate = both[:, :hidden_width]
     up = both[:, hidden_width:2 * hidden_width]
@@ -103,8 +117,6 @@
     sig = jax.nn.sigmoid(gate)
     hidden = (gate * sig * up).astype(jnp.bfloat16)
 
-    hg_part = lax.dot_general(dyall, w_down, contract_cols, preferred_element_type=jnp.float32)
-    hidden_grad = reduce_rows(hg_part, "dp", n_dp)
     gate_grad = (hidden_grad * up * sig * (1.0 + gate * (1.0 - sig))).astype(jnp.bfloat16)
     up_grad = (hidden_grad * gate * sig).astype(jnp.bfloat16)
     gathered = gather_rows(jnp.concatenate([hidden, gate_grad, up_grad, keys], axis=1), "dp", n_dp)

time: 193 us -> 190 us (0.984)
  waiting for transfers between devices: 59.8 us -> 41.5 us
  starting transfers between devices: 21 us -> 27.9 us
  local copies, waits for them, and re-layouts: 8.36 us -> 13.2 us
  blocking collectives: 65.2 us -> 69.7 us
    all_to_all x2 -> x1, waiting for transfers between devices: 38.5 us -> 0.01 us  [reduce_rows(): lax.all_to_all(part.astype(jnp.bfloat16).reshape(n, rows // n, cols), axi...]
    ppermute x0 -> x7, waiting for transfers between devices: none -> 20.1 us  [reduce_rows_permuted(): moved = lax.ppermute(chunk, axis, [(i, (i + k) % n) for i in range(n)])]
    ppermute x0 -> x7, starting transfers between devices: none -> 12 us  [reduce_rows_permuted(): moved = lax.ppermute(chunk, axis, [(i, (i + k) % n) for i in range(n)])]
    all_to_all x1, blocking collectives: 38.5 us -> 42.9 us  [gather_rows(): lax.all_to_all(jnp.broadcast_to(block[None], (n, rows, cols)), axis, 0, 0...]
    all_to_all x2 -> x1, starting transfers between devices: 10.9 us -> 6.6 us  [reduce_rows(): lax.all_to_all(part.astype(jnp.bfloat16).reshape(n, rows // n, cols), axi...]
    unnamed x30 -> x32, local copies, waits for them, and re-layouts: 3.16 us -> 6.67 us
  transfers between devices with their start and end apart: 6 -> 12, of which waited for: 5 -> 5; matrix products, arithmetic and copies ran while one was open for 10% -> 11% of each run, Pallas kernels for 0% -> 0%
where the time goes in v11:
time: 190 us
  blocking collectives  69.7 us (37%)
  waiting for transfers between devices  41.5 us (22%)
  starting transfers between devices  27.9 us (15%)
  matrix products  23.4 us (12%)
  local copies, waits for them, and re-layouts  13.2 us (7%)
  other arithmetic  12.9 us (7%)
    all_to_all x1, blocking collectives, gather_rows(): lax.all_to_all(jnp.broadcast_to(block[None], (n, rows, cols)), axis, 0, 0...  42.9 us
    all_to_all x1, blocking collectives, per_device(): lax.all_to_all(jnp.tile(halves, (n_fsdp // 2, 1, 1)), 'fsdp', 0, 0, tiled...  26.8 us
    ppermute x7, waiting for transfers between devices, reduce_rows_permuted(): moved = lax.ppermute(chunk, axis, [(i, (i + k) % n) for i in range(n)])  20.1 us
    all_to_all x1, waiting for transfers between devices, reduce_dealt(): came = lax.all_to_all(pair, 'fsdp', 0, 0, tiled=True)  14.1 us
    ppermute x7, starting transfers between devices, reduce_rows_permuted(): moved = lax.ppermute(chunk, axis, [(i, (i + k) % n) for i in range(n)])  12 us
    unnamed x32, local copies, waits for them, and re-layouts  6.67 us
    all_to_all x1, starting transfers between devices, reduce_rows(): lax.all_to_all(part.astype(jnp.bfloat16).reshape(n, rows // n, cols), axi...  6.6 us
    all_to_all x1, starting transfers between devices, reduce_dealt(): came = lax.all_to_all(pair, 'fsdp', 0, 0, tiled=True)  5.62 us
  transfers between devices with their start and end apart: 12, of which 5 were waited for; matrix products, arithmetic and copies ran while one was open for 11% of the time, Pallas kernels for 0%

profile of v11, /device:TPU:33, one launch (start us, length us, event | category | flops | bytes accessed | tf_op | source)
XLA Modules:
  0.0 189.7 jit_solution(8926605370690974327)
XLA Ops:
  2.7 26.8 %all_to_all.20 = bf16[16,48,1024]{2,1,0:T(8,128)(2,1)} all-to-all(bf16[16,48,1024]{2,1,0:T(8,128)(2,1)S(1)} %bitcast.88), channel_id=1, replica_groups=mesh['dp'=8,'fsdp'=16] {'fsdp'}, dimensions={0} | all-to-all | bytes 3145728 | tf_op jit(solution)/shard_map/all_to_all | solution.py:98
  29.8 3.5 %collective-permute-done = bf16[16,48,1024]{2,1,0:T(8,128)(2,1)} collective-permute-done((bf16[16,48,1024]{2,1,0:T(8,128)(2,1)}, bf16[16,48,1024]{2,1,0:T(8,128)(2,1)}, u32[]{:S(2)}, u32[]{:S(2)}) %collective-permute-start) | collective-permute-done | bytes 1572896 | tf_op jit(solution)/shard_map/ppermute | solution.py:99
  33.3 2.1 %broadcast_select_fusion.1 = (bf16[16,48,1024]{2,1,0:T(8,128)(2,1)S(1)}, bf16[16,48,1024]{2,1,0:T(8,128)(2,1)S(1)}) fusion(bf16[16,48,1024]{2,1,0:T(8,128)(2,1)} %collective-permute-done, bf16[16,48,1024]{2,1,0:T(8,128)(2,1)} %all_to_all.20, pred[]{:T(512)S(6)} %eq.67), kind=kLoop, calls=%fused_computation.23 | loop fusion | flops 1572864 | bytes 6291457 | tf_op jit(solution)/shard_map/jit(_where)/select_n | solution.py:101
  41.3 1.6 pad_maximum_fusion
  42.9 6.6 %all-to-all-start.1 = ((bf16[8,64,2048]{2,1,0:T(8,128)(2,1)}), bf16[8,64,2048]{2,1,0:T(8,128)(2,1)}, u32[]{:S(2)}, u32[]{:S(2)}) async-start(bf16[8,64,2048]{2,1,0:T(8,128)(2,1)} %pad_maximum_fusion), calls=%async_computation.1 | async-start | bytes 4194304 | tf_op jit(solution)/shard_map/all_to_all | solution.py:44
  49.9 1.4 slice.83
  51.9 1.3 fusion.12
  53.4 1.3 convolution_convert_fusion.2
  56.5 3.0 %collective-permute-start.1 = (bf16[64,896]{1,0:T(8,128)(2,1)}, bf16[64,896]{1,0:T(8,128)(2,1)S(1)}, u32[]{:S(2)}, u32[]{:S(2)}) collective-permute-start(bf16[64,896]{1,0:T(8,128)(2,1)} %get-tuple-element.11), channel_id=1, source_target_pairs={{0,16},{16,32},{32,48},{48,64},{64,80},{80,96},{96,112},{112,0},{1... | collective-permute-start | bytes 344072 | tf_op jit(solution)/shard_map/ppermute | solution.py:55
  59.4 2.1 %collective-permute-start.7 = (bf16[64,896]{1,0:T(8,128)(2,1)}, bf16[64,896]{1,0:T(8,128)(2,1)}, u32[]{:S(2)}, u32[]{:S(2)}) collective-permute-start(bf16[64,896]{1,0:T(8,128)(2,1)} %get-tuple-element.12), channel_id=1, source_target_pairs={{0,112},{16,0},{32,16},{48,32},{64,48},{80,64},{96,80},{112,96},{1... | collective-permute-start | bytes 344072 | tf_op jit(solution)/shard_map/ppermute | solution.py:55
  61.6 1.5 collective-permute-start.6
  63.0 2.1 %collective-permute-start.5 = (bf16[64,896]{1,0:T(8,128)(2,1)}, bf16[64,896]{1,0:T(8,128)(2,1)}, u32[]{:S(2)}, u32[]{:S(2)}) collective-permute-start(bf16[64,896]{1,0:T(8,128)(2,1)} %get-tuple-element.14), channel_id=1, source_target_pairs={{0,80},{16,96},{32,112},{48,0},{64,16},{80,32},{96,48},{112,64},{1... | collective-permute-start | bytes 344072 | tf_op jit(solution)/shard_map/ppermute | solution.py:55
  65.1 2.4 %collective-permute-start.4 = (bf16[64,896]{1,0:T(8,128)(2,1)}, bf16[64,896]{1,0:T(8,128)(2,1)}, u32[]{:S(2)}, u32[]{:S(2)}) collective-permute-start(bf16[64,896]{1,0:T(8,128)(2,1)} %get-tuple-element.15), channel_id=1, source_target_pairs={{0,64},{16,80},{32,96},{48,112},{64,0},{80,16},{96,32},{112,48},{1... | collective-permute-start | bytes 344072 | tf_op jit(solution)/shard_map/ppermute | solution.py:55
  67.5 15.4 %collective-permute-done.1 = bf16[64,896]{1,0:T(8,128)(2,1)S(1)} collective-permute-done((bf16[64,896]{1,0:T(8,128)(2,1)}, bf16[64,896]{1,0:T(8,128)(2,1)S(1)}, u32[]{:S(2)}, u32[]{:S(2)}) %collective-permute-start.1) | collective-permute-done | bytes 114720 | tf_op jit(solution)/shard_map/ppermute | solution.py:55
  83.9 2.0 %convert_reduce_fusion = f32[64,2048]{1,0:T(8,128)S(1)} fusion(bf16[8,64,2048]{2,1,0:T(8,128)(2,1)} %all-to-all-done.1), kind=kLoop, calls=%fused_computation.2 | loop fusion | flops 1966080 | bytes 2621440 | tf_op jit(solution)/shard_map/reduce_sum | solution.py:45
  86.0 4.6 %collective-permute-done.3 = bf16[64,896]{1,0:T(8,128)(2,1)} collective-permute-done((bf16[64,896]{1,0:T(8,128)(2,1)S(1)}, bf16[64,896]{1,0:T(8,128)(2,1)}, u32[]{:S(2)}, u32[]{:S(2)}) %collective-permute-start.3) | collective-permute-done | bytes 114720 | tf_op jit(solution)/shard_map/ppermute | solution.py:55
  90.6 1.4 multiply_convert_fusion.1
  92.6 42.9 %all_to_all.21 = bf16[8,64,2944]{2,1,0:T(8,128)(2,1)S(1)} all-to-all(bf16[8,64,2944]{2,1,0:T(8,128)(2,1)S(1)} %broadcast_in_dim.2), channel_id=1, replica_groups=mesh['dp'=8,'fsdp'=16] {'dp'}, dimensions={0} | all-to-all | bytes 6029312 | tf_op jit(solution)/shard_map/all_to_all | solution.py:62
  135.5 1.3 convolution_convert_fusion.1
  136.8 1.3 copy-done.13
  138.1 1.3 fusion.28
  139.6 1.3 add_convert_fusion
  140.9 2.5 %convolution_convert_fusion = bf16[1024,2048]{1,0:T(8,128)(2,1)S(1)} fusion(bf16[512,1024]{1,0:T(8,128)(2,1)S(1)} %add_convert_fusion, bf16[512,1024]{1,0:T(8,128)(2,1)S(1)} %convolution_convert_fusion.1, s32[512]{0:T(512)S(1)} %sub.30), kind=kOutput, calls=%fused_computation.4 | convolution fusion | flops 2154299392 | bytes 6293504 | tf_op jit(solution)/shard_map/dot_general | solution.py:69
  143.6 3.1 %collective-permute-start.8 = (bf16[16,32,2048]{2,1,0:T(8,128)(2,1)S(1)}, bf16[16,32,2048]{2,1,0:T(8,128)(2,1)S(1)}, u32[]{:S(2)}, u32[]{:S(2)}) collective-permute-start(bf16[16,32,2048]{2,1,0:T(8,128)(2,1)S(1)} %fusion.1), channel_id=1, source_target_pairs={{0,1},{1,0},{2,3},{3,2},{4,5},{5,4},{6,7},{7,6},{8,9},{9,8},{10,11... | collective-permute-start | bytes 6291464 | tf_op jit(solution)/shard_map/ppermute | solution.py:74
  146.7 3.8 %collective-permute-done.8 = bf16[16,32,2048]{2,1,0:T(8,128)(2,1)S(1)} collective-permute-done((bf16[16,32,2048]{2,1,0:T(8,128)(2,1)S(1)}, bf16[16,32,2048]{2,1,0:T(8,128)(2,1)S(1)}, u32[]{:S(2)}, u32[]{:S(2)}) %collective-permute-start.8) | collective-permute-done | bytes 2097184 | tf_op jit(solution)/shard_map/ppermute | solution.py:74
  150.5 2.7 %fusion = bf16[16,32,2048]{2,1,0:T(8,128)(2,1)} fusion(bf16[16,32,2048]{2,1,0:T(8,128)(2,1)S(1)} %collective-permute-done.8, pred[]{:T(512)S(6)} %eq.67, bf16[16,2,32,2048]{3,2,1,0:T(8,128)(2,1)S(1)} %bitcast.80), kind=kLoop, calls=%fused_computation.1 | loop fusion | flops 5242880 | bytes 8388609 | tf_op jit(solution)/shard_map/convert_element_type | solution.py:75
  153.2 5.6 %all-to-all-start.3 = ((bf16[16,32,2048]{2,1,0:T(8,128)(2,1)}), bf16[16,32,2048]{2,1,0:T(8,128)(2,1)}, u32[]{:S(2)}, u32[]{:S(2)}) async-start(bf16[16,32,2048]{2,1,0:T(8,128)(2,1)} %fusion), calls=%async_computation.3 | async-start | bytes 4194304 | tf_op jit(solution)/shard_map/all_to_all | solution.py:76
  160.2 4.5 %fusion.30 = f32[896,1024]{1,0:T(8,128)} fusion(bf16[512,1024]{1,0:T(8,128)(2,1)} %copy-done.6, bf16[512,2944]{1,0:T(8,128)(2,1)} %bitcast.85), kind=kOutput, calls=%fused_computation.42 | convolution fusion | flops 939524096 | bytes 5636096 | tf_op jit(solution)/shard_map/dot_general | solution.py:134
  166.6 3.1 %fusion.23 = f32[1024,896]{1,0:T(8,128)} fusion(bf16[512,1024]{1,0:T(8,128)(2,1)S(1)} %fusion.6, bf16[512,2944]{1,0:T(8,128)(2,1)S(1)} %bitcast.86), kind=kOutput, calls=%fused_computation.35 | convolution fusion | flops 939524096 | bytes 5636096 | tf_op jit(solution)/shard_map/dot_general | solution.py:146
  169.7 3.1 %fusion.26 = f32[1024,896]{1,0:T(8,128)} fusion(bf16[512,1024]{1,0:T(8,128)(2,1)S(1)} %fusion.6, bf16[512,2944]{1,0:T(8,128)(2,1)S(1)} %bitcast.87), kind=kOutput, calls=%fused_computation.38 | convolution fusion | flops 939524096 | bytes 5636096 | tf_op jit(solution)/shard_map/dot_general | solution.py:145
  172.8 14.1 %all-to-all-done.3 = bf16[16,32,2048]{2,1,0:T(8,128)(2,1)} async-done(((bf16[16,32,2048]{2,1,0:T(8,128)(2,1)}), bf16[16,32,2048]{2,1,0:T(8,128)(2,1)}, u32[]{:S(2)}, u32[]{:S(2)}) %all-to-all-start.3) | async-done | bytes 2097184 | tf_op jit(solution)/shard_map/all_to_all | solution.py:76
  187.0 2.0 %reduce = bf16[2,32,2048]{2,1,0:T(8,128)(2,1)S(1)} reduce(bf16[8,2,32,2048]{3,2,1,0:T(8,128)(2,1)} %bitcast.24, bf16[]{:T(256)} %constant.110), dimensions={0}, to_apply=%region_8.9.clone | reduce | flops 917504 | bytes 2359298 | tf_op jit(solution)/shard_map/reduce_sum | solution.py:77
  (75 shorter events, 16.9 us)
Async XLA Ops:
  0.6 40.1 %copy-start = (f32[1024,512]{1,0:T(8,128)S(1)}, f32[1024,512]{1,0:T(8,128)}, u32[]{:S(2)}) copy-start(f32[1024,512]{1,0:T(8,128)} %param.14) | copy-start | bytes 6291460
  2.7 26.9 %copy-start.8 = (s32[16,4]{0,1:T(4,128)S(1)}, s32[16,4]{0,1:T(4,128)}, u32[]{:S(2)}) copy-start(s32[16,4]{0,1:T(4,128)} %param.9) | copy-start | bytes 772
  2.7 27.0 %copy-start.9 = (s32[16,4]{0,1:T(4,128)S(1)}, s32[16,4]{0,1:T(4,128)}, u32[]{:S(2)}) copy-start(s32[16,4]{0,1:T(4,128)} %param.10) | copy-start | bytes 772
  29.5 3.8 %collective-permute-start = (bf16[16,48,1024]{2,1,0:T(8,128)(2,1)}, bf16[16,48,1024]{2,1,0:T(8,128)(2,1)}, u32[]{:S(2)}, u32[]{:S(2)}) collective-permute-start(bf16[16,48,1024]{2,1,0:T(8,128)(2,1)} %all_to_all.20), channel_id=1, source_target_pairs={{0,1},{1,0},{2,3},{3,2},{4,5},{5,4},{6,7},{7,6},{8,9},{9,8},{10,11... | collective-permute-start | bytes 4718600 | tf_op jit(solution)/shard_map/ppermute | solution.py:99
  35.4 1.1 copy-start.3
  35.4 1.7 copy-start.5
  35.4 2.6 %copy-start.14 = (bf16[1024,896]{1,0:T(8,128)(2,1)S(1)}, bf16[1024,896]{1,0:T(8,128)(2,1)}, u32[]{:S(2)}) copy-start(bf16[1024,896]{1,0:T(8,128)(2,1)} %param.12) | copy-start | bytes 5505028
  38.0 1.5 copy-start.12
  42.9 41.0 %all-to-all-start.1 = ((bf16[8,64,2048]{2,1,0:T(8,128)(2,1)}), bf16[8,64,2048]{2,1,0:T(8,128)(2,1)}, u32[]{:S(2)}, u32[]{:S(2)}) async-start(bf16[8,64,2048]{2,1,0:T(8,128)(2,1)} %pad_maximum_fusion), calls=%async_computation.1 | async-start | bytes 4194304 | tf_op jit(solution)/shard_map/all_to_all | solution.py:44
  49.9 1.7 copy-start.4
  51.9 1.5 copy-start.10
  53.4 1.3 copy-start.6
  54.7 0.9 copy-start.7
  56.5 26.5 %collective-permute-start.1 = (bf16[64,896]{1,0:T(8,128)(2,1)}, bf16[64,896]{1,0:T(8,128)(2,1)S(1)}, u32[]{:S(2)}, u32[]{:S(2)}) collective-permute-start(bf16[64,896]{1,0:T(8,128)(2,1)} %get-tuple-element.11), channel_id=1, source_target_pairs={{0,16},{16,32},{32,48},{48,64},{64,80},{80,96},{96,112},{112,0},{1... | collective-permute-start | bytes 344072 | tf_op jit(solution)/shard_map/ppermute | solution.py:55
  59.4 23.5 %collective-permute-start.7 = (bf16[64,896]{1,0:T(8,128)(2,1)}, bf16[64,896]{1,0:T(8,128)(2,1)}, u32[]{:S(2)}, u32[]{:S(2)}) collective-permute-start(bf16[64,896]{1,0:T(8,128)(2,1)} %get-tuple-element.12), channel_id=1, source_target_pairs={{0,112},{16,0},{32,16},{48,32},{64,48},{80,64},{96,80},{112,96},{1... | collective-permute-start | bytes 344072 | tf_op jit(solution)/shard_map/ppermute | solution.py:55
  61.6 24.4 %collective-permute-start.6 = (bf16[64,896]{1,0:T(8,128)(2,1)}, bf16[64,896]{1,0:T(8,128)(2,1)}, u32[]{:S(2)}, u32[]{:S(2)}) collective-permute-start(bf16[64,896]{1,0:T(8,128)(2,1)} %get-tuple-element.13), channel_id=1, source_target_pairs={{0,96},{16,112},{32,0},{48,16},{64,32},{80,48},{96,64},{112,80},{1... | collective-permute-start | bytes 344072 | tf_op jit(solution)/shard_map/ppermute | solution.py:55
  63.0 22.9 %collective-permute-start.5 = (bf16[64,896]{1,0:T(8,128)(2,1)}, bf16[64,896]{1,0:T(8,128)(2,1)}, u32[]{:S(2)}, u32[]{:S(2)}) collective-permute-start(bf16[64,896]{1,0:T(8,128)(2,1)} %get-tuple-element.14), channel_id=1, source_target_pairs={{0,80},{16,96},{32,112},{48,0},{64,16},{80,32},{96,48},{112,64},{1... | collective-permute-start | bytes 344072 | tf_op jit(solution)/shard_map/ppermute | solution.py:55
  65.1 20.8 %collective-permute-start.4 = (bf16[64,896]{1,0:T(8,128)(2,1)}, bf16[64,896]{1,0:T(8,128)(2,1)}, u32[]{:S(2)}, u32[]{:S(2)}) collective-permute-start(bf16[64,896]{1,0:T(8,128)(2,1)} %get-tuple-element.15), channel_id=1, source_target_pairs={{0,64},{16,80},{32,96},{48,112},{64,0},{80,16},{96,32},{112,48},{1... | collective-permute-start | bytes 344072 | tf_op jit(solution)/shard_map/ppermute | solution.py:55
  82.9 7.7 %collective-permute-start.3 = (bf16[64,896]{1,0:T(8,128)(2,1)S(1)}, bf16[64,896]{1,0:T(8,128)(2,1)}, u32[]{:S(2)}, u32[]{:S(2)}) collective-permute-start(bf16[64,896]{1,0:T(8,128)(2,1)S(1)} %get-tuple-element.16), channel_id=1, source_target_pairs={{0,48},{16,64},{32,80},{48,96},{64,112},{80,0},{96,16},{112,32},{1... | collective-permute-start | bytes 344072 | tf_op jit(solution)/shard_map/ppermute | solution.py:55
  82.9 7.7 %collective-permute-start.2 = (bf16[64,896]{1,0:T(8,128)(2,1)S(1)}, bf16[64,896]{1,0:T(8,128)(2,1)}, u32[]{:S(2)}, u32[]{:S(2)}) collective-permute-start(bf16[64,896]{1,0:T(8,128)(2,1)S(1)} %get-tuple-element.17), channel_id=1, source_target_pairs={{0,32},{16,48},{32,64},{48,80},{64,96},{80,112},{96,0},{112,16},{1... | collective-permute-start | bytes 344072 | tf_op jit(solution)/shard_map/ppermute | solution.py:55
  92.6 42.9 %copy-start.11 = (bf16[896,1024]{1,0:T(8,128)(2,1)S(1)}, bf16[896,1024]{1,0:T(8,128)(2,1)}, u32[]{:S(2)}) copy-start(bf16[896,1024]{1,0:T(8,128)(2,1)} %param.13) | copy-start | bytes 5505028
  135.5 3.9 %copy-start.1 = (bf16[8,64,2944]{2,1,0:T(8,128)(2,1)}, bf16[8,64,2944]{2,1,0:T(8,128)(2,1)S(1)}, u32[]{:S(2)}) copy-start(bf16[8,64,2944]{2,1,0:T(8,128)(2,1)S(1)} %all_to_all.21) | copy-start | bytes 9043972
  135.5 2.6 %copy-start.13 = (bf16[1024,896]{1,0:T(8,128)(2,1)S(1)}, bf16[1024,896]{1,0:T(8,128)(2,1)}, u32[]{:S(2)}) copy-start(bf16[1024,896]{1,0:T(8,128)(2,1)} %param.11) | copy-start | bytes 5505028
  138.1 1.5 copy-start.15
  143.6 6.9 %collective-permute-start.8 = (bf16[16,32,2048]{2,1,0:T(8,128)(2,1)S(1)}, bf16[16,32,2048]{2,1,0:T(8,128)(2,1)S(1)}, u32[]{:S(2)}, u32[]{:S(2)}) collective-permute-start(bf16[16,32,2048]{2,1,0:T(8,128)(2,1)S(1)} %fusion.1), channel_id=1, source_target_pairs={{0,1},{1,0},{2,3},{3,2},{4,5},{5,4},{6,7},{7,6},{8,9},{9,8},{10,11... | collective-permute-start | bytes 6291464 | tf_op jit(solution)/shard_map/ppermute | solution.py:74
  153.2 33.8 %all-to-all-start.3 = ((bf16[16,32,2048]{2,1,0:T(8,128)(2,1)}), bf16[16,32,2048]{2,1,0:T(8,128)(2,1)}, u32[]{:S(2)}, u32[]{:S(2)}) async-start(bf16[16,32,2048]{2,1,0:T(8,128)(2,1)} %fusion), calls=%async_computation.3 | async-start | bytes 4194304 | tf_op jit(solution)/shard_map/all_to_all | solution.py:76
  159.8 5.0 %collective-permute-start.9 = (bf16[512,256]{1,0:T(8,128)(2,1)S(1)}, bf16[512,256]{1,0:T(8,128)(2,1)S(1)}, u32[]{:S(2)}, u32[]{:S(2)}) collective-permute-start(bf16[512,256]{1,0:T(8,128)(2,1)S(1)} %slice.93), channel_id=1, source_target_pairs={{0,1},{1,0},{2,3},{3,2},{4,5},{5,4},{6,7},{7,6},{8,9},{9,8},{10,11... | collective-permute-start | bytes 786440 | tf_op jit(solution)/shard_map/ppermute | solution.py:127
  164.7 1.9 copy-start.2

commit v12 on v10

--- a/solution.py
+++ b/solution.py
@@ -90,12 +90,22 @@
     high = jnp.where(odd, came, other)
     xall = jnp.concatenate([low[:, :half_x], high[:, :half_x]], axis=1).reshape(-1, x_src.shape[1])
     dy_dealt = jnp.concatenate([low[:, half_x:], high[:, half_x:]], axis=1).reshape(-1, x_src.shape[1])
+    x_came = came[:, :half_x].reshape(-1, x_src.shape[1])
+    x_other = other[:, :half_x].reshape(-1, x_src.shape[1])
     dyall = jnp.dot(pick, dy_dealt, preferred_element_type=jnp.float32).astype(jnp.bfloat16)
-    first = jnp.dot(xall, w_gate, preferred_element_type=jnp.float32)
-    second = jnp.dot(xall, w_up, preferred_element_type=jnp.float32)
     key_half = basis.shape[1] // 2
     basis_half = lax.dynamic_slice_in_dim(basis, (lax.axis_index("fsdp") % 2) * key_half, key_half, 1)
-    keys_local = jnp.dot(xall, basis_half, preferred_element_type=jnp.float32)
+    w_in = jnp.concatenate([w_gate, w_up, basis_half.astype(jnp.bfloat16)], axis=1)
+    p_came = jnp.dot(x_came, w_in, preferred_element_type=jnp.float32).astype(jnp.bfloat16)
+    p_other = jnp.dot(x_other, w_in, preferred_element_type=jnp.float32).astype(jnp.bfloat16)
+    p_came = p_came.reshape(n_fsdp, half_x, -1)
+    p_other = p_other.reshape(n_fsdp, half_x, -1)
+    p_low = jnp.where(odd, p_other, p_came)
+    p_high = jnp.where(odd, p_came, p_other)
+    p_all = jnp.concatenate([p_low, p_high], axis=1).reshape(n_fsdp * tok, -1)
+    first = p_all[:, :hidden_width]
+    second = p_all[:, hidden_width:2 * hidden_width]
+    keys_local = p_all[:, 2 * hidden_width:]
     hg_part = lax.dot_general(dyall, w_down, contract_cols, preferred_element_type=jnp.float32)
     both = reduce_rows(jnp.concatenate([first, second, keys_local, hg_part], axis=1), "dp", n_dp)
     gate = both[:, :hidden_width]

time: 181 us -> 184 us (1.017)
  local copies, waits for them, and re-layouts: 7.04 us -> 10.3 us
  waiting for transfers between devices: 21 us -> 19 us
    ppermute x1, waiting for transfers between devices: 3.07 us -> 0.01 us  [per_device(): other = lax.ppermute(came, 'fsdp', [(f, f ^ 1) for f in range(n_fsdp)])]
    dot_general x3 -> x2, matrix products: 2.99 us -> 5.84 us  [the longest x1 2.95 us: per_device(): jnp.dot(x_other, w_in, preferred_element_type=jnp.float32)]
    slice x0 -> x4, local copies, waits for them, and re-layouts: none -> 2.49 us  [the longest x1 1.21 us: per_device(): x_came = came[:, :half_x].reshape(-1, x_src.shape[1])]
  transfers between devices with their start and end apart: 4 -> 4, of which waited for: 3 -> 2; matrix products, arithmetic and copies ran while one was open for 7% -> 9% of each run, Pallas kernels for 0% -> 0%
where the time goes in v12:
time: 184 us; the launch traced here: 183 us
  blocking collectives  109 us (59%)
  matrix products  24.8 us (13%)
  waiting for transfers between devices  19 us (10%)
  starting transfers between devices  10.6 us (6%)
  local copies, waits for them, and re-layouts  10.3 us (6%)
  other arithmetic  8.72 us (5%)
    all_to_all x1, blocking collectives, reduce_rows(): lax.all_to_all(part.astype(jnp.bfloat16).reshape(n, rows // n, cols), axi...  43.3 us
    all_to_all x1, blocking collectives, gather_rows(): lax.all_to_all(jnp.broadcast_to(block[None], (n, rows, cols)), axis, 0, 0...  39.1 us
    all_to_all x1, blocking collectives, per_device(): lax.all_to_all(jnp.tile(halves, (n_fsdp // 2, 1, 1)), 'fsdp', 0, 0, tiled...  26.6 us
    all_to_all x1, waiting for transfers between devices, reduce_dealt(): came = lax.all_to_all(pair, 'fsdp', 0, 0, tiled=True)  15.2 us
    all_to_all x1, starting transfers between devices, reduce_dealt(): came = lax.all_to_all(pair, 'fsdp', 0, 0, tiled=True)  6.88 us
    ppermute x1, waiting for transfers between devices, reduce_dealt(): got = lax.ppermute(give, 'fsdp', [(f, f ^ 1) for f in range(blocks)])  3.79 us
  transfers between devices with their start and end apart: 4, of which 2 were waited for; matrix products, arithmetic and copies ran while one was open for 9% of the time, Pallas kernels for 0%

profile of v12, /device:TPU:33, one launch (start us, length us, event | category | flops | bytes accessed | tf_op | source)
XLA Modules:
  0.0 183.4 jit_solution(11858682201639434394)
XLA Ops:
  0.6 0.9 fusion.34
  1.6 0.9 fusion.33
  2.7 26.6 %all_to_all.20 = bf16[16,48,1024]{2,1,0:T(8,128)(2,1)} all-to-all(bf16[16,48,1024]{2,1,0:T(8,128)(2,1)S(1)} %bitcast.65), channel_id=1, replica_groups=mesh['dp'=8,'fsdp'=16] {'fsdp'}, dimensions={0} | all-to-all | bytes 3145728 | tf_op jit(solution)/shard_map/all_to_all | solution.py:86
  30.1 1.2 slice.104
  31.7 2.9 %convolution_convert_fusion.1 = bf16[256,2048]{1,0:T(8,128)(2,1)S(1)} fusion(bf16[256,1024]{1,0:T(8,128)(2,1)S(1)} %bitcast.76, bf16[1024,256]{1,0:T(8,128)(2,1)S(1)} %dynamic-slice_convert_fusion, bf16[1024,896]{1,0:T(8,128)(2,1)} %param.12, bf16[1024,896]{1,0:T(8,128)(2,1)S(1)} %copy-done.8), kind=kOutput, calls=%fused_computation.7 | convolution fusion | flops 1086849024 | bytes 5767168 | tf_op jit(solution)/shard_map/dot_general | solution.py:99
  34.6 1.1 slice.103
  35.7 3.0 %broadcast_select_fusion.3 = (bf16[256,2048]{1,0:T(8,128)(2,1)S(1)}, bf16[256,2048]{1,0:T(8,128)(2,1)S(1)}) fusion(bf16[256,2048]{1,0:T(8,128)(2,1)S(1)} %convolution_convert_fusion.1, pred[]{:T(512)S(6)} %eq.30, bf16[256,1024]{1,0:T(8,128)(2,1)S(1)} %bitcast.75, bf16[1024,256]{1,0:T(8,128)(2,1)S(1)} %dynamic-slice_convert_fusion, ...), kind=kOutput, calls=%fused_computation.32 | convolution fusion | flops 1087897600 | bytes 7864321 | tf_op jit(solution)/shard_map/dot_general | solution.py:100
  39.1 2.1 %broadcast_select_fusion.1 = (bf16[16,48,1024]{2,1,0:T(8,128)(2,1)S(1)}, bf16[16,48,1024]{2,1,0:T(8,128)(2,1)S(1)}) fusion(bf16[16,48,1024]{2,1,0:T(8,128)(2,1)} %collective-permute-done, bf16[16,48,1024]{2,1,0:T(8,128)(2,1)} %all_to_all.20, pred[]{:T(512)S(6)} %eq.30), kind=kLoop, calls=%fused_computation.23 | loop fusion | flops 1572864 | bytes 6291457 | tf_op jit(solution)/shard_map/jit(_where)/select_n | solution.py:89
  41.4 0.9 copy-done.3
  42.3 0.5 copy-done.4
  43.1 1.3 fusion.8
  44.5 1.3 convolution_convert_fusion.4
  46.1 43.3 %all_to_all.21 = bf16[8,64,2944]{2,1,0:T(8,128)(2,1)S(1)} all-to-all(bf16[8,64,2944]{2,1,0:T(8,128)(2,1)S(1)} %pad_maximum_fusion.1), channel_id=1, replica_groups=mesh['dp'=8,'fsdp'=16] {'dp'}, dimensions={0} | all-to-all | bytes 6029312 | tf_op jit(solution)/shard_map/all_to_all | solution.py:44
  90.4 39.1 %all_to_all.22 = bf16[8,64,2944]{2,1,0:T(8,128)(2,1)S(1)} all-to-all(bf16[8,64,2944]{2,1,0:T(8,128)(2,1)S(1)} %broadcast_in_dim.2), channel_id=1, replica_groups=mesh['dp'=8,'fsdp'=16] {'dp'}, dimensions={0} | all-to-all | bytes 6029312 | tf_op jit(solution)/shard_map/all_to_all | solution.py:50
  129.5 1.3 convolution_convert_fusion.3
  130.8 1.3 fusion.16
  132.1 1.3 add_convert_fusion
  133.4 2.5 %convolution_convert_fusion = bf16[1024,2048]{1,0:T(8,128)(2,1)S(1)} fusion(bf16[512,1024]{1,0:T(8,128)(2,1)S(1)} %add_convert_fusion, bf16[512,1024]{1,0:T(8,128)(2,1)S(1)} %convolution_convert_fusion.3, s32[512]{0:T(512)S(1)} %sub.30), kind=kOutput, calls=%fused_computation.5 | convolution fusion | flops 2154299392 | bytes 6293504 | tf_op jit(solution)/shard_map/dot_general | solution.py:57
  136.1 3.1 %collective-permute-start.1 = (bf16[16,32,2048]{2,1,0:T(8,128)(2,1)S(1)}, bf16[16,32,2048]{2,1,0:T(8,128)(2,1)S(1)}, u32[]{:S(2)}, u32[]{:S(2)}) collective-permute-start(bf16[16,32,2048]{2,1,0:T(8,128)(2,1)S(1)} %fusion.1), channel_id=1, source_target_pairs={{0,1},{1,0},{2,3},{3,2},{4,5},{5,4},{6,7},{7,6},{8,9},{9,8},{10,11... | collective-permute-start | bytes 6291464 | tf_op jit(solution)/shard_map/ppermute | solution.py:62
  139.2 3.8 %collective-permute-done.1 = bf16[16,32,2048]{2,1,0:T(8,128)(2,1)S(1)} collective-permute-done((bf16[16,32,2048]{2,1,0:T(8,128)(2,1)S(1)}, bf16[16,32,2048]{2,1,0:T(8,128)(2,1)S(1)}, u32[]{:S(2)}, u32[]{:S(2)}) %collective-permute-start.1) | collective-permute-done | bytes 2097184 | tf_op jit(solution)/shard_map/ppermute | solution.py:62
  143.0 2.6 %fusion = bf16[16,32,2048]{2,1,0:T(8,128)(2,1)} fusion(bf16[16,32,2048]{2,1,0:T(8,128)(2,1)S(1)} %collective-permute-done.1, pred[]{:T(512)S(6)} %eq.30, bf16[16,2,32,2048]{3,2,1,0:T(8,128)(2,1)S(1)} %bitcast.55), kind=kLoop, calls=%fused_computation.3 | loop fusion | flops 5242880 | bytes 8388609 | tf_op jit(solution)/shard_map/convert_element_type | solution.py:63
  145.7 6.9 %all-to-all-start.3 = ((bf16[16,32,2048]{2,1,0:T(8,128)(2,1)}), bf16[16,32,2048]{2,1,0:T(8,128)(2,1)}, u32[]{:S(2)}, u32[]{:S(2)}) async-start(bf16[16,32,2048]{2,1,0:T(8,128)(2,1)} %fusion), calls=%async_computation.3 | async-start | bytes 4194304 | tf_op jit(solution)/shard_map/all_to_all | solution.py:64
  152.5 1.2 slice.121
  153.8 1.1 slice.122
  155.0 0.5 collective-permute-start.2
  155.5 3.0 %fusion.18 = f32[896,1024]{1,0:T(8,128)} fusion(bf16[512,1024]{1,0:T(8,128)(2,1)S(1)} %fusion.8, bf16[512,2944]{1,0:T(8,128)(2,1)S(1)} %bitcast.60), kind=kOutput, calls=%fused_computation.40 | convolution fusion | flops 939524096 | bytes 5636096 | tf_op jit(solution)/shard_map/dot_general | solution.py:132
  158.5 0.8 fusion.6
  159.3 3.1 %fusion.11 = f32[1024,896]{1,0:T(8,128)} fusion(bf16[512,1024]{1,0:T(8,128)(2,1)S(1)} %fusion.6, bf16[512,2944]{1,0:T(8,128)(2,1)S(1)} %bitcast.61), kind=kOutput, calls=%fused_computation.33 | convolution fusion | flops 939524096 | bytes 5636096 | tf_op jit(solution)/shard_map/dot_general | solution.py:144
  162.4 3.1 %fusion.14 = f32[1024,896]{1,0:T(8,128)} fusion(bf16[512,1024]{1,0:T(8,128)(2,1)S(1)} %fusion.6, bf16[512,2944]{1,0:T(8,128)(2,1)S(1)} %bitcast.62), kind=kOutput, calls=%fused_computation.36 | convolution fusion | flops 939524096 | bytes 5636096 | tf_op jit(solution)/shard_map/dot_general | solution.py:143
  165.5 15.2 %all-to-all-done.3 = bf16[16,32,2048]{2,1,0:T(8,128)(2,1)} async-done(((bf16[16,32,2048]{2,1,0:T(8,128)(2,1)}), bf16[16,32,2048]{2,1,0:T(8,128)(2,1)}, u32[]{:S(2)}, u32[]{:S(2)}) %all-to-all-start.3) | async-done | bytes 2097184 | tf_op jit(solution)/shard_map/all_to_all | solution.py:64
  180.7 2.0 %reduce = bf16[2,32,2048]{2,1,0:T(8,128)(2,1)S(1)} reduce(bf16[8,2,32,2048]{3,2,1,0:T(8,128)(2,1)} %bitcast.20, bf16[]{:T(256)} %constant.45), dimensions={0}, to_apply=%region_8.9.clone | reduce | flops 917504 | bytes 2359298 | tf_op jit(solution)/shard_map/reduce_sum | solution.py:65
  182.7 0.7 fusion.32
  (51 shorter events, 3.8 us)
Async XLA Ops:
  0.6 29.4 %copy-start = (f32[1024,512]{1,0:T(8,128)S(1)}, f32[1024,512]{1,0:T(8,128)}, u32[]{:S(2)}) copy-start(f32[1024,512]{1,0:T(8,128)} %param.14) | copy-start | bytes 6291460
  2.5 27.0 %copy-start.5 = (s32[16,4]{0,1:T(4,128)S(1)}, s32[16,4]{0,1:T(4,128)}, u32[]{:S(2)}) copy-start(s32[16,4]{0,1:T(4,128)} %param.9) | copy-start | bytes 772
  2.5 27.0 %copy-start.6 = (s32[16,4]{0,1:T(4,128)S(1)}, s32[16,4]{0,1:T(4,128)}, u32[]{:S(2)}) copy-start(s32[16,4]{0,1:T(4,128)} %param.10) | copy-start | bytes 772
  29.4 5.2 %collective-permute-start = (bf16[16,48,1024]{2,1,0:T(8,128)(2,1)}, bf16[16,48,1024]{2,1,0:T(8,128)(2,1)}, u32[]{:S(2)}, u32[]{:S(2)}) collective-permute-start(bf16[16,48,1024]{2,1,0:T(8,128)(2,1)} %all_to_all.20), channel_id=1, source_target_pairs={{0,1},{1,0},{2,3},{3,2},{4,5},{5,4},{6,7},{7,6},{8,9},{9,8},{10,11... | collective-permute-start | bytes 4718600 | tf_op jit(solution)/shard_map/ppermute | solution.py:87
  30.1 1.7 copy-start.8
  31.7 4.0 %copy-start.9 = (bf16[1024,896]{1,0:T(8,128)(2,1)S(1)}, bf16[1024,896]{1,0:T(8,128)(2,1)}, u32[]{:S(2)}) copy-start(bf16[1024,896]{1,0:T(8,128)(2,1)} %param.12) | copy-start | bytes 5505028
  41.1 1.1 copy-start.3
  41.2 1.7 copy-start.4
  43.0 1.5 copy-start.7
  129.5 2.6 %copy-start.1 = (bf16[8,64,2944]{2,1,0:T(8,128)(2,1)}, bf16[8,64,2944]{2,1,0:T(8,128)(2,1)S(1)}, u32[]{:S(2)}) copy-start(bf16[8,64,2944]{2,1,0:T(8,128)(2,1)S(1)} %all_to_all.22) | copy-start | bytes 9043972
  136.1 6.9 %collective-permute-start.1 = (bf16[16,32,2048]{2,1,0:T(8,128)(2,1)S(1)}, bf16[16,32,2048]{2,1,0:T(8,128)(2,1)S(1)}, u32[]{:S(2)}, u32[]{:S(2)}) collective-permute-start(bf16[16,32,2048]{2,1,0:T(8,128)(2,1)S(1)} %fusion.1), channel_id=1, source_target_pairs={{0,1},{1,0},{2,3},{3,2},{4,5},{5,4},{6,7},{7,6},{8,9},{9,8},{10,11... | collective-permute-start | bytes 6291464 | tf_op jit(solution)/shard_map/ppermute | solution.py:62
  145.7 35.0 %all-to-all-start.3 = ((bf16[16,32,2048]{2,1,0:T(8,128)(2,1)}), bf16[16,32,2048]{2,1,0:T(8,128)(2,1)}, u32[]{:S(2)}, u32[]{:S(2)}) async-start(bf16[16,32,2048]{2,1,0:T(8,128)(2,1)} %fusion), calls=%async_computation.3 | async-start | bytes 4194304 | tf_op jit(solution)/shard_map/all_to_all | solution.py:64
  152.5 2.4 %copy-start.2 = (bf16[8,64,2944]{2,1,0:T(8,128)(2,1)S(1)}, bf16[8,64,2944]{2,1,0:T(8,128)(2,1)}, u32[]{:S(2)}) copy-start(bf16[8,64,2944]{2,1,0:T(8,128)(2,1)} %copy-done.1) | copy-start | bytes 9043972
  155.0 3.5 %collective-permute-start.2 = (bf16[512,256]{1,0:T(8,128)(2,1)S(1)}, bf16[512,256]{1,0:T(8,128)(2,1)S(1)}, u32[]{:S(2)}, u32[]{:S(2)}) collective-permute-start(bf16[512,256]{1,0:T(8,128)(2,1)S(1)} %slice.123), channel_id=1, source_target_pairs={{0,1},{1,0},{2,3},{3,2},{4,5},{5,4},{6,7},{7,6},{8,9},{9,8},{10,11... | collective-permute-start | bytes 786440 | tf_op jit(solution)/shard_map/ppermute | solution.py:125

commit v13 on v10

--- a/solution.py
+++ b/solution.py
@@ -51,7 +51,7 @@
     return got.reshape(n * rows, cols)
 
 
-def reduce_dealt(part, pick, blocks):
+def pair_dealt(part, pick, blocks):
     cols = part.shape[1]
     contract_rows = (((0,), (0,)), ((), ()))
     send = lax.dot_general(pick, part.astype(jnp.bfloat16), contract_rows, preferred_element_type=jnp.float32)
@@ -60,7 +60,11 @@
     keep = jnp.where(odd, send[:, 1], send[:, 0])
     give = jnp.where(odd, send[:, 0], send[:, 1])
     got = lax.ppermute(give, "fsdp", [(f, f ^ 1) for f in range(blocks)])
-    pair = (keep.astype(jnp.float32) + got.astype(jnp.float32)).astype(jnp.bfloat16)
+    return (keep.astype(jnp.float32) + got.astype(jnp.float32)).astype(jnp.bfloat16)
+
+
+def reduce_dealt(pair, blocks):
+    cols = pair.shape[2]
     came = lax.all_to_all(pair, "fsdp", 0, 0, tiled=True)
     halves = jnp.sum(came.astype(jnp.float32).reshape(blocks // 2, 2, -1, cols), axis=0)
     return halves.reshape(-1, cols).astype(jnp.bfloat16)
@@ -123,7 +127,8 @@
     total = lax.dot_general(gate_all, w_gate, contract_cols, preferred_element_type=jnp.float32)
     total = total + lax.dot_general(up_all, w_up, contract_cols, preferred_element_type=jnp.float32)
     model_width = out_part.shape[1]
-    dealt = reduce_dealt(jnp.concatenate([out_part, total], axis=1), pick, n_fsdp)
+    pairs = jnp.concatenate([pair_dealt(out_part, pick, n_fsdp), pair_dealt(total, pick, n_fsdp)], axis=2)
+    dealt = reduce_dealt(pairs, n_fsdp)
     layer_out = dealt[:, :model_width]
     input_grad = dealt[:, model_width:]
 

time: 181 us -> 193 us (1.066)
  matrix products: 23.5 us -> 30.9 us
  other arithmetic: 8.59 us -> 12.9 us
  local copies, waits for them, and re-layouts: 7.04 us -> 9.36 us
    dot_general x3 -> x2, matrix products: 5.06 us -> 11.6 us  [pair_dealt(): lax.dot_general(pick, part.astype(jnp.bfloat16), contract_rows, preferred...]
    select_n x1 -> x2, other arithmetic: 0.22 us -> 4.44 us  [pair_dealt(): give = jnp.where(odd, send[:, 0], send[:, 1])]
    unnamed x18 -> x28, local copies, waits for them, and re-layouts: 2.65 us -> 4.96 us
    ppermute x1 -> x2, waiting for transfers between devices: 3.79 us -> 1.7 us  [pair_dealt(): got = lax.ppermute(give, 'fsdp', [(f, f ^ 1) for f in range(blocks)])]
  transfers between devices with their start and end apart: 4 -> 5, of which waited for: 3 -> 3; matrix products, arithmetic and copies ran while one was open for 7% -> 11% of each run, Pallas kernels for 0% -> 0%
where the time goes in v13:
time: 193 us; the launch traced here: 192 us
  blocking collectives  109 us (56%)
  matrix products  30.9 us (16%)
  waiting for transfers between devices  19.2 us (10%)
  other arithmetic  12.9 us (7%)
  starting transfers between devices  9.48 us (5%)
  local copies, waits for them, and re-layouts  9.36 us (5%)
    all_to_all x1, blocking collectives, reduce_rows(): lax.all_to_all(part.astype(jnp.bfloat16).reshape(n, rows // n, cols), axi...  43.8 us
    all_to_all x1, blocking collectives, gather_rows(): lax.all_to_all(jnp.broadcast_to(block[None], (n, rows, cols)), axis, 0, 0...  38.9 us
    all_to_all x1, blocking collectives, per_device(): lax.all_to_all(jnp.tile(halves, (n_fsdp // 2, 1, 1)), 'fsdp', 0, 0, tiled...  26.6 us
    all_to_all x1, waiting for transfers between devices, reduce_dealt(): came = lax.all_to_all(pair, 'fsdp', 0, 0, tiled=True)  14.4 us
    dot_general x2, matrix products, pair_dealt(): lax.dot_general(pick, part.astype(jnp.bfloat16), contract_rows, preferred...  11.6 us
    all_to_all x1, starting transfers between devices, reduce_dealt(): came = lax.all_to_all(pair, 'fsdp', 0, 0, tiled=True)  5.9 us
    unnamed x28, local copies, waits for them, and re-layouts  4.96 us
    select_n x2, other arithmetic, pair_dealt(): give = jnp.where(odd, send[:, 0], send[:, 1])  4.44 us
  transfers between devices with their start and end apart: 5, of which 3 were waited for; matrix products, arithmetic and copies ran while one was open for 11% of the time, Pallas kernels for 0%

profile of v13, /device:TPU:33, one launch (start us, length us, event | category | flops | bytes accessed | tf_op | source)
XLA Modules:
  0.0 192.3 jit_solution(5663054224961509332)
XLA Ops:
  0.6 0.9 fusion.50
  1.6 0.9 fusion.49
  2.7 26.6 %all_to_all.20 = bf16[16,48,1024]{2,1,0:T(8,128)(2,1)} all-to-all(bf16[16,48,1024]{2,1,0:T(8,128)(2,1)S(1)} %bitcast.90), channel_id=1, replica_groups=mesh['dp'=8,'fsdp'=16] {'fsdp'}, dimensions={0} | all-to-all | bytes 3145728 | tf_op jit(solution)/shard_map/all_to_all | solution.py:90
  30.1 3.1 %collective-permute-done = bf16[16,48,1024]{2,1,0:T(8,128)(2,1)} collective-permute-done((bf16[16,48,1024]{2,1,0:T(8,128)(2,1)}, bf16[16,48,1024]{2,1,0:T(8,128)(2,1)}, u32[]{:S(2)}, u32[]{:S(2)}) %collective-permute-start) | collective-permute-done | bytes 1572896 | tf_op jit(solution)/shard_map/ppermute | solution.py:91
  33.1 2.1 %broadcast_select_fusion.1 = (bf16[16,48,1024]{2,1,0:T(8,128)(2,1)S(1)}, bf16[16,48,1024]{2,1,0:T(8,128)(2,1)S(1)}) fusion(bf16[16,48,1024]{2,1,0:T(8,128)(2,1)} %collective-permute-done, bf16[16,48,1024]{2,1,0:T(8,128)(2,1)} %all_to_all.20, pred[]{:T(512)S(6)} %eq.31), kind=kLoop, calls=%fused_computation.23 | loop fusion | flops 1572864 | bytes 6291457 | tf_op jit(solution)/shard_map/jit(_where)/select_n | solution.py:93
  35.6 1.7 copy-done.12
  37.3 1.2 fusion.16
  38.8 1.2 fusion.13
  40.3 1.3 fusion.12
  42.1 1.3 convolution_convert_fusion.1
  43.7 43.8 %all_to_all.21 = bf16[8,64,2944]{2,1,0:T(8,128)(2,1)S(1)} all-to-all(bf16[8,64,2944]{2,1,0:T(8,128)(2,1)S(1)} %pad_maximum_fusion), channel_id=1, replica_groups=mesh['dp'=8,'fsdp'=16] {'dp'}, dimensions={0} | all-to-all | bytes 6029312 | tf_op jit(solution)/shard_map/all_to_all | solution.py:44
  88.6 38.9 %all_to_all.22 = bf16[8,64,2944]{2,1,0:T(8,128)(2,1)S(1)} all-to-all(bf16[8,64,2944]{2,1,0:T(8,128)(2,1)S(1)} %broadcast_in_dim.2), channel_id=1, replica_groups=mesh['dp'=8,'fsdp'=16] {'dp'}, dimensions={0} | all-to-all | bytes 6029312 | tf_op jit(solution)/shard_map/all_to_all | solution.py:50
  127.5 1.6 copy-done.1
  129.1 2.6 %fusion.31 = f32[512,1024]{1,0:T(8,128)} fusion(bf16[1024,896]{1,0:T(8,128)(2,1)S(1)} %copy-done.11, bf16[512,2944]{1,0:T(8,128)(2,1)S(1)} %bitcast.79), kind=kOutput, calls=%fused_computation.47 | convolution fusion | flops 939524096 | bytes 4849664 | tf_op jit(solution)/shard_map/dot_general | solution.py:127
  131.7 6.1 %fusion.7 = bf16[1024,1024]{1,0:T(8,128)(2,1)} fusion(s32[512]{0:T(512)S(1)} %sub.30, f32[512,1024]{1,0:T(8,128)} %fusion.31, bf16[1024,896]{1,0:T(8,128)(2,1)} %param.12, bf16[512,2944]{1,0:T(8,128)(2,1)} %bitcast.80), kind=kOutput, calls=%fused_computation.17 | convolution fusion | flops 2015887360 | bytes 6948864 | tf_op jit(solution)/shard_map/dot_general | solution.py:57
  137.8 2.6 %select_bitcast_fusion = bf16[16,32,1024]{2,1,0:T(8,128)(2,1)} fusion(pred[]{:T(512)S(6)} %eq.31, bf16[16,2,32,1024]{3,2,1,0:T(8,128)(2,1)} %bitcast.86), kind=kLoop, calls=%fused_computation.37 | loop fusion | flops 524288 | bytes 3145729 | tf_op jit(solution)/shard_map/jit(_where)/select_n | solution.py:61
  140.5 2.9 %collective-permute-start.2 = (bf16[16,32,1024]{2,1,0:T(8,128)(2,1)}, bf16[16,32,1024]{2,1,0:T(8,128)(2,1)S(1)}, u32[]{:S(2)}, u32[]{:S(2)}) collective-permute-start(bf16[16,32,1024]{2,1,0:T(8,128)(2,1)} %select_bitcast_fusion), channel_id=1, source_target_pairs={{0,1},{1,0},{2,3},{3,2},{4,5},{5,4},{6,7},{7,6},{8,9},{9,8},{10,11... | collective-permute-start | bytes 3145736 | tf_op jit(solution)/shard_map/ppermute | solution.py:62
  143.4 5.4 %fusion.6 = bf16[1024,1024]{1,0:T(8,128)(2,1)} fusion(s32[512]{0:T(512)S(1)} %sub.30, bf16[896,1024]{1,0:T(8,128)(2,1)} %param.13, bf16[512,2944]{1,0:T(8,128)(2,1)} %bitcast.81), kind=kOutput, calls=%fused_computation.16 | convolution fusion | flops 2015363072 | bytes 4851712 | tf_op jit(solution)/shard_map/dot_general | solution.py:57
  148.9 1.8 fusion.19
  151.7 1.7 collective-permute-done.1
  153.4 0.6 fusion.2
  154.1 1.5 pad_maximum_fusion.2
  155.6 5.9 %all-to-all-start.3 = ((bf16[16,32,2048]{2,1,0:T(8,128)(2,1)}), bf16[16,32,2048]{2,1,0:T(8,128)(2,1)}, u32[]{:S(2)}, u32[]{:S(2)}) async-start(bf16[16,32,2048]{2,1,0:T(8,128)(2,1)} %pad_maximum_fusion.2), calls=%async_computation.3 | async-start | bytes 4194304 | tf_op jit(solution)/shard_map/all_to_all | solution.py:68
  161.5 1.0 slice.110
  162.9 4.2 %fusion.33 = f32[896,1024]{1,0:T(8,128)} fusion(bf16[512,1024]{1,0:T(8,128)(2,1)S(1)} %copy-done.8, bf16[512,2944]{1,0:T(8,128)(2,1)} %bitcast.83), kind=kOutput, calls=%fused_computation.49 | convolution fusion | flops 939524096 | bytes 5636096 | tf_op jit(solution)/shard_map/dot_general | solution.py:126
  167.1 0.8 fusion
  167.9 1.1 copy-done.2
  168.9 3.1 %fusion.26 = f32[1024,896]{1,0:T(8,128)} fusion(bf16[512,1024]{1,0:T(8,128)(2,1)S(1)} %fusion, bf16[512,2944]{1,0:T(8,128)(2,1)S(1)} %bitcast.84), kind=kOutput, calls=%fused_computation.42 | convolution fusion | flops 939524096 | bytes 5636096 | tf_op jit(solution)/shard_map/dot_general | solution.py:139
  172.1 3.1 %fusion.29 = f32[1024,896]{1,0:T(8,128)} fusion(bf16[512,1024]{1,0:T(8,128)(2,1)S(1)} %fusion, bf16[512,2944]{1,0:T(8,128)(2,1)S(1)} %bitcast.85), kind=kOutput, calls=%fused_computation.45 | convolution fusion | flops 939524096 | bytes 5636096 | tf_op jit(solution)/shard_map/dot_general | solution.py:138
  175.2 14.4 %all-to-all-done.3 = bf16[16,32,2048]{2,1,0:T(8,128)(2,1)} async-done(((bf16[16,32,2048]{2,1,0:T(8,128)(2,1)}), bf16[16,32,2048]{2,1,0:T(8,128)(2,1)}, u32[]{:S(2)}, u32[]{:S(2)}) %all-to-all-start.3) | async-done | bytes 2097184 | tf_op jit(solution)/shard_map/all_to_all | solution.py:68
  189.6 2.0 %reduce = bf16[2,32,2048]{2,1,0:T(8,128)(2,1)S(1)} reduce(bf16[8,2,32,2048]{3,2,1,0:T(8,128)(2,1)} %bitcast.19, bf16[]{:T(256)} %constant.47), dimensions={0}, to_apply=%region_8.9.clone | reduce | flops 917504 | bytes 2359298 | tf_op jit(solution)/shard_map/reduce_sum | solution.py:69
  191.6 0.7 fusion.48
  (58 shorter events, 4.9 us)
Async XLA Ops:
  0.6 41.0 %copy-start = (f32[1024,512]{1,0:T(8,128)S(1)}, f32[1024,512]{1,0:T(8,128)}, u32[]{:S(2)}) copy-start(f32[1024,512]{1,0:T(8,128)} %param.14) | copy-start | bytes 6291460
  2.5 27.0 %copy-start.9 = (s32[16,4]{0,1:T(4,128)S(1)}, s32[16,4]{0,1:T(4,128)}, u32[]{:S(2)}) copy-start(s32[16,4]{0,1:T(4,128)} %param.9) | copy-start | bytes 772
  2.5 27.0 %copy-start.10 = (s32[16,4]{0,1:T(4,128)S(1)}, s32[16,4]{0,1:T(4,128)}, u32[]{:S(2)}) copy-start(s32[16,4]{0,1:T(4,128)} %param.10) | copy-start | bytes 772
  29.4 3.8 %collective-permute-start = (bf16[16,48,1024]{2,1,0:T(8,128)(2,1)}, bf16[16,48,1024]{2,1,0:T(8,128)(2,1)}, u32[]{:S(2)}, u32[]{:S(2)}) collective-permute-start(bf16[16,48,1024]{2,1,0:T(8,128)(2,1)} %all_to_all.20), channel_id=1, source_target_pairs={{0,1},{1,0},{2,3},{3,2},{4,5},{5,4},{6,7},{7,6},{8,9},{9,8},{10,11... | collective-permute-start | bytes 4718600 | tf_op jit(solution)/shard_map/ppermute | solution.py:91
  35.4 1.9 copy-start.12
  35.6 6.0 %copy-start.5 = (bf16[16,32,1024]{2,1,0:T(8,128)(2,1)}, bf16[16,32,1024]{2,1,0:T(8,128)(2,1)S(1)}, u32[]{:S(2)}) copy-start(bf16[16,32,1024]{2,1,0:T(8,128)(2,1)S(1)} %pad_maximum_fusion.3) | copy-start | bytes 3145732
  37.3 1.5 copy-start.11
  40.3 1.8 copy-start.13
  41.6 1.8 copy-start.7
  127.5 1.6 copy-start.1
  140.5 10.3 %collective-permute-start.2 = (bf16[16,32,1024]{2,1,0:T(8,128)(2,1)}, bf16[16,32,1024]{2,1,0:T(8,128)(2,1)S(1)}, u32[]{:S(2)}, u32[]{:S(2)}) collective-permute-start(bf16[16,32,1024]{2,1,0:T(8,128)(2,1)} %select_bitcast_fusion), channel_id=1, source_target_pairs={{0,1},{1,0},{2,3},{3,2},{4,5},{5,4},{6,7},{7,6},{8,9},{9,8},{10,11... | collective-permute-start | bytes 3145736 | tf_op jit(solution)/shard_map/ppermute | solution.py:62
  148.9 2.2 %copy-start.3 = (bf16[1024,1024]{1,0:T(8,128)(2,1)S(1)}, bf16[1024,1024]{1,0:T(8,128)(2,1)}, u32[]{:S(2)}) copy-start(bf16[1024,1024]{1,0:T(8,128)(2,1)} %fusion.7) | copy-start | bytes 6291460
  150.7 2.8 %copy-start.4 = (bf16[1024,1024]{1,0:T(8,128)(2,1)S(1)}, bf16[1024,1024]{1,0:T(8,128)(2,1)}, u32[]{:S(2)}) copy-start(bf16[1024,1024]{1,0:T(8,128)(2,1)} %fusion.6) | copy-start | bytes 6291460
  150.7 2.7 %collective-permute-start.1 = (bf16[16,32,1024]{2,1,0:T(8,128)(2,1)S(1)}, bf16[16,32,1024]{2,1,0:T(8,128)(2,1)S(1)}, u32[]{:S(2)}, u32[]{:S(2)}) collective-permute-start(bf16[16,32,1024]{2,1,0:T(8,128)(2,1)S(1)} %fusion.19), channel_id=1, source_target_pairs={{0,1},{1,0},{2,3},{3,2},{4,5},{5,4},{6,7},{7,6},{8,9},{9,8},{10,11... | collective-permute-start | bytes 3145736 | tf_op jit(solution)/shard_map/ppermute | solution.py:62
  155.6 7.3 %copy-start.8 = (bf16[512,1024]{1,0:T(8,128)(2,1)S(1)}, bf16[512,1024]{1,0:T(8,128)(2,1)}, u32[]{:S(2)}) copy-start(bf16[512,1024]{1,0:T(8,128)(2,1)} %copy-done.7) | copy-start | bytes 3145732
  155.6 34.1 %all-to-all-start.3 = ((bf16[16,32,2048]{2,1,0:T(8,128)(2,1)}), bf16[16,32,2048]{2,1,0:T(8,128)(2,1)}, u32[]{:S(2)}, u32[]{:S(2)}) async-start(bf16[16,32,2048]{2,1,0:T(8,128)(2,1)} %pad_maximum_fusion.2), calls=%async_computation.3 | async-start | bytes 4194304 | tf_op jit(solution)/shard_map/all_to_all | solution.py:68
  162.4 4.6 %copy-start.6 = (bf16[16,32,1024]{2,1,0:T(8,128)(2,1)S(1)}, bf16[16,32,1024]{2,1,0:T(8,128)(2,1)}, u32[]{:S(2)}) copy-start(bf16[16,32,1024]{2,1,0:T(8,128)(2,1)} %copy-done.5) | copy-start | bytes 3145732
  162.4 4.6 %collective-permute-start.3 = (bf16[512,256]{1,0:T(8,128)(2,1)S(1)}, bf16[512,256]{1,0:T(8,128)(2,1)S(1)}, u32[]{:S(2)}, u32[]{:S(2)}) collective-permute-start(bf16[512,256]{1,0:T(8,128)(2,1)S(1)} %slice.110), channel_id=1, source_target_pairs={{0,1},{1,0},{2,3},{3,2},{4,5},{5,4},{6,7},{7,6},{8,9},{9,8},{10,11... | collective-permute-start | bytes 786440 | tf_op jit(solution)/shard_map/ppermute | solution.py:119
  167.1 1.9 copy-start.2

commit v14 on v10

--- a/solution.py
+++ b/solution.py
@@ -73,7 +73,6 @@
     loads, firsts = deal_tables(doc_lengths, doc_dests)
     rows_of = token_rows(doc_lengths, doc_dests, loads, tok, recv)
     dealt_rows = jnp.arange(n_fsdp * recv, dtype=jnp.int32)
-    pick = (rows_of[:, None] == dealt_rows[None, :]).astype(jnp.bfloat16)
     contract_rows = (((0,), (0,)), ((), ()))
     contract_cols = (((1,), (1,)), ((), ()))
 
@@ -86,11 +85,23 @@
     came = lax.all_to_all(jnp.tile(halves, (n_fsdp // 2, 1, 1)), "fsdp", 0, 0, tiled=True)
     other = lax.ppermute(came, "fsdp", [(f, f ^ 1) for f in range(n_fsdp)])
     odd = lax.axis_index("fsdp") % 2 == 1
-    low = jnp.where(odd, other, came)
-    high = jnp.where(odd, came, other)
-    xall = jnp.concatenate([low[:, :half_x], high[:, :half_x]], axis=1).reshape(-1, x_src.shape[1])
-    dy_dealt = jnp.concatenate([low[:, half_x:], high[:, half_x:]], axis=1).reshape(-1, x_src.shape[1])
-    dyall = jnp.dot(pick, dy_dealt, preferred_element_type=jnp.float32).astype(jnp.bfloat16)
+    parity = lax.axis_index("fsdp") % 2
+    width = x_src.shape[1]
+    xall = jnp.concatenate([came[:, :half_x].reshape(-1, width), other[:, :half_x].reshape(-1, width)])
+    dy_rows = jnp.concatenate([came[:, half_x:].reshape(-1, width), other[:, half_x:].reshape(-1, width)])
+    rows3 = rows_of.reshape(n_fsdp, 2, half_x)
+    mine = jnp.where(odd, rows3[:, 1], rows3[:, 0])
+    theirs = jnp.where(odd, rows3[:, 0], rows3[:, 1])
+    rows_perm = jnp.concatenate([mine.reshape(-1), theirs.reshape(-1)])
+    pick = (rows_perm[:, None] == dealt_rows[None, :]).astype(jnp.bfloat16)
+    src_i = jnp.arange(n_fsdp, dtype=jnp.int32)[:, None] * recv
+    within = jnp.arange(half_dy, dtype=jnp.int32)[None, :]
+    label = jnp.concatenate([
+        (src_i + parity * half_dy + within).reshape(-1),
+        (src_i + (1 - parity) * half_dy + within).reshape(-1),
+    ])
+    pick_dy = (rows_perm[:, None] == label[None, :]).astype(jnp.bfloat16)
+    dyall = jnp.dot(pick_dy, dy_rows, preferred_element_type=jnp.float32).astype(jnp.bfloat16)
     first = jnp.dot(xall, w_gate, preferred_element_type=jnp.float32)
     second = jnp.dot(xall, w_up, preferred_element_type=jnp.float32)
     key_half = basis.shape[1] // 2
@@ -113,6 +124,8 @@
     up_all = gathered[:, 2 * hidden_width:3 * hidden_width]
     keys_mine = gathered[:, 3 * hidden_width:]
     keys_other = lax.ppermute(keys_mine, "fsdp", [(f, f ^ 1) for f in range(n_fsdp)])
+    rows_half = keys_other.shape[0] // 2
+    keys_other = jnp.concatenate([keys_other[rows_half:], keys_other[:rows_half]])
     keys_all = jnp.where(
         odd,
         jnp.concatenate([keys_other, keys_mine], axis=1),

time: 181 us -> 181 us (level)
  blocking collectives: 109 us -> 82.4 us
  waiting for transfers between devices: 21 us -> 39.3 us
  starting transfers between devices: 9.57 us -> 15.8 us
  local copies, waits for them, and re-layouts: 7.04 us -> 12.5 us
  other arithmetic: 8.59 us -> 6.42 us
    all_to_all x1 -> x0, blocking collectives: 26.6 us -> none  [per_device(): lax.all_to_all(jnp.tile(halves, (n_fsdp // 2, 1, 1)), 'fsdp', 0, 0, tiled...]
    all_to_all x0 -> x1, waiting for transfers between devices: none -> 21.1 us  [per_device(): lax.all_to_all(jnp.tile(halves, (n_fsdp // 2, 1, 1)), 'fsdp', 0, 0, tiled...]
    all_to_all x0 -> x1, starting transfers between devices: none -> 6.06 us  [per_device(): lax.all_to_all(jnp.tile(halves, (n_fsdp // 2, 1, 1)), 'fsdp', 0, 0, tiled...]
    slice x4 -> x5, local copies, waits for them, and re-layouts: 0.25 us -> 5.11 us  [the longest x1 1.49 us: per_device(): came[:, half_x:].reshape(-1, width)]
    ppermute x1, waiting for transfers between devices: 3.07 us -> 0.02 us  [per_device(): other = lax.ppermute(came, 'fsdp', [(f, f ^ 1) for f in range(n_fsdp)])]
    select_n x1, other arithmetic: 2.09 us -> 0.05 us  [per_device(): mine = jnp.where(odd, rows3[:, 1], rows3[:, 0])]
  transfers between devices with their start and end apart: 4 -> 5, of which waited for: 3 -> 3; matrix products, arithmetic and copies ran while one was open for 7% -> 9% of each run, Pallas kernels for 0% -> 0%
where the time goes in v14:
time: 181 us
  blocking collectives  82.4 us (46%)
  waiting for transfers between devices  39.3 us (22%)
  matrix products  23.1 us (13%)
  starting transfers between devices  15.8 us (9%)
  local copies, waits for them, and re-layouts  12.5 us (7%)
  other arithmetic  6.42 us (4%)
    all_to_all x1, blocking collectives, reduce_rows(): lax.all_to_all(part.astype(jnp.bfloat16).reshape(n, rows // n, cols), axi...  43.3 us
    all_to_all x1, blocking collectives, gather_rows(): lax.all_to_all(jnp.broadcast_to(block[None], (n, rows, cols)), axis, 0, 0...  39.1 us
    all_to_all x1, waiting for transfers between devices, per_device(): lax.all_to_all(jnp.tile(halves, (n_fsdp // 2, 1, 1)), 'fsdp', 0, 0, tiled...  21.1 us
    all_to_all x1, waiting for transfers between devices, reduce_dealt(): came = lax.all_to_all(pair, 'fsdp', 0, 0, tiled=True)  14.4 us
    all_to_all x1, starting transfers between devices, reduce_dealt(): came = lax.all_to_all(pair, 'fsdp', 0, 0, tiled=True)  6.07 us
    all_to_all x1, starting transfers between devices, per_device(): lax.all_to_all(jnp.tile(halves, (n_fsdp // 2, 1, 1)), 'fsdp', 0, 0, tiled...  6.06 us
    dot_general x1, matrix products, per_device(): lax.dot_general(hall, dyall, contract_rows, preferred_element_type=jnp.fl...  4.16 us
    ppermute x1, waiting for transfers between devices, reduce_dealt(): got = lax.ppermute(give, 'fsdp', [(f, f ^ 1) for f in range(blocks)])  3.79 us
  transfers between devices with their start and end apart: 5, of which 3 were waited for; matrix products, arithmetic and copies ran while one was open for 9% of the time, Pallas kernels for 0%

profile of v14, /device:TPU:33, one launch (start us, length us, event | category | flops | bytes accessed | tf_op | source)
XLA Modules:
  0.0 180.6 jit_solution(5624044184128960216)
XLA Ops:
  0.6 0.9 fusion.52
  1.6 0.9 fusion.51
  2.5 1.3 tile.4
  3.9 6.1 %all-to-all-start = ((bf16[16,48,1024]{2,1,0:T(8,128)(2,1)}), bf16[16,48,1024]{2,1,0:T(8,128)(2,1)}, u32[]{:S(2)}, u32[]{:S(2)}) async-start(bf16[16,48,1024]{2,1,0:T(8,128)(2,1)} %bitcast.62), calls=%async_computation | async-start | bytes 3145728 | tf_op jit(solution)/shard_map/all_to_all | solution.py:85
  10.3 21.1 %all-to-all-done = bf16[16,48,1024]{2,1,0:T(8,128)(2,1)} async-done(((bf16[16,48,1024]{2,1,0:T(8,128)(2,1)}), bf16[16,48,1024]{2,1,0:T(8,128)(2,1)}, u32[]{:S(2)}, u32[]{:S(2)}) %all-to-all-start) | async-done | bytes 1572896 | tf_op jit(solution)/shard_map/all_to_all | solution.py:85
  32.4 1.2 slice.103
  33.7 1.5 slice.105
  35.2 1.1 slice.104
  36.3 1.3 convolution_convert_fusion.3
  38.0 1.3 convolution_convert_fusion.4
  39.7 1.3 slice.106
  41.1 1.3 fusion.11
  42.5 1.3 convolution_convert_fusion.2
  44.1 43.3 %all_to_all.20 = bf16[8,64,2944]{2,1,0:T(8,128)(2,1)S(1)} all-to-all(bf16[8,64,2944]{2,1,0:T(8,128)(2,1)S(1)} %pad_maximum_fusion), channel_id=1, replica_groups=mesh['dp'=8,'fsdp'=16] {'dp'}, dimensions={0} | all-to-all | bytes 6029312 | tf_op jit(solution)/shard_map/all_to_all | solution.py:44
  88.4 39.1 %all_to_all.21 = bf16[8,64,2944]{2,1,0:T(8,128)(2,1)S(1)} all-to-all(bf16[8,64,2944]{2,1,0:T(8,128)(2,1)S(1)} %broadcast_in_dim.2), channel_id=1, replica_groups=mesh['dp'=8,'fsdp'=16] {'dp'}, dimensions={0} | all-to-all | bytes 6029312 | tf_op jit(solution)/shard_map/all_to_all | solution.py:50
  127.5 1.3 convolution_convert_fusion.1
  128.8 1.3 fusion.25
  130.1 1.3 add_convert_fusion
  131.4 2.5 %convolution_convert_fusion = bf16[1024,2048]{1,0:T(8,128)(2,1)S(1)} fusion(bf16[512,1024]{1,0:T(8,128)(2,1)S(1)} %add_convert_fusion, bf16[512,1024]{1,0:T(8,128)(2,1)S(1)} %convolution_convert_fusion.1, s32[512]{0:T(512)S(1)} %pad_add_fusion.1), kind=kOutput, calls=%fused_computation.4 | convolution fusion | flops 2154299392 | bytes 6293504 | tf_op jit(solution)/shard_map/dot_general | solution.py:57
  134.1 3.1 %collective-permute-start.1 = (bf16[16,32,2048]{2,1,0:T(8,128)(2,1)S(1)}, bf16[16,32,2048]{2,1,0:T(8,128)(2,1)S(1)}, u32[]{:S(2)}, u32[]{:S(2)}) collective-permute-start(bf16[16,32,2048]{2,1,0:T(8,128)(2,1)S(1)} %fusion.1), channel_id=1, source_target_pairs={{0,1},{1,0},{2,3},{3,2},{4,5},{5,4},{6,7},{7,6},{8,9},{9,8},{10,11... | collective-permute-start | bytes 6291464 | tf_op jit(solution)/shard_map/ppermute | solution.py:62
  137.2 3.8 %collective-permute-done.1 = bf16[16,32,2048]{2,1,0:T(8,128)(2,1)S(1)} collective-permute-done((bf16[16,32,2048]{2,1,0:T(8,128)(2,1)S(1)}, bf16[16,32,2048]{2,1,0:T(8,128)(2,1)S(1)}, u32[]{:S(2)}, u32[]{:S(2)}) %collective-permute-start.1) | collective-permute-done | bytes 2097184 | tf_op jit(solution)/shard_map/ppermute | solution.py:62
  141.0 2.6 %fusion = bf16[16,32,2048]{2,1,0:T(8,128)(2,1)} fusion(bf16[16,32,2048]{2,1,0:T(8,128)(2,1)S(1)} %collective-permute-done.1, pred[]{:T(512)S(6)} %eq.35, bf16[16,2,32,2048]{3,2,1,0:T(8,128)(2,1)S(1)} %bitcast.54), kind=kLoop, calls=%fused_computation.2 | loop fusion | flops 5242880 | bytes 8388609 | tf_op jit(solution)/shard_map/convert_element_type | solution.py:63
  143.6 6.1 %all-to-all-start.3 = ((bf16[16,32,2048]{2,1,0:T(8,128)(2,1)}), bf16[16,32,2048]{2,1,0:T(8,128)(2,1)}, u32[]{:S(2)}, u32[]{:S(2)}) async-start(bf16[16,32,2048]{2,1,0:T(8,128)(2,1)} %fusion), calls=%async_computation.3 | async-start | bytes 4194304 | tf_op jit(solution)/shard_map/all_to_all | solution.py:64
  149.7 1.0 slice.118
  151.2 4.2 %fusion.27 = f32[896,1024]{1,0:T(8,128)} fusion(bf16[512,1024]{1,0:T(8,128)(2,1)S(1)} %fusion.11, bf16[512,2944]{1,0:T(8,128)(2,1)} %bitcast.59), kind=kOutput, calls=%fused_computation.38 | convolution fusion | flops 939524096 | bytes 5636096 | tf_op jit(solution)/shard_map/dot_general | solution.py:135
  155.4 0.8 subtract_convert_fusion
  156.2 1.1 copy-done.2
  157.2 3.1 %fusion.20 = f32[1024,896]{1,0:T(8,128)} fusion(bf16[512,1024]{1,0:T(8,128)(2,1)S(1)} %subtract_convert_fusion, bf16[512,2944]{1,0:T(8,128)(2,1)S(1)} %bitcast.60), kind=kOutput, calls=%fused_computation.31 | convolution fusion | flops 939524096 | bytes 5636096 | tf_op jit(solution)/shard_map/dot_general | solution.py:147
  160.4 3.1 %fusion.23 = f32[1024,896]{1,0:T(8,128)} fusion(bf16[512,1024]{1,0:T(8,128)(2,1)S(1)} %subtract_convert_fusion, bf16[512,2944]{1,0:T(8,128)(2,1)S(1)} %bitcast.61), kind=kOutput, calls=%fused_computation.34 | convolution fusion | flops 939524096 | bytes 5636096 | tf_op jit(solution)/shard_map/dot_general | solution.py:146
  163.5 14.4 %all-to-all-done.3 = bf16[16,32,2048]{2,1,0:T(8,128)(2,1)} async-done(((bf16[16,32,2048]{2,1,0:T(8,128)(2,1)}), bf16[16,32,2048]{2,1,0:T(8,128)(2,1)}, u32[]{:S(2)}, u32[]{:S(2)}) %all-to-all-start.3) | async-done | bytes 2097184 | tf_op jit(solution)/shard_map/all_to_all | solution.py:64
  177.9 2.0 %reduce = bf16[2,32,2048]{2,1,0:T(8,128)(2,1)S(1)} reduce(bf16[8,2,32,2048]{3,2,1,0:T(8,128)(2,1)} %bitcast.18, bf16[]{:T(256)} %constant.52), dimensions={0}, to_apply=%region_8.9.clone | reduce | flops 917504 | bytes 2359298 | tf_op jit(solution)/shard_map/reduce_sum | solution.py:65
  179.8 0.7 fusion.50
  (64 shorter events, 4.4 us)
Async XLA Ops:
  0.6 38.6 %copy-start = (f32[1024,512]{1,0:T(8,128)S(1)}, f32[1024,512]{1,0:T(8,128)}, u32[]{:S(2)}) copy-start(f32[1024,512]{1,0:T(8,128)} %param.14) | copy-start | bytes 6291460
  2.5 7.4 %copy-start.7 = (s32[16,4]{0,1:T(4,128)S(1)}, s32[16,4]{0,1:T(4,128)}, u32[]{:S(2)}) copy-start(s32[16,4]{0,1:T(4,128)} %param.9) | copy-start | bytes 772
  2.5 29.0 %copy-start.8 = (s32[16,4]{0,1:T(4,128)S(1)}, s32[16,4]{0,1:T(4,128)}, u32[]{:S(2)}) copy-start(s32[16,4]{0,1:T(4,128)} %param.10) | copy-start | bytes 772
  3.9 27.5 %all-to-all-start = ((bf16[16,48,1024]{2,1,0:T(8,128)(2,1)}), bf16[16,48,1024]{2,1,0:T(8,128)(2,1)}, u32[]{:S(2)}, u32[]{:S(2)}) async-start(bf16[16,48,1024]{2,1,0:T(8,128)(2,1)} %bitcast.62), calls=%async_computation | async-start | bytes 3145728 | tf_op jit(solution)/shard_map/all_to_all | solution.py:85
  31.4 3.8 %collective-permute-start = (bf16[16,48,1024]{2,1,0:T(8,128)(2,1)}, bf16[16,48,1024]{2,1,0:T(8,128)(2,1)}, u32[]{:S(2)}, u32[]{:S(2)}) collective-permute-start(bf16[16,48,1024]{2,1,0:T(8,128)(2,1)} %all-to-all-done), channel_id=1, source_target_pairs={{0,1},{1,0},{2,3},{3,2},{4,5},{5,4},{6,7},{7,6},{8,9},{9,8},{10,11... | collective-permute-start | bytes 4718600 | tf_op jit(solution)/shard_map/ppermute | solution.py:86
  32.4 3.9 %copy-start.11 = (bf16[1024,896]{1,0:T(8,128)(2,1)S(1)}, bf16[1024,896]{1,0:T(8,128)(2,1)}, u32[]{:S(2)}) copy-start(bf16[1024,896]{1,0:T(8,128)(2,1)} %param.12) | copy-start | bytes 5505028
  33.7 5.6 %copy-start.3 = (bf16[16,16,1024]{2,1,0:T(8,128)(2,1)}, bf16[16,16,1024]{2,1,0:T(8,128)(2,1)S(1)}, u32[]{:S(2)}) copy-start(bf16[16,16,1024]{2,1,0:T(8,128)(2,1)S(1)} %slice.103) | copy-start | bytes 1572868
  36.3 3.0 %copy-start.5 = (bf16[16,16,1024]{2,1,0:T(8,128)(2,1)}, bf16[16,16,1024]{2,1,0:T(8,128)(2,1)S(1)}, u32[]{:S(2)}) copy-start(bf16[16,16,1024]{2,1,0:T(8,128)(2,1)S(1)} %slice.104) | copy-start | bytes 1572868
  36.3 1.7 copy-start.10
  41.0 1.5 copy-start.9
  127.5 2.6 %copy-start.1 = (bf16[8,64,2944]{2,1,0:T(8,128)(2,1)}, bf16[8,64,2944]{2,1,0:T(8,128)(2,1)S(1)}, u32[]{:S(2)}) copy-start(bf16[8,64,2944]{2,1,0:T(8,128)(2,1)S(1)} %all_to_all.21) | copy-start | bytes 9043972
  134.1 6.9 %collective-permute-start.1 = (bf16[16,32,2048]{2,1,0:T(8,128)(2,1)S(1)}, bf16[16,32,2048]{2,1,0:T(8,128)(2,1)S(1)}, u32[]{:S(2)}, u32[]{:S(2)}) collective-permute-start(bf16[16,32,2048]{2,1,0:T(8,128)(2,1)S(1)} %fusion.1), channel_id=1, source_target_pairs={{0,1},{1,0},{2,3},{3,2},{4,5},{5,4},{6,7},{7,6},{8,9},{9,8},{10,11... | collective-permute-start | bytes 6291464 | tf_op jit(solution)/shard_map/ppermute | solution.py:62
  143.6 34.2 %all-to-all-start.3 = ((bf16[16,32,2048]{2,1,0:T(8,128)(2,1)}), bf16[16,32,2048]{2,1,0:T(8,128)(2,1)}, u32[]{:S(2)}, u32[]{:S(2)}) async-start(bf16[16,32,2048]{2,1,0:T(8,128)(2,1)} %fusion), calls=%async_computation.3 | async-start | bytes 4194304 | tf_op jit(solution)/shard_map/all_to_all | solution.py:64
  150.7 4.7 %copy-start.4 = (bf16[16,16,1024]{2,1,0:T(8,128)(2,1)S(1)}, bf16[16,16,1024]{2,1,0:T(8,128)(2,1)}, u32[]{:S(2)}) copy-start(bf16[16,16,1024]{2,1,0:T(8,128)(2,1)} %copy-done.3) | copy-start | bytes 1572868
  150.7 4.7 %copy-start.6 = (bf16[16,16,1024]{2,1,0:T(8,128)(2,1)S(1)}, bf16[16,16,1024]{2,1,0:T(8,128)(2,1)}, u32[]{:S(2)}) copy-start(bf16[16,16,1024]{2,1,0:T(8,128)(2,1)} %copy-done.5) | copy-start | bytes 1572868
  150.7 4.6 %collective-permute-start.2 = (bf16[512,256]{1,0:T(8,128)(2,1)S(1)}, bf16[512,256]{1,0:T(8,128)(2,1)S(1)}, u32[]{:S(2)}, u32[]{:S(2)}) collective-permute-start(bf16[512,256]{1,0:T(8,128)(2,1)S(1)} %slice.118), channel_id=1, source_target_pairs={{0,1},{1,0},{2,3},{3,2},{4,5},{5,4},{6,7},{7,6},{8,9},{9,8},{10,11... | collective-permute-start | bytes 786440 | tf_op jit(solution)/shard_map/ppermute | solution.py:126
  155.4 1.9 %copy-start.2 = (bf16[8,64,2944]{2,1,0:T(8,128)(2,1)S(1)}, bf16[8,64,2944]{2,1,0:T(8,128)(2,1)}, u32[]{:S(2)}) copy-start(bf16[8,64,2944]{2,1,0:T(8,128)(2,1)} %copy-done.1) | copy-start | bytes 9043972
